TPU v7x, 256 devices: a whole 4x4x8 slice. The times are simulated.
256 devices in a mesh: dp: 4 (over z_hi), expert: 16 (over y, z_lo, core), mp: 4 (over x).
Axes of the slice: x: 4, y: 4, z: 8 (z_hi: 4, z_lo: 2; z = z_hi * 2 + z_lo), core: 2. Of those that a mesh axis runs over, the one named last changes fastest.
Arguments:
- hidden: bfloat16 [16384, 2048], P(('dp', 'expert', 'mp')), may hold values from -6 to 6
- norm_gain: float32 [2048], replicated, may hold values from 0.1 to 1.9
- expert_in: float32 [64, 2048, 2816], P('dp', ('expert', 'mp')), may hold values from -0.125 to 0.125
- expert_out: float32 [64, 2048, 1408], P('dp', ('expert', 'mp')), may hold values from -0.15625 to 0.15625
- expert_ids: int32 [16384, 6], P(('dp', 'expert', 'mp')), may hold values from 0 to 63, all different within a row; in each aligned block of 64 rows (0 to 63, 64 to 127, ...) at most 12 rows name the same one
- gate_levels: int32 [16384, 6], P(('dp', 'expert', 'mp')), may hold values from 1 to 255
- shared_gate: bfloat16 [2048, 2816], P(('dp', 'expert'), 'mp'), may hold values from -0.125 to 0.125
- shared_up: bfloat16 [2048, 2816], P(('dp', 'expert'), 'mp'), may hold values from -0.125 to 0.125
- shared_down: bfloat16 [2048, 2816], P(('dp', 'expert'), 'mp'), may hold values from -0.109375 to 0.109375
- next_gain: float32 [2048], replicated, may hold values from 0.1 to 1.9
- kv_weight: bfloat16 [2048, 576], P(None, 'mp'), may hold values from -0.125 to 0.125
Outputs:
- layer_out: bfloat16 [16384, 2048], P(('dp', 'expert', 'mp'))
- kv_latent: bfloat16 [16384, 576], P(('dp', 'expert'), 'mp')
Inputs may be any that keep to these rules, and one draw needn't show every extreme that they name: `expert_ids`: each row names 6 different experts. Among the 64 rows of one device no expert is named by more than 12 rows, and in every draw some expert is named by exactly 12 rows of some device.
All inputs are finite; a program needn't handle non-finite values.
Results may differ from a plain program's by a relative error of at most 0.012.
Values may be sent and summed in bfloat16 or wider, within the bound.
No kernel may reach another device: no remote copies, remote signals or barrier semaphores. Data moves between devices by JAX's collectives and lax.ppermute only.
A program may use at most 128 MiB of HBM per device.

v0:
```python
import jax
import jax.numpy as jnp
from jax import lax
from jax.sharding import PartitionSpec as P


def rms_scale(values, gain):
    wide = values.astype(jnp.float32)
    mean_sq = jnp.mean(wide * wide, axis=-1, keepdims=True)
    return (wide * lax.rsqrt(mean_sq + 1e-06) * gain).astype(jnp.bfloat16)


def expert_part(rows, gate_up_w, down_w):
    quarter = down_w.shape[1]
    gate_up = jnp.dot(rows, gate_up_w, preferred_element_type=jnp.float32)
    act = (jax.nn.silu(gate_up[:, :quarter]) * gate_up[:, quarter:]).astype(jnp.bfloat16)
    return lax.dot_general(
        act, down_w, (((1,), (1,)), ((), ())), preferred_element_type=jnp.float32
    )


def on_device(
    hidden,
    norm_gain,
    expert_in,
    expert_out,
    expert_ids,
    gate_levels,
    shared_gate,
    shared_up,
    shared_down,
    next_gain,
    kv_weight,
):
    tok_rows, width = hidden.shape
    top = expert_ids.shape[1]
    n_mp = lax.axis_size("mp")
    n_groups = lax.axis_size(("dp", "expert"))
    capacity = min(tok_rows, (2 * tok_rows * top + n_groups - 1) // n_groups)
    local_e, local_rows, double = expert_in.shape
    full_ff = double // 2
    quarter = full_ff // n_mp
    in_cast = (
        expert_in.astype(jnp.bfloat16)
        .reshape(local_e, local_rows, 2, n_mp, quarter)
        .transpose(0, 3, 1, 2, 4)
    )
    out_cast = (
        expert_out.astype(jnp.bfloat16)
        .reshape(local_e, local_rows, n_mp, quarter)
        .transpose(0, 2, 1, 3)
    )
    in_send = in_cast.reshape(local_e * n_mp, local_rows, 2, quarter)
    out_send = out_cast.reshape(local_e * n_mp, local_rows, quarter)
    in_recv, out_recv = (
        lax.all_to_all(in_send, ("expert", "mp"), split_axis=0, concat_axis=1, tiled=True),
        lax.all_to_all(out_send, ("expert", "mp"), split_axis=0, concat_axis=1, tiled=True),
    )
    gate_up_w = in_recv.reshape(width, 2 * quarter)
    down_w = out_recv.reshape(width, quarter)
    normed = rms_scale(hidden, norm_gain)
    levels = gate_levels.astype(jnp.float32)
    gate_weights = levels / jnp.sum(levels, axis=1, keepdims=True)
    flat_ids = expert_ids.reshape(-1)
    pairs = flat_ids.shape[0]
    onehot = (flat_ids[:, None] == jnp.arange(n_groups, dtype=jnp.int32)[None, :]).astype(jnp.int32)
    before = jnp.cumsum(onehot, axis=0) - onehot
    slot_of_pair = jnp.sum(before * onehot, axis=1)
    target = flat_ids * capacity + slot_of_pair
    token_of_pair = jnp.arange(pairs, dtype=jnp.int32) // top
    send = (
        jnp.zeros((n_groups * capacity, width), jnp.bfloat16).at[target].set(normed[token_of_pair])
    )
    received = lax.all_to_all(
        send.reshape(n_groups, capacity, width),
        ("dp", "expert"),
        split_axis=0,
        concat_axis=0,
        tiled=True,
    )
    slots_here = received.reshape(n_groups * capacity, width)
    every_slot = lax.all_gather(slots_here, "mp", axis=0, tiled=True)
    rows = every_slot
    summed = lax.psum_scatter(
        expert_part(rows, gate_up_w, down_w).astype(jnp.bfloat16),
        "mp",
        scatter_dimension=0,
        tiled=True,
    )
    result = summed.reshape(n_groups, capacity, width)
    back = lax.all_to_all(
        result, ("dp", "expert"), split_axis=0, concat_axis=0, tiled=True
    ).reshape(n_groups * capacity, width)
    picked = back[target].reshape(tok_rows, top, width)
    routed = jnp.sum(picked.astype(jnp.float32) * gate_weights[:, :, None], axis=1)
    gate_w, up_w, down_s = (
        lax.all_gather(shared_gate, ("dp", "expert"), axis=0, tiled=True),
        lax.all_gather(shared_up, ("dp", "expert"), axis=0, tiled=True),
        lax.all_gather(shared_down, ("dp", "expert"), axis=0, tiled=True),
    )
    group_rows = lax.all_gather(normed, "mp", axis=0, tiled=True)
    rows = group_rows
    gate_part = jnp.dot(rows, gate_w, preferred_element_type=jnp.float32)
    up_part = jnp.dot(rows, up_w, preferred_element_type=jnp.float32)
    act = (jax.nn.silu(gate_part) * up_part).astype(jnp.bfloat16)
    shared_out = lax.psum_scatter(
        lax.dot_general(act, down_s, (((1,), (1,)), ((), ())), preferred_element_type=jnp.float32),
        "mp",
        scatter_dimension=0,
        tiled=True,
    )
    layer_out = (hidden.astype(jnp.float32) + routed + shared_out).astype(jnp.bfloat16)
    next_rows = rms_scale(layer_out, next_gain)
    next_group = lax.all_gather(next_rows, "mp", axis=0, tiled=True)
    kv_latent = jnp.dot(next_group, kv_weight, preferred_element_type=jnp.float32).astype(
        jnp.bfloat16
    )
    return (layer_out, kv_latent)


def solution(mesh):
    in_specs = (
        P(("dp", "expert", "mp"), None),
        P(),
        P("dp", ("expert", "mp"), None),
        P("dp", ("expert", "mp"), None),
        P(("dp", "expert", "mp"), None),
        P(("dp", "expert", "mp"), None),
        P(("dp", "expert"), "mp"),
        P(("dp", "expert"), "mp"),
        P(("dp", "expert"), "mp"),
        P(),
        P(None, "mp"),
    )
    out_specs = (P(("dp", "expert", "mp"), None), P(("dp", "expert"), "mp"))
    return jax.shard_map(
        on_device, mesh=mesh, in_specs=in_specs, out_specs=out_specs, check_vma=False
    )
```

profile of v0, /device:TPU:8, one launch (start us, length us, event | category | flops | bytes accessed | tf_op | source)
XLA Modules:
  0.0 935.2 jit_solution(4523954897152339868)
XLA Ops:
  12.9 10.0 %scatter_custom_fusion = bf16[768,2048]{1,0:T(8,128)(2,1)} fusion(s32[384]{0:T(512)S(1)} %fusion.26, bf16[64,2048]{1,0:T(8,128)(2,1)S(1)} %fusion.18, s32[1024]{0:T(1024)S(1)} %pad_clamp_fusion.1, bf16[]{:T(256)} %constant.12.clone.1), kind=kCustom, calls=%fused_computation.9 | custom fusion | bytes 3145730 | tf_op jit(solution)/shard_map/scatter | solution.py:72
  22.8 6.1 reshape.153
  28.9 108.9 %all_to_all.28 = bf16[64,12,2048]{2,1,0:T(8,128)(2,1)} all-to-all(bf16[64,12,2048]{2,1,0:T(8,128)(2,1)} %reshape.153), channel_id=1, replica_groups=mesh['dp'=4,'expert'=16,'mp'=4] {'dp','expert'}, dimensions={0} | all-to-all | bytes 6291456 | tf_op jit(solution)/shard_map/all_to_all | solution.py:74
  137.8 6.2 reshape.154
  144.0 3.0 convert_element_type.54
  147.0 5.1 reshape.155
  152.1 4.8 copy.24
  156.9 8.3 all-to-all-start.1
  165.8 1.4 pad_maximum_fusion
  167.2 50.3 %all-to-all-done.1 = bf16[64,32,2,352]{3,1,2,0:T(8,128)(2,1)} async-done(((bf16[64,32,2,352]{3,1,2,0:T(8,128)(2,1)}), bf16[64,32,2,352]{3,1,2,0:T(8,128)(2,1)}, u32[]{:S(2)}, u32[]{:S(2)}) %all-to-all-start.1) | async-done | bytes 2883616 | tf_op jit(solution)/shard_map/all_to_all | solution.py:56
  217.5 8.9 all-to-all-start.2
  226.4 6.9 copy.25
  233.3 7.8 reshape.157
  241.1 70.9 %all-gather.7.cloned.1.call-done = bf16[3072,2048]{1,0:T(8,128)(2,1)} async-done(((bf16[768,2048]{1,0:T(8,128)(2,1)}), bf16[3072,2048]{1,0:T(8,128)(2,1)}) %all-gather.7.cloned.1.call-update) | async-done | bytes 12582928 | tf_op jit(solution)/shard_map/all_gather | solution.py:82
  312.0 15.2 %fusion.32 = f32[3072,704]{0,1:T(8,128)} fusion(bf16[3072,2048]{1,0:T(8,128)(2,1)} %all-gather.7.cloned.1.call-done, bf16[2048,704]{1,0:T(8,128)(2,1)} %reshape.157), kind=kOutput, calls=%fused_computation.62 | convolution fusion | flops 8858370048 | bytes 24117248 | tf_op jit(solution)/shard_map/dot_general | solution.py:15
  327.2 13.5 %convolution_convert_fusion = bf16[3072,2048]{1,0:T(8,128)(2,1)} fusion(bf16[2048,352]{1,0:T(8,128)(2,1)S(1)} %bitcast.36, f32[3072,704]{0,1:T(8,128)} %fusion.32), kind=kOutput, calls=%fused_computation.3 | convolution fusion | flops 4441964544 | bytes 22675456 | tf_op jit(solution)/shard_map/dot_general | solution.py:17
  343.2 115.7 %reduce-scatter.3.cloned.1.call-done = bf16[768,2048]{1,0:T(8,128)(2,1)} async-done(((bf16[3072,2048]{1,0:T(8,128)(2,1)}), bf16[768,2048]{1,0:T(8,128)(2,1)}) %reduce-scatter.3.cloned.1.call-update) | async-done | bytes 3145744 | tf_op jit(solution)/shard_map/reduce_scatter | solution.py:84
  458.9 6.1 reshape.160
  465.0 10.8 %all-to-all-start.3 = ((bf16[64,12,2048]{2,1,0:T(8,128)(2,1)}), bf16[64,12,2048]{2,1,0:T(8,128)(2,1)}, u32[]{:S(2)}, u32[]{:S(2)}) async-start(bf16[64,12,2048]{2,1,0:T(8,128)(2,1)} %reshape.160), calls=%async_computation.4 | async-start | bytes 8388608 | tf_op jit(solution)/shard_map/all_to_all | solution.py:91
  476.0 11.6 %all-gather.9.cloned.1.call-done = bf16[256,2048]{1,0:T(8,128)(2,1)} async-done(((bf16[64,2048]{1,0:T(8,128)(2,1)}), bf16[256,2048]{1,0:T(8,128)(2,1)}) %all-gather.9.cloned.1.call-update) | async-done | bytes 1048592 | tf_op jit(solution)/shard_map/all_gather | solution.py:101
  487.5 137.4 %all-gather.11.cloned.1.call-done = bf16[2048,704]{1,0:T(8,128)(2,1)} async-done(((bf16[32,704]{1,0:T(8,128)(2,1)}), bf16[2048,704]{1,0:T(8,128)(2,1)}) %all-gather.11.cloned.1.call-update) | async-done | bytes 2883600 | tf_op jit(solution)/shard_map/all_gather | solution.py:97
  625.0 3.5 fusion.33
  628.5 114.5 %all-gather.13.cloned.1.call-done = bf16[2048,704]{1,0:T(8,128)(2,1)} async-done(((bf16[32,704]{1,0:T(8,128)(2,1)}), bf16[2048,704]{1,0:T(8,128)(2,1)}) %all-gather.13.cloned.1.call-update) | async-done | bytes 2883600 | tf_op jit(solution)/shard_map/all_gather | solution.py:98
  742.9 115.5 %all-gather.15.cloned.1.call-done = bf16[2048,704]{1,0:T(8,128)(2,1)} async-done(((bf16[32,704]{1,0:T(8,128)(2,1)}), bf16[2048,704]{1,0:T(8,128)(2,1)}) %all-gather.15.cloned.1.call-update) | async-done | bytes 2883600 | tf_op jit(solution)/shard_map/all_gather | solution.py:99
  858.5 7.6 fusion.7
  866.3 6.2 reshape.161
  872.5 6.7 gather_fusion
  879.2 2.1 reshape.162
  881.3 3.8 multiply_reduce_fusion
  885.2 12.0 %reduce-scatter.5.cloned.1.call-done = f32[64,2048]{1,0:T(8,128)} async-done(((f32[256,2048]{1,0:T(8,128)}), f32[64,2048]{1,0:T(8,128)}) %reduce-scatter.5.cloned.1.call-update) | async-done | bytes 524304 | tf_op jit(solution)/shard_map/reduce_scatter | solution.py:106
  899.3 26.4 %all-gather.17.cloned.1.call-done = bf16[256,2048]{1,0:T(8,128)(2,1)} async-done(((bf16[64,2048]{1,0:T(8,128)(2,1)}), bf16[256,2048]{1,0:T(8,128)(2,1)}) %all-gather.17.cloned.1.call-update) | async-done | bytes 1048592 | tf_op jit(solution)/shard_map/all_gather | solution.py:114
  925.7 2.4 convolution_convert_fusion.1
  (60 shorter events, 11.3 us)
Async XLA Ops:
  7.2 918.6 %copy-start = (bf16[2048,144]{0,1:T(8,128)(2,1)S(1)}, bf16[2048,144]{0,1:T(8,128)(2,1)}, u32[]{:S(2)}) copy-start(bf16[2048,144]{0,1:T(8,128)(2,1)} %param.21) | copy-start | bytes 1769476
  7.2 304.9 %all-gather.7.cloned.1.call-start = ((), (), s32[]{:S(2)}) async-start(), calls=%async_computation.6 | async-start | bytes 15728640 | tf_op jit(solution)/shard_map/all_gather | solution.py:82
  12.9 16.1 %copy-start.3 = (bf16[64,2048]{1,0:T(8,128)(2,1)}, bf16[64,2048]{1,0:T(8,128)(2,1)S(1)}, u32[]{:S(2)}) copy-start(bf16[64,2048]{1,0:T(8,128)(2,1)S(1)} %fusion.18) | copy-start | bytes 786436
  156.9 8.3 copy-start.1
  156.9 60.6 %all-to-all-start.1 = ((bf16[64,32,2,352]{3,1,2,0:T(8,128)(2,1)}), bf16[64,32,2,352]{3,1,2,0:T(8,128)(2,1)}, u32[]{:S(2)}, u32[]{:S(2)}) async-start(bf16[64,32,2,352]{3,1,2,0:T(8,128)(2,1)} %bitcast.34), calls=%async_computation.1 | async-start | bytes 6291456 | tf_op jit(solution)/shard_map/all_to_all | solution.py:56
  217.5 109.7 %all-to-all-start.2 = ((bf16[64,32,352]{2,1,0:T(8,128)(2,1)}), bf16[64,32,352]{2,1,0:T(8,128)(2,1)S(1)}, u32[]{:S(2)}, u32[]{:S(2)}) async-start(bf16[64,32,352]{2,1,0:T(8,128)(2,1)} %bitcast.3), calls=%async_computation.2 | async-start | bytes 3145728 | tf_op jit(solution)/shard_map/all_to_all | solution.py:57
  226.4 232.5 %reduce-scatter.3.cloned.1.call-start = ((), (), s32[]{:S(2)}) async-start(), calls=%async_computation.7 | async-start | bytes 15728640 | tf_op jit(solution)/shard_map/reduce_scatter | solution.py:84
  340.7 146.9 %all-gather.9.cloned.1.call-start = ((), (), s32[]{:S(2)}) async-start(), calls=%async_computation.8 | async-start | bytes 1310720 | tf_op jit(solution)/shard_map/all_gather | solution.py:101
  341.4 283.5 %all-gather.11.cloned.1.call-start = ((), (), s32[]{:S(2)}) async-start(), calls=%async_computation.9 | async-start | bytes 3194880 | tf_op jit(solution)/shard_map/all_gather | solution.py:97
  342.0 400.9 %all-gather.13.cloned.1.call-start = ((), (), s32[]{:S(2)}) async-start(), calls=%async_computation.10 | async-start | bytes 3194880 | tf_op jit(solution)/shard_map/all_gather | solution.py:98
  342.6 515.9 %all-gather.15.cloned.1.call-start = ((), (), s32[]{:S(2)}) async-start(), calls=%async_computation.11 | async-start | bytes 3194880 | tf_op jit(solution)/shard_map/all_gather | solution.py:99
  465.0 401.4 %all-to-all-start.3 = ((bf16[64,12,2048]{2,1,0:T(8,128)(2,1)}), bf16[64,12,2048]{2,1,0:T(8,128)(2,1)}, u32[]{:S(2)}, u32[]{:S(2)}) async-start(bf16[64,12,2048]{2,1,0:T(8,128)(2,1)} %reshape.160), calls=%async_computation.4 | async-start | bytes 8388608 | tf_op jit(solution)/shard_map/all_to_all | solution.py:91
  475.7 421.4 %reduce-scatter.5.cloned.1.call-start = ((), (), s32[]{:S(2)}) async-start(), calls=%async_computation.12 | async-start | bytes 2621440 | tf_op jit(solution)/shard_map/reduce_scatter | solution.py:106
  487.5 370.9 %copy-start.7 = (bf16[256,2048]{1,0:T(8,128)(2,1)S(1)}, bf16[256,2048]{1,0:T(8,128)(2,1)}, u32[]{:S(2)}) copy-start(bf16[256,2048]{1,0:T(8,128)(2,1)} %all-gather.9.cloned.1.call-done) | copy-start | bytes 3145732
  628.5 237.7 %copy-start.5 = (s32[64,6]{0,1:T(8,128)S(1)}, s32[64,6]{0,1:T(8,128)}, u32[]{:S(2)}) copy-start(s32[64,6]{0,1:T(8,128)} %param.16) | copy-start | bytes 4612
  866.1 59.6 %all-gather.17.cloned.1.call-start = ((), (), s32[]{:S(2)}) async-start(), calls=%async_computation.13 | async-start | bytes 1310720 | tf_op jit(solution)/shard_map/all_gather | solution.py:114
  881.3 15.8 %copy-start.2 = (bf16[64,2048]{1,0:T(8,128)(2,1)S(1)}, bf16[64,2048]{1,0:T(8,128)(2,1)}, u32[]{:S(2)}) copy-start(bf16[64,2048]{1,0:T(8,128)(2,1)} %param.11) | copy-start | bytes 786436
  881.3 17.1 %copy-start.6 = (f32[2048]{0:T(1024)S(1)}, f32[2048]{0:T(1024)}, u32[]{:S(2)}) copy-start(f32[2048]{0:T(1024)} %param.20) | copy-start | bytes 24580
  898.4 29.7 %copy-start.4 = (bf16[64,2048]{1,0:T(8,128)(2,1)}, bf16[64,2048]{1,0:T(8,128)(2,1)S(1)}, u32[]{:S(2)}) copy-start(bf16[64,2048]{1,0:T(8,128)(2,1)S(1)} %get-tuple-element.3) | copy-start | bytes 786436
Sparse Core Ops, SparseCore 0:
  144.1 167.8 all-gather.6
  340.8 118.0 reduce-scatter.2
  461.3 26.2 all-gather.8
  489.3 135.6 all-gather.10
  626.7 116.2 all-gather.12
  744.7 113.7 all-gather.14
  866.2 30.8 reduce-scatter.4
  899.4 26.2 all-gather.16
where the time goes:
time: 945 us; the launch traced here: 935 us
  waiting for transfers between devices  657 us (70%)
  blocking collectives  109 us (12%)
  local copies, waits for them, and re-layouts  70 us (7%)
  matrix products  42.1 us (4%)
  starting transfers between devices  28.5 us (3%)
  between operations  14.6 us (2%)
  other arithmetic  14.5 us (2%)
    all_gather x1, waiting for transfers between devices, on_device(): lax.all_gather(shared_gate, ('dp', 'expert'), axis=0, tiled=True)  137 us
    reduce_scatter x1, waiting for transfers between devices, on_device(): lax.psum_scatter(expert_part(rows, gate_up_w, down_w).astype(jnp.bfloat16...  116 us
    all_gather x1, waiting for transfers between devices, on_device(): lax.all_gather(shared_down, ('dp', 'expert'), axis=0, tiled=True)  116 us
    all_gather x1, waiting for transfers between devices, on_device(): lax.all_gather(shared_up, ('dp', 'expert'), axis=0, tiled=True)  114 us
    all_to_all x1, blocking collectives, on_device(): lax.all_to_all(send.reshape(n_groups, capacity, width), ('dp', 'expert'),...  109 us
    all_gather x1, waiting for transfers between devices, on_device(): every_slot = lax.all_gather(slots_here, 'mp', axis=0, tiled=True)  70.9 us
    all_to_all x1, waiting for transfers between devices, on_device(): lax.all_to_all(in_send, ('expert', 'mp'), split_axis=0, concat_axis=1, ti...  50.3 us
    all_gather x1, waiting for transfers between devices, on_device(): next_group = lax.all_gather(next_rows, 'mp', axis=0, tiled=True)  26.4 us
  transfers between devices with their start and end apart: 11, of which 9 were waited for; matrix products, arithmetic and copies ran while one was open for 9% of the time, Pallas kernels for 0%

commit v1 on v0

--- a/solution.py
+++ b/solution.py
@@ -93,11 +93,14 @@
     ).reshape(n_groups * capacity, width)
     picked = back[target].reshape(tok_rows, top, width)
     routed = jnp.sum(picked.astype(jnp.float32) * gate_weights[:, :, None], axis=1)
-    gate_w, up_w, down_s = (
-        lax.all_gather(shared_gate, ("dp", "expert"), axis=0, tiled=True),
-        lax.all_gather(shared_up, ("dp", "expert"), axis=0, tiled=True),
-        lax.all_gather(shared_down, ("dp", "expert"), axis=0, tiled=True),
-    )
+    shared_cols = shared_gate.shape[1]
+    shared_cat = jnp.concatenate([shared_gate, shared_up, shared_down], axis=1)
+    shared_cat = lax.all_gather(shared_cat, "dp", axis=0, tiled=False)
+    shared_cat = lax.all_gather(shared_cat, "expert", axis=1, tiled=False)
+    shared_cat = shared_cat.reshape(width, 3 * shared_cols)
+    gate_w = shared_cat[:, :shared_cols]
+    up_w = shared_cat[:, shared_cols : 2 * shared_cols]
+    down_s = shared_cat[:, 2 * shared_cols :]
     group_rows = lax.all_gather(normed, "mp", axis=0, tiled=True)
     rows = group_rows
     gate_part = jnp.dot(rows, gate_w, preferred_element_type=jnp.float32)

time: 945 us -> 702 us (0.74)
  waiting for transfers between devices: 657 us -> 391 us
  blocking collectives: 109 us -> 130 us
    all_gather x3 -> x1, waiting for transfers between devices: 367 us -> 121 us  [on_device(): shared_cat = lax.all_gather(shared_cat, 'expert', axis=1, tiled=False)]
    all_gather x0 -> x1, blocking collectives: none -> 21.1 us  [on_device(): shared_cat = lax.all_gather(shared_cat, 'dp', axis=0, tiled=False)]
    reduce_scatter x1, waiting for transfers between devices: 116 us -> 96.2 us  [on_device(): lax.psum_scatter(expert_part(rows, gate_up_w, down_w).astype(jnp.bfloat16...]
  transfers between devices with their start and end apart: 11 -> 9, of which waited for: 9 -> 7; matrix products, arithmetic and copies ran while one was open for 9% -> 12% of each run, Pallas kernels for 0% -> 0%
where the time goes in v1:
time: 702 us; the launch traced here: 692 us
  waiting for transfers between devices  391 us (56%)
  blocking collectives  130 us (19%)
  local copies, waits for them, and re-layouts  70.2 us (10%)
  matrix products  43.3 us (6%)
  starting transfers between devices  28.4 us (4%)
  between operations  14.8 us (2%)
  other arithmetic  14.5 us (2%)
    all_gather x1, waiting for transfers between devices, on_device(): shared_cat = lax.all_gather(shared_cat, 'expert', axis=1, tiled=False)  121 us
    all_to_all x1, blocking collectives, on_device(): lax.all_to_all(send.reshape(n_groups, capacity, width), ('dp', 'expert'),...  109 us
    reduce_scatter x1, waiting for transfers between devices, on_device(): lax.psum_scatter(expert_part(rows, gate_up_w, down_w).astype(jnp.bfloat16...  96.2 us
    all_gather x1, waiting for transfers between devices, on_device(): every_slot = lax.all_gather(slots_here, 'mp', axis=0, tiled=True)  70.9 us
    all_to_all x1, waiting for transfers between devices, on_device(): lax.all_to_all(in_send, ('expert', 'mp'), split_axis=0, concat_axis=1, ti...  50.3 us
    all_gather x1, waiting for transfers between devices, on_device(): next_group = lax.all_gather(next_rows, 'mp', axis=0, tiled=True)  26.4 us
    all_gather x1, blocking collectives, on_device(): shared_cat = lax.all_gather(shared_cat, 'dp', axis=0, tiled=False)  21.1 us
    dot_general x1, matrix products, expert_part(): gate_up = jnp.dot(rows, gate_up_w, preferred_element_type=jnp.float32)  15.1 us
  transfers between devices with their start and end apart: 9, of which 7 were waited for; matrix products, arithmetic and copies ran while one was open for 12% of the time, Pallas kernels for 0%

profile of v1, /device:TPU:8, one launch (start us, length us, event | category | flops | bytes accessed | tf_op | source)
XLA Modules:
  0.0 692.2 jit_solution(3124470099262172469)
XLA Ops:
  12.9 10.0 %scatter_custom_fusion = bf16[768,2048]{1,0:T(8,128)(2,1)} fusion(s32[384]{0:T(512)S(1)} %fusion.38, bf16[64,2048]{1,0:T(8,128)(2,1)S(1)} %fusion.30, s32[1024]{0:T(1024)S(1)} %pad_clamp_fusion.1, bf16[]{:T(256)} %constant.12.clone.1), kind=kCustom, calls=%fused_computation.15 | custom fusion | bytes 3145730 | tf_op jit(solution)/shard_map/scatter | solution.py:72
  22.8 6.1 reshape.156
  28.9 108.6 %all_to_all.28 = bf16[64,12,2048]{2,1,0:T(8,128)(2,1)} all-to-all(bf16[64,12,2048]{2,1,0:T(8,128)(2,1)} %reshape.156), channel_id=1, replica_groups=mesh['dp'=4,'expert'=16,'mp'=4] {'dp','expert'}, dimensions={0} | all-to-all | bytes 6291456 | tf_op jit(solution)/shard_map/all_to_all | solution.py:74
  137.5 6.2 reshape.157
  143.7 3.0 convert_element_type.54
  146.7 5.1 reshape.158
  151.8 4.8 copy.24
  156.6 8.3 %all-to-all-start.1 = ((bf16[64,32,2,352]{3,1,2,0:T(8,128)(2,1)}), bf16[64,32,2,352]{3,1,2,0:T(8,128)(2,1)}, u32[]{:S(2)}, u32[]{:S(2)}) async-start(bf16[64,32,2,352]{3,1,2,0:T(8,128)(2,1)} %bitcast.33), calls=%async_computation.1 | async-start | bytes 6291456 | tf_op jit(solution)/shard_map/all_to_all | solution.py:56
  165.5 1.4 pad_maximum_fusion
  166.9 50.3 %all-to-all-done.1 = bf16[64,32,2,352]{3,1,2,0:T(8,128)(2,1)} async-done(((bf16[64,32,2,352]{3,1,2,0:T(8,128)(2,1)}), bf16[64,32,2,352]{3,1,2,0:T(8,128)(2,1)}, u32[]{:S(2)}, u32[]{:S(2)}) %all-to-all-start.1) | async-done | bytes 2883616 | tf_op jit(solution)/shard_map/all_to_all | solution.py:56
  217.2 8.9 %all-to-all-start.2 = ((bf16[64,32,352]{2,1,0:T(8,128)(2,1)}), bf16[64,32,352]{2,1,0:T(8,128)(2,1)S(1)}, u32[]{:S(2)}, u32[]{:S(2)}) async-start(bf16[64,32,352]{2,1,0:T(8,128)(2,1)} %bitcast.3), calls=%async_computation.2 | async-start | bytes 3145728 | tf_op jit(solution)/shard_map/all_to_all | solution.py:57
  226.2 6.9 copy.25
  233.0 7.8 %reshape.160 = bf16[2048,704]{1,0:T(8,128)(2,1)} reshape(bf16[64,32,2,352]{3,2,1,0:T(2,128)(2,1)} %copy.25) | data formatting | bytes 5767168 | tf_op jit(solution)/shard_map/reshape | solution.py:59
  240.9 70.9 %all-gather.7.cloned.1.call-done = bf16[3072,2048]{1,0:T(8,128)(2,1)} async-done(((bf16[768,2048]{1,0:T(8,128)(2,1)}), bf16[3072,2048]{1,0:T(8,128)(2,1)}) %all-gather.7.cloned.1.call-update) | async-done | bytes 12582928 | tf_op jit(solution)/shard_map/all_gather | solution.py:82
  311.7 15.1 %fusion.44 = f32[3072,704]{0,1:T(8,128)} fusion(bf16[3072,2048]{1,0:T(8,128)(2,1)} %all-gather.7.cloned.1.call-done, bf16[2048,704]{1,0:T(8,128)(2,1)} %reshape.160), kind=kOutput, calls=%fused_computation.67 | convolution fusion | flops 8858370048 | bytes 24117248 | tf_op jit(solution)/shard_map/dot_general | solution.py:15
  326.9 13.5 %convolution_convert_fusion = bf16[3072,2048]{1,0:T(8,128)(2,1)} fusion(bf16[2048,352]{1,0:T(8,128)(2,1)S(1)} %bitcast.36, f32[3072,704]{0,1:T(8,128)} %fusion.44), kind=kOutput, calls=%fused_computation.3 | convolution fusion | flops 4441964544 | bytes 22675456 | tf_op jit(solution)/shard_map/dot_general | solution.py:17
  341.3 21.1 %all-gather = bf16[128,2112]{1,0:T(8,128)(2,1)} all-gather(bf16[32,2112]{1,0:T(8,128)(2,1)S(1)} %concatenate.7), channel_id=2, replica_groups=mesh['dp'=4,'expert'=16,'mp'=4] {'dp'}, dimensions={0}, use_global_device_ids=true | all-gather | bytes 675840 | tf_op jit(solution)/shard_map/all_gather | solution.py:98
  362.4 96.2 %reduce-scatter.3.cloned.1.call-done = bf16[768,2048]{1,0:T(8,128)(2,1)} async-done(((bf16[3072,2048]{1,0:T(8,128)(2,1)}), bf16[768,2048]{1,0:T(8,128)(2,1)}) %reduce-scatter.3.cloned.1.call-update) | async-done | bytes 3145744 | tf_op jit(solution)/shard_map/reduce_scatter | solution.py:84
  458.6 6.1 reshape.163
  464.7 10.7 %all-to-all-start.3 = ((bf16[64,12,2048]{2,1,0:T(8,128)(2,1)}), bf16[64,12,2048]{2,1,0:T(8,128)(2,1)}, u32[]{:S(2)}, u32[]{:S(2)}) async-start(bf16[64,12,2048]{2,1,0:T(8,128)(2,1)} %reshape.163), calls=%async_computation.4 | async-start | bytes 8388608 | tf_op jit(solution)/shard_map/all_to_all | solution.py:91
  475.7 11.6 %all-gather.9.cloned.1.call-done = bf16[256,2048]{1,0:T(8,128)(2,1)} async-done(((bf16[64,2048]{1,0:T(8,128)(2,1)}), bf16[256,2048]{1,0:T(8,128)(2,1)}) %all-gather.9.cloned.1.call-update) | async-done | bytes 1048592 | tf_op jit(solution)/shard_map/all_gather | solution.py:104
  487.3 121.1 %all-gather.13.cloned.1.call-done = bf16[4,512,2112]{2,1,0:T(8,128)(2,1)} async-done(((bf16[4,32,2112]{2,1,0:T(8,128)(2,1)}), bf16[4,512,2112]{2,1,0:T(8,128)(2,1)}) %all-gather.13.cloned.1.call-update) | async-done | bytes 8650768 | tf_op jit(solution)/shard_map/all_gather | solution.py:99
  608.4 3.5 fusion.5
  611.9 8.8 %fusion.1 = f32[256,2048]{1,0:T(8,128)} fusion(bf16[2048,2112]{1,0:T(8,128)(2,1)} %bitcast.39, bf16[256,2048]{1,0:T(8,128)(2,1)S(1)} %copy-done.10, f32[256,704]{0,1:T(8,128)S(1)} %fusion.5), kind=kOutput, calls=%fused_computation.7 | convolution fusion | flops 1477476352 | bytes 10158080 | tf_op jit(solution)/shard_map/dot_general | solution.py:110
  620.9 6.2 reshape.164
  627.1 6.7 gather_fusion
  633.8 2.1 reshape.166
  635.9 3.8 multiply_reduce_fusion
  639.7 14.3 %reduce-scatter.5.cloned.1.call-done = f32[64,2048]{1,0:T(8,128)} async-done(((f32[256,2048]{1,0:T(8,128)}), f32[64,2048]{1,0:T(8,128)}) %reduce-scatter.5.cloned.1.call-update) | async-done | bytes 524304 | tf_op jit(solution)/shard_map/reduce_scatter | solution.py:109
  654.0 1.2 fusion.25
  656.1 26.4 %all-gather.11.cloned.1.call-done = bf16[256,2048]{1,0:T(8,128)(2,1)} async-done(((bf16[64,2048]{1,0:T(8,128)(2,1)}), bf16[256,2048]{1,0:T(8,128)(2,1)}) %all-gather.11.cloned.1.call-update) | async-done | bytes 1048592 | tf_op jit(solution)/shard_map/all_gather | solution.py:117
  682.6 2.4 convolution_convert_fusion.1
  (62 shorter events, 8.6 us)
Async XLA Ops:
  7.2 675.4 %copy-start = (bf16[2048,144]{0,1:T(8,128)(2,1)S(1)}, bf16[2048,144]{0,1:T(8,128)(2,1)}, u32[]{:S(2)}) copy-start(bf16[2048,144]{0,1:T(8,128)(2,1)} %param.21) | copy-start | bytes 1769476
  7.2 304.6 %all-gather.7.cloned.1.call-start = ((), (), s32[]{:S(2)}) async-start(), calls=%async_computation.6 | async-start | bytes 15728640 | tf_op jit(solution)/shard_map/all_gather | solution.py:82
  12.9 16.1 %copy-start.3 = (bf16[64,2048]{1,0:T(8,128)(2,1)}, bf16[64,2048]{1,0:T(8,128)(2,1)S(1)}, u32[]{:S(2)}) copy-start(bf16[64,2048]{1,0:T(8,128)(2,1)S(1)} %fusion.30) | copy-start | bytes 786436
  156.6 8.3 %copy-start.1 = (f32[16,32,1408]{2,1,0:T(8,128)S(1)}, f32[16,32,1408]{2,1,0:T(8,128)}, u32[]{:S(2)}) copy-start(f32[16,32,1408]{2,1,0:T(8,128)} %param.14) | copy-start | bytes 8650756
  156.6 60.6 %all-to-all-start.1 = ((bf16[64,32,2,352]{3,1,2,0:T(8,128)(2,1)}), bf16[64,32,2,352]{3,1,2,0:T(8,128)(2,1)}, u32[]{:S(2)}, u32[]{:S(2)}) async-start(bf16[64,32,2,352]{3,1,2,0:T(8,128)(2,1)} %bitcast.33), calls=%async_computation.1 | async-start | bytes 6291456 | tf_op jit(solution)/shard_map/all_to_all | solution.py:56
  217.2 109.7 %all-to-all-start.2 = ((bf16[64,32,352]{2,1,0:T(8,128)(2,1)}), bf16[64,32,352]{2,1,0:T(8,128)(2,1)S(1)}, u32[]{:S(2)}, u32[]{:S(2)}) async-start(bf16[64,32,352]{2,1,0:T(8,128)(2,1)} %bitcast.3), calls=%async_computation.2 | async-start | bytes 3145728 | tf_op jit(solution)/shard_map/all_to_all | solution.py:57
  226.1 232.5 %reduce-scatter.3.cloned.1.call-start = ((), (), s32[]{:S(2)}) async-start(), calls=%async_computation.7 | async-start | bytes 15728640 | tf_op jit(solution)/shard_map/reduce_scatter | solution.py:84
  340.4 0.8 copy-start.5
  340.4 0.8 copy-start.6
  340.4 0.8 copy-start.7
  340.4 146.9 %all-gather.9.cloned.1.call-start = ((), (), s32[]{:S(2)}) async-start(), calls=%async_computation.8 | async-start | bytes 1310720 | tf_op jit(solution)/shard_map/all_gather | solution.py:104
  341.1 267.2 %all-gather.13.cloned.1.call-start = ((), (), s32[]{:S(2)}) async-start(), calls=%async_computation.11 | async-start | bytes 9469952 | tf_op jit(solution)/shard_map/all_gather | solution.py:99
  464.7 156.2 %all-to-all-start.3 = ((bf16[64,12,2048]{2,1,0:T(8,128)(2,1)}), bf16[64,12,2048]{2,1,0:T(8,128)(2,1)}, u32[]{:S(2)}, u32[]{:S(2)}) async-start(bf16[64,12,2048]{2,1,0:T(8,128)(2,1)} %reshape.163), calls=%async_computation.4 | async-start | bytes 8388608 | tf_op jit(solution)/shard_map/all_to_all | solution.py:91
  475.4 178.5 %reduce-scatter.5.cloned.1.call-start = ((), (), s32[]{:S(2)}) async-start(), calls=%async_computation.9 | async-start | bytes 2621440 | tf_op jit(solution)/shard_map/reduce_scatter | solution.py:109
  487.3 124.6 %copy-start.10 = (bf16[256,2048]{1,0:T(8,128)(2,1)S(1)}, bf16[256,2048]{1,0:T(8,128)(2,1)}, u32[]{:S(2)}) copy-start(bf16[256,2048]{1,0:T(8,128)(2,1)} %all-gather.9.cloned.1.call-done) | copy-start | bytes 3145732
  611.9 8.8 %copy-start.8 = (s32[64,6]{0,1:T(8,128)S(1)}, s32[64,6]{0,1:T(8,128)}, u32[]{:S(2)}) copy-start(s32[64,6]{0,1:T(8,128)} %param.16) | copy-start | bytes 4612
  620.7 61.9 %all-gather.11.cloned.1.call-start = ((), (), s32[]{:S(2)}) async-start(), calls=%async_computation.10 | async-start | bytes 1310720 | tf_op jit(solution)/shard_map/all_gather | solution.py:117
  635.9 18.1 %copy-start.2 = (bf16[64,2048]{1,0:T(8,128)(2,1)S(1)}, bf16[64,2048]{1,0:T(8,128)(2,1)}, u32[]{:S(2)}) copy-start(bf16[64,2048]{1,0:T(8,128)(2,1)} %param.11) | copy-start | bytes 786436
  635.9 19.3 %copy-start.9 = (f32[2048]{0:T(1024)S(1)}, f32[2048]{0:T(1024)}, u32[]{:S(2)}) copy-start(f32[2048]{0:T(1024)} %param.20) | copy-start | bytes 24580
  655.2 29.7 %copy-start.4 = (bf16[64,2048]{1,0:T(8,128)(2,1)}, bf16[64,2048]{1,0:T(8,128)(2,1)S(1)}, u32[]{:S(2)}) copy-start(bf16[64,2048]{1,0:T(8,128)(2,1)S(1)} %get-tuple-element.3) | copy-start | bytes 786436
Sparse Core Ops, SparseCore 0:
  143.8 167.8 all-gather.6
  340.5 118.0 reduce-scatter.2
  461.0 26.2 all-gather.8
  489.0 119.3 all-gather.12
  620.8 33.1 reduce-scatter.4
  656.3 26.2 all-gather.10

commit v2 on v1

--- a/solution.py
+++ b/solution.py
@@ -78,6 +78,15 @@
         concat_axis=0,
         tiled=True,
     )
+    shared_cols = shared_gate.shape[1]
+    shared_cat = jnp.concatenate([shared_gate, shared_up, shared_down], axis=1)
+    shared_cat = lax.all_gather(shared_cat, "dp", axis=0, tiled=False)
+    shared_cat = lax.all_gather(shared_cat, "expert", axis=1, tiled=False)
+    shared_cat = shared_cat.reshape(width, 3 * shared_cols)
+    group_rows = lax.all_gather(normed, "mp", axis=0, tiled=True)
+    received, shared_cat, group_rows = lax.optimization_barrier(
+        (received, shared_cat, group_rows)
+    )
     slots_here = received.reshape(n_groups * capacity, width)
     every_slot = lax.all_gather(slots_here, "mp", axis=0, tiled=True)
     rows = every_slot
@@ -93,15 +102,9 @@
     ).reshape(n_groups * capacity, width)
     picked = back[target].reshape(tok_rows, top, width)
     routed = jnp.sum(picked.astype(jnp.float32) * gate_weights[:, :, None], axis=1)
-    shared_cols = shared_gate.shape[1]
-    shared_cat = jnp.concatenate([shared_gate, shared_up, shared_down], axis=1)
-    shared_cat = lax.all_gather(shared_cat, "dp", axis=0, tiled=False)
-    shared_cat = lax.all_gather(shared_cat, "expert", axis=1, tiled=False)
-    shared_cat = shared_cat.reshape(width, 3 * shared_cols)
     gate_w = shared_cat[:, :shared_cols]
     up_w = shared_cat[:, shared_cols : 2 * shared_cols]
     down_s = shared_cat[:, 2 * shared_cols :]
-    group_rows = lax.all_gather(normed, "mp", axis=0, tiled=True)
     rows = group_rows
     gate_part = jnp.dot(rows, gate_w, preferred_element_type=jnp.float32)
     up_part = jnp.dot(rows, up_w, preferred_element_type=jnp.float32)

time: 702 us -> 686 us (0.977)
  blocking collectives: 130 us -> 21.2 us
  waiting for transfers between devices: 391 us -> 470 us
  starting transfers between devices: 28.4 us -> 42.4 us
    all_to_all x0 -> x1, waiting for transfers between devices: none -> 125 us  [on_device(): lax.all_to_all(send.reshape(n_groups, capacity, width), ('dp', 'expert'),...]
    all_gather x1, waiting for transfers between devices: 121 us -> 0.01 us  [on_device(): shared_cat = lax.all_gather(shared_cat, 'expert', axis=1, tiled=False)]
    all_to_all x1 -> x0, blocking collectives: 109 us -> none  [on_device(): lax.all_to_all(send.reshape(n_groups, capacity, width), ('dp', 'expert'),...]
    all_to_all x1, waiting for transfers between devices: 0.01 us -> 83.6 us  [on_device(): lax.all_to_all(result, ('dp', 'expert'), split_axis=0, concat_axis=0, til...]
    reduce_scatter x1, waiting for transfers between devices: 96.2 us -> 118 us  [on_device(): lax.psum_scatter(expert_part(rows, gate_up_w, down_w).astype(jnp.bfloat16...]
    reduce_scatter x1, waiting for transfers between devices: 14.3 us -> 0.02 us  [on_device(): lax.psum_scatter(lax.dot_general(act, down_s, (((1,), (1,)), ((), ())), p...]
    all_gather x1, waiting for transfers between devices: 11.6 us -> 0.02 us  [on_device(): group_rows = lax.all_gather(normed, 'mp', axis=0, tiled=True)]
    all_to_all x0 -> x1, starting transfers between devices: none -> 8.72 us  [on_device(): lax.all_to_all(send.reshape(n_groups, capacity, width), ('dp', 'expert'),...]
  transfers between devices with their start and end apart: 9 -> 10, of which waited for: 7 -> 6; matrix products, arithmetic and copies ran while one was open for 12% -> 14% of each run, Pallas kernels for 0% -> 0%
where the time goes in v2:
time: 686 us; the launch traced here: 678 us
  waiting for transfers between devices  470 us (69%)
  local copies, waits for them, and re-layouts  71.1 us (10%)
  matrix products  43 us (6%)
  starting transfers between devices  42.4 us (6%)
  blocking collectives  21.2 us (3%)
  other arithmetic  15.3 us (2%)
  between operations  14.8 us (2%)
    all_to_all x1, waiting for transfers between devices, on_device(): lax.all_to_all(send.reshape(n_groups, capacity, width), ('dp', 'expert'),...  125 us
    reduce_scatter x1, waiting for transfers between devices, on_device(): lax.psum_scatter(expert_part(rows, gate_up_w, down_w).astype(jnp.bfloat16...  118 us
    all_to_all x1, waiting for transfers between devices, on_device(): lax.all_to_all(result, ('dp', 'expert'), split_axis=0, concat_axis=0, til...  83.6 us
    all_gather x1, waiting for transfers between devices, on_device(): every_slot = lax.all_gather(slots_here, 'mp', axis=0, tiled=True)  71.1 us
    all_to_all x1, waiting for transfers between devices, on_device(): lax.all_to_all(in_send, ('expert', 'mp'), split_axis=0, concat_axis=1, ti...  50.2 us
    all_gather x1, waiting for transfers between devices, on_device(): next_group = lax.all_gather(next_rows, 'mp', axis=0, tiled=True)  21.3 us
    all_gather x1, blocking collectives, on_device(): shared_cat = lax.all_gather(shared_cat, 'dp', axis=0, tiled=False)  21.2 us
    dot_general x1, matrix products, expert_part(): gate_up = jnp.dot(rows, gate_up_w, preferred_element_type=jnp.float32)  15.2 us
  transfers between devices with their start and end apart: 10, of which 6 were waited for; matrix products, arithmetic and copies ran while one was open for 14% of the time, Pallas kernels for 0%

profile of v2, /device:TPU:8, one launch (start us, length us, event | category | flops | bytes accessed | tf_op | source)
XLA Modules:
  0.0 677.7 jit_solution(15276062408479485813)
XLA Ops:
  8.4 1.8 fusion.30
  11.2 21.2 %all-gather = bf16[128,2112]{1,0:T(8,128)(2,1)} all-gather(bf16[32,2112]{1,0:T(8,128)(2,1)S(1)} %concatenate.6), channel_id=2, replica_groups=mesh['dp'=4,'expert'=16,'mp'=4] {'dp'}, dimensions={0}, use_global_device_ids=true | all-gather | bytes 675840 | tf_op jit(solution)/shard_map/all_gather | solution.py:83
  35.8 10.6 %scatter_custom_fusion = bf16[768,2048]{1,0:T(8,128)(2,1)} fusion(s32[384]{0:T(512)S(1)} %fusion.38, bf16[64,2048]{1,0:T(8,128)(2,1)} %fusion.30, s32[1024]{0:T(1024)S(1)} %pad_clamp_fusion.1, bf16[]{:T(256)} %constant.12.clone.1), kind=kCustom, calls=%fused_computation.15 | custom fusion | bytes 3146240 | tf_op jit(solution)/shard_map/scatter | solution.py:72
  46.4 6.1 reshape.156
  52.5 8.7 %all-to-all-start = ((bf16[64,12,2048]{2,1,0:T(8,128)(2,1)}), bf16[64,12,2048]{2,1,0:T(8,128)(2,1)}, u32[]{:S(2)}, u32[]{:S(2)}) async-start(bf16[64,12,2048]{2,1,0:T(8,128)(2,1)} %reshape.156), calls=%async_computation | async-start | bytes 8388608 | tf_op jit(solution)/shard_map/all_to_all | solution.py:74
  61.5 125.4 %all-to-all-done = bf16[64,12,2048]{2,1,0:T(8,128)(2,1)} async-done(((bf16[64,12,2048]{2,1,0:T(8,128)(2,1)}), bf16[64,12,2048]{2,1,0:T(8,128)(2,1)}, u32[]{:S(2)}, u32[]{:S(2)}) %all-to-all-start) | async-done | bytes 3145760 | tf_op jit(solution)/shard_map/all_to_all | solution.py:74
  186.9 6.1 reshape.158
  193.1 3.0 convert_element_type.54
  196.1 5.1 reshape.159
  201.1 4.4 copy.24
  205.5 13.2 %all-to-all-start.1 = ((bf16[64,32,2,352]{3,1,2,0:T(8,128)(2,1)}), bf16[64,32,2,352]{3,1,2,0:T(8,128)(2,1)}, u32[]{:S(2)}, u32[]{:S(2)}) async-start(bf16[64,32,2,352]{3,1,2,0:T(8,128)(2,1)} %bitcast.33), calls=%async_computation.1 | async-start | bytes 6291456 | tf_op jit(solution)/shard_map/all_to_all | solution.py:56
  219.4 1.4 pad_maximum_fusion
  220.8 50.2 %all-to-all-done.1 = bf16[64,32,2,352]{3,1,2,0:T(8,128)(2,1)} async-done(((bf16[64,32,2,352]{3,1,2,0:T(8,128)(2,1)}), bf16[64,32,2,352]{3,1,2,0:T(8,128)(2,1)}, u32[]{:S(2)}, u32[]{:S(2)}) %all-to-all-start.1) | async-done | bytes 2883616 | tf_op jit(solution)/shard_map/all_to_all | solution.py:56
  271.1 8.9 %all-to-all-start.2 = ((bf16[64,32,352]{2,1,0:T(8,128)(2,1)}), bf16[64,32,352]{2,1,0:T(8,128)(2,1)S(1)}, u32[]{:S(2)}, u32[]{:S(2)}) async-start(bf16[64,32,352]{2,1,0:T(8,128)(2,1)} %bitcast.5), calls=%async_computation.2 | async-start | bytes 3145728 | tf_op jit(solution)/shard_map/all_to_all | solution.py:57
  280.0 6.8 %copy.25 = bf16[64,32,2,352]{3,2,1,0:T(2,128)(2,1)} copy(bf16[64,32,2,352]{3,1,2,0:T(8,128)(2,1)} %all-to-all-done.1) | data formatting | bytes 5767168 | tf_op jit(solution)/shard_map/all_to_all | solution.py:56
  286.8 7.8 %reshape.161 = bf16[2048,704]{1,0:T(8,128)(2,1)} reshape(bf16[64,32,2,352]{3,2,1,0:T(2,128)(2,1)} %copy.25) | data formatting | bytes 5767168 | tf_op jit(solution)/shard_map/reshape | solution.py:59
  294.7 71.1 %all-gather.9.cloned.1.call-done = bf16[3072,2048]{1,0:T(8,128)(2,1)} async-done(((bf16[768,2048]{1,0:T(8,128)(2,1)}), bf16[3072,2048]{1,0:T(8,128)(2,1)}) %all-gather.9.cloned.1.call-update) | async-done | bytes 12582928 | tf_op jit(solution)/shard_map/all_gather | solution.py:91
  365.8 15.2 %fusion.44 = f32[3072,704]{0,1:T(8,128)} fusion(bf16[3072,2048]{1,0:T(8,128)(2,1)} %all-gather.9.cloned.1.call-done, bf16[2048,704]{1,0:T(8,128)(2,1)} %reshape.161), kind=kOutput, calls=%fused_computation.67 | convolution fusion | flops 8858370048 | bytes 24117248 | tf_op jit(solution)/shard_map/dot_general | solution.py:15
  381.0 13.5 %convolution_convert_fusion = bf16[3072,2048]{1,0:T(8,128)(2,1)} fusion(bf16[2048,352]{1,0:T(8,128)(2,1)S(1)} %bitcast.36, f32[3072,704]{0,1:T(8,128)} %fusion.44), kind=kOutput, calls=%fused_computation.3 | convolution fusion | flops 4441964544 | bytes 22675456 | tf_op jit(solution)/shard_map/dot_general | solution.py:17
  394.5 118.2 %reduce-scatter.3.cloned.1.call-done = bf16[768,2048]{1,0:T(8,128)(2,1)} async-done(((bf16[3072,2048]{1,0:T(8,128)(2,1)}), bf16[768,2048]{1,0:T(8,128)(2,1)}) %reduce-scatter.3.cloned.1.call-update) | async-done | bytes 3145744 | tf_op jit(solution)/shard_map/reduce_scatter | solution.py:93
  512.7 6.1 reshape.164
  518.8 10.9 %all-to-all-start.3 = ((bf16[64,12,2048]{2,1,0:T(8,128)(2,1)}), bf16[64,12,2048]{2,1,0:T(8,128)(2,1)}, u32[]{:S(2)}, u32[]{:S(2)}) async-start(bf16[64,12,2048]{2,1,0:T(8,128)(2,1)} %reshape.164), calls=%async_computation.4 | async-start | bytes 8388608 | tf_op jit(solution)/shard_map/all_to_all | solution.py:100
  530.0 3.2 fusion.5
  533.2 8.8 %fusion.1 = f32[256,2048]{1,0:T(8,128)} fusion(bf16[2048,2112]{1,0:T(8,128)(2,1)} %bitcast.39, bf16[256,2048]{1,0:T(8,128)(2,1)S(1)} %copy-done.6, f32[256,704]{0,1:T(8,128)S(1)} %fusion.5), kind=kOutput, calls=%fused_computation.7 | convolution fusion | flops 1477476352 | bytes 10158080 | tf_op jit(solution)/shard_map/dot_general | solution.py:113
  542.2 83.6 %all-to-all-done.3 = bf16[64,12,2048]{2,1,0:T(8,128)(2,1)} async-done(((bf16[64,12,2048]{2,1,0:T(8,128)(2,1)}), bf16[64,12,2048]{2,1,0:T(8,128)(2,1)}, u32[]{:S(2)}, u32[]{:S(2)}) %all-to-all-start.3) | async-done | bytes 3145760 | tf_op jit(solution)/shard_map/all_to_all | solution.py:100
  625.8 6.2 reshape.165
  632.0 6.7 gather_fusion
  638.7 2.1 reshape.166
  640.8 3.8 multiply_reduce_fusion
  644.6 1.2 fusion.25
  646.8 21.3 %all-gather.11.cloned.1.call-done = bf16[256,2048]{1,0:T(8,128)(2,1)} async-done(((bf16[64,2048]{1,0:T(8,128)(2,1)}), bf16[256,2048]{1,0:T(8,128)(2,1)}) %all-gather.11.cloned.1.call-update) | async-done | bytes 1048592 | tf_op jit(solution)/shard_map/all_gather | solution.py:120
  668.1 2.4 convolution_convert_fusion.1
  (55 shorter events, 7.9 us)
Async XLA Ops:
  7.2 660.9 %copy-start = (bf16[2048,144]{0,1:T(8,128)(2,1)S(1)}, bf16[2048,144]{0,1:T(8,128)(2,1)}, u32[]{:S(2)}) copy-start(bf16[2048,144]{0,1:T(8,128)(2,1)} %param.21) | copy-start | bytes 1769476
  7.2 54.3 %all-gather.7.cloned.1.call-start = ((), (), s32[]{:S(2)}) async-start(), calls=%async_computation.6 | async-start | bytes 1310720 | tf_op jit(solution)/shard_map/all_gather | solution.py:86
  10.2 176.7 %all-gather.13.cloned.1.call-start = ((), (), s32[]{:S(2)}) async-start(), calls=%async_computation.11 | async-start | bytes 9469952 | tf_op jit(solution)/shard_map/all_gather | solution.py:84
  52.5 134.4 %all-to-all-start = ((bf16[64,12,2048]{2,1,0:T(8,128)(2,1)}), bf16[64,12,2048]{2,1,0:T(8,128)(2,1)}, u32[]{:S(2)}, u32[]{:S(2)}) async-start(bf16[64,12,2048]{2,1,0:T(8,128)(2,1)} %reshape.156), calls=%async_computation | async-start | bytes 8388608 | tf_op jit(solution)/shard_map/all_to_all | solution.py:74
  61.2 304.6 %all-gather.9.cloned.1.call-start = ((), (), s32[]{:S(2)}) async-start(), calls=%async_computation.7 | async-start | bytes 15728640 | tf_op jit(solution)/shard_map/all_gather | solution.py:91
  205.5 13.2 %copy-start.1 = (f32[16,32,1408]{2,1,0:T(8,128)S(1)}, f32[16,32,1408]{2,1,0:T(8,128)}, u32[]{:S(2)}) copy-start(f32[16,32,1408]{2,1,0:T(8,128)} %param.14) | copy-start | bytes 8650756
  205.5 65.5 %all-to-all-start.1 = ((bf16[64,32,2,352]{3,1,2,0:T(8,128)(2,1)}), bf16[64,32,2,352]{3,1,2,0:T(8,128)(2,1)}, u32[]{:S(2)}, u32[]{:S(2)}) async-start(bf16[64,32,2,352]{3,1,2,0:T(8,128)(2,1)} %bitcast.33), calls=%async_computation.1 | async-start | bytes 6291456 | tf_op jit(solution)/shard_map/all_to_all | solution.py:56
  271.1 110.0 %all-to-all-start.2 = ((bf16[64,32,352]{2,1,0:T(8,128)(2,1)}), bf16[64,32,352]{2,1,0:T(8,128)(2,1)S(1)}, u32[]{:S(2)}, u32[]{:S(2)}) async-start(bf16[64,32,352]{2,1,0:T(8,128)(2,1)} %bitcast.5), calls=%async_computation.2 | async-start | bytes 3145728 | tf_op jit(solution)/shard_map/all_to_all | solution.py:57
  280.0 232.7 %reduce-scatter.3.cloned.1.call-start = ((), (), s32[]{:S(2)}) async-start(), calls=%async_computation.8 | async-start | bytes 15728640 | tf_op jit(solution)/shard_map/reduce_scatter | solution.py:93
  518.8 11.2 %copy-start.6 = (bf16[256,2048]{1,0:T(8,128)(2,1)S(1)}, bf16[256,2048]{1,0:T(8,128)(2,1)}, u32[]{:S(2)}) copy-start(bf16[256,2048]{1,0:T(8,128)(2,1)} %all-gather.7.cloned.1.call-done) | copy-start | bytes 3145732
  518.8 107.0 %all-to-all-start.3 = ((bf16[64,12,2048]{2,1,0:T(8,128)(2,1)}), bf16[64,12,2048]{2,1,0:T(8,128)(2,1)}, u32[]{:S(2)}, u32[]{:S(2)}) async-start(bf16[64,12,2048]{2,1,0:T(8,128)(2,1)} %reshape.164), calls=%async_computation.4 | async-start | bytes 8388608 | tf_op jit(solution)/shard_map/all_to_all | solution.py:100
  529.7 114.9 %reduce-scatter.5.cloned.1.call-start = ((), (), s32[]{:S(2)}) async-start(), calls=%async_computation.9 | async-start | bytes 2621440 | tf_op jit(solution)/shard_map/reduce_scatter | solution.py:112
  533.2 8.8 %copy-start.4 = (s32[64,6]{0,1:T(8,128)S(1)}, s32[64,6]{0,1:T(8,128)}, u32[]{:S(2)}) copy-start(s32[64,6]{0,1:T(8,128)} %param.16) | copy-start | bytes 4612
  542.0 126.0 %all-gather.11.cloned.1.call-start = ((), (), s32[]{:S(2)}) async-start(), calls=%async_computation.10 | async-start | bytes 1310720 | tf_op jit(solution)/shard_map/all_gather | solution.py:120
  640.8 3.8 copy-start.2
  640.8 5.1 copy-start.5
  645.9 24.5 %copy-start.3 = (bf16[64,2048]{1,0:T(8,128)(2,1)}, bf16[64,2048]{1,0:T(8,128)(2,1)S(1)}, u32[]{:S(2)}) copy-start(bf16[64,2048]{1,0:T(8,128)(2,1)S(1)} %get-tuple-element.9) | copy-start | bytes 786436
Sparse Core Ops, SparseCore 0:
  10.4 29.3 all-gather.6
  41.6 118.3 all-gather.12
  193.2 172.5 all-gather.8
  394.7 118.0 reduce-scatter.2
  542.1 31.7 reduce-scatter.4
  646.9 21.1 all-gather.10

commit v3 on v2

--- a/solution.py
+++ b/solution.py
@@ -71,35 +71,48 @@
     send = (
         jnp.zeros((n_groups * capacity, width), jnp.bfloat16).at[target].set(normed[token_of_pair])
     )
-    received = lax.all_to_all(
-        send.reshape(n_groups, capacity, width),
-        ("dp", "expert"),
-        split_axis=0,
-        concat_axis=0,
-        tiled=True,
-    )
+    n_chunks = 2 if capacity % 2 == 0 else 1
+    chunk = capacity // n_chunks
+    send = send.reshape(n_groups, capacity, width)
+    received = [
+        lax.all_to_all(
+            send[:, c * chunk : (c + 1) * chunk],
+            ("dp", "expert"),
+            split_axis=0,
+            concat_axis=0,
+            tiled=True,
+        )
+        for c in range(n_chunks)
+    ]
     shared_cols = shared_gate.shape[1]
     shared_cat = jnp.concatenate([shared_gate, shared_up, shared_down], axis=1)
     shared_cat = lax.all_gather(shared_cat, "dp", axis=0, tiled=False)
     shared_cat = lax.all_gather(shared_cat, "expert", axis=1, tiled=False)
     shared_cat = shared_cat.reshape(width, 3 * shared_cols)
     group_rows = lax.all_gather(normed, "mp", axis=0, tiled=True)
-    received, shared_cat, group_rows = lax.optimization_barrier(
-        (received, shared_cat, group_rows)
+    received[0], shared_cat, group_rows = lax.optimization_barrier(
+        (received[0], shared_cat, group_rows)
     )
-    slots_here = received.reshape(n_groups * capacity, width)
-    every_slot = lax.all_gather(slots_here, "mp", axis=0, tiled=True)
-    rows = every_slot
-    summed = lax.psum_scatter(
-        expert_part(rows, gate_up_w, down_w).astype(jnp.bfloat16),
-        "mp",
-        scatter_dimension=0,
-        tiled=True,
-    )
-    result = summed.reshape(n_groups, capacity, width)
-    back = lax.all_to_all(
-        result, ("dp", "expert"), split_axis=0, concat_axis=0, tiled=True
-    ).reshape(n_groups * capacity, width)
+    back = []
+    for c in range(n_chunks):
+        slots_here = received[c].reshape(n_groups * chunk, width)
+        rows = lax.all_gather(slots_here, "mp", axis=0, tiled=True)
+        summed = lax.psum_scatter(
+            expert_part(rows, gate_up_w, down_w).astype(jnp.bfloat16),
+            "mp",
+            scatter_dimension=0,
+            tiled=True,
+        )
+        back.append(
+            lax.all_to_all(
+                summed.reshape(n_groups, chunk, width),
+                ("dp", "expert"),
+                split_axis=0,
+                concat_axis=0,
+                tiled=True,
+            )
+        )
+    back = jnp.concatenate(back, axis=1).reshape(n_groups * capacity, width)
     picked = back[target].reshape(tok_rows, top, width)
     routed = jnp.sum(picked.astype(jnp.float32) * gate_weights[:, :, None], axis=1)
     gate_w = shared_cat[:, :shared_cols]

time: 686 us -> 591 us (0.86)
  waiting for transfers between devices: 470 us -> 276 us
  blocking collectives: 21.2 us -> 98.4 us
  starting transfers between devices: 42.4 us -> 49.7 us
    all_to_all x2 -> x3, waiting for transfers between devices: 209 us -> 102 us  [the longest x1 51.2 us: on_device(): lax.all_to_all(send[:, c * chunk:(c + 1) * chunk], ('dp', 'expert'), spli...]
    all_to_all x0 -> x1, blocking collectives: none -> 77.1 us  [on_device(): lax.all_to_all(send[:, c * chunk:(c + 1) * chunk], ('dp', 'expert'), spli...]
    all_gather x1 -> x2, waiting for transfers between devices: 71.1 us -> 11.1 us  [on_device(): rows = lax.all_gather(slots_here, 'mp', axis=0, tiled=True)]
    reduce_scatter x1 -> x2, waiting for transfers between devices: 118 us -> 92.5 us  [on_device(): lax.psum_scatter(expert_part(rows, gate_up_w, down_w).astype(jnp.bfloat16...]
    all_to_all x2 -> x3, starting transfers between devices: 19.6 us -> 31.3 us  [the longest x2 21.3 us: on_device(): lax.all_to_all(summed.reshape(n_groups, chunk, width), ('dp', 'expert'),...]
    dot_general x1 -> x2, matrix products: 15.2 us -> 18.6 us  [expert_part(): gate_up = jnp.dot(rows, gate_up_w, preferred_element_type=jnp.float32)]
    reshape x4 -> x6, local copies, waits for them, and re-layouts: 24.5 us -> 22.5 us  [the longest x2 7.35 us: on_device(): summed.reshape(n_groups, chunk, width)]
  transfers between devices with their start and end apart: 10 -> 13, of which waited for: 6 -> 8; matrix products, arithmetic and copies ran while one was open for 14% -> 23% of each run, Pallas kernels for 0% -> 0%
where the time goes in v3:
time: 591 us; the launch traced here: 581 us
  waiting for transfers between devices  276 us (47%)
  blocking collectives  98.4 us (17%)
  local copies, waits for them, and re-layouts  74.4 us (13%)
  starting transfers between devices  49.7 us (8%)
  matrix products  47 us (8%)
  other arithmetic  20.3 us (3%)
  between operations  14.6 us (2%)
    reduce_scatter x2, waiting for transfers between devices, on_device(): lax.psum_scatter(expert_part(rows, gate_up_w, down_w).astype(jnp.bfloat16...  92.5 us
    all_to_all x1, blocking collectives, on_device(): lax.all_to_all(send[:, c * chunk:(c + 1) * chunk], ('dp', 'expert'), spli...  77.1 us
    all_to_all x1, waiting for transfers between devices, on_device(): lax.all_to_all(send[:, c * chunk:(c + 1) * chunk], ('dp', 'expert'), spli...  51.2 us
    all_to_all x2, waiting for transfers between devices, on_device(): lax.all_to_all(summed.reshape(n_groups, chunk, width), ('dp', 'expert'),...  50.8 us
    all_to_all x1, waiting for transfers between devices, on_device(): lax.all_to_all(in_send, ('expert', 'mp'), split_axis=0, concat_axis=1, ti...  45.1 us
    all_to_all x2, starting transfers between devices, on_device(): lax.all_to_all(summed.reshape(n_groups, chunk, width), ('dp', 'expert'),...  21.3 us
    all_gather x1, waiting for transfers between devices, on_device(): next_group = lax.all_gather(next_rows, 'mp', axis=0, tiled=True)  21.3 us
    all_gather x1, blocking collectives, on_device(): shared_cat = lax.all_gather(shared_cat, 'dp', axis=0, tiled=False)  21.2 us
  transfers between devices with their start and end apart: 13, of which 8 were waited for; matrix products, arithmetic and copies ran while one was open for 23% of the time, Pallas kernels for 0%

profile of v3, /device:TPU:8, one launch (start us, length us, event | category | flops | bytes accessed | tf_op | source)
XLA Modules:
  0.0 580.6 jit_solution(15546364585013328885)
XLA Ops:
  11.2 21.2 %all-gather = bf16[128,2112]{1,0:T(8,128)(2,1)} all-gather(bf16[32,2112]{1,0:T(8,128)(2,1)S(1)} %concatenate.9), channel_id=2, replica_groups=mesh['dp'=4,'expert'=16,'mp'=4] {'dp'}, dimensions={0}, use_global_device_ids=true | all-gather | bytes 675840 | tf_op jit(solution)/shard_map/all_gather | solution.py:89
  35.9 10.6 %scatter_custom_fusion = bf16[768,2048]{1,0:T(8,128)(2,1)} fusion(s32[384]{0:T(512)S(1)} %fusion.41, bf16[64,2048]{1,0:T(8,128)(2,1)} %fusion.33, s32[1024]{0:T(1024)S(1)} %pad_clamp_fusion.1, bf16[]{:T(256)} %constant.13.clone.1), kind=kCustom, calls=%fused_computation.18 | custom fusion | bytes 3146240 | tf_op jit(solution)/shard_map/scatter | solution.py:72
  46.5 6.1 %reshape.162 = bf16[64,12,2048]{2,1,0:T(8,128)(2,1)} reshape(bf16[768,2048]{1,0:T(8,128)(2,1)} %scatter_custom_fusion) | data formatting | bytes 6291456 | tf_op jit(solution)/shard_map/reshape | solution.py:76
  52.5 5.6 fusion.47
  58.1 77.1 %all_to_all.38 = bf16[64,6,2048]{2,1,0:T(8,128)(2,1)S(1)} all-to-all(bf16[64,6,2048]{2,1,0:T(8,128)(2,1)S(1)} %get-tuple-element.10), channel_id=1, replica_groups=mesh['dp'=4,'expert'=16,'mp'=4] {'dp','expert'}, dimensions={0} | all-to-all | bytes 3145728 | tf_op jit(solution)/shard_map/all_to_all | solution.py:78
  136.7 10.0 %all-to-all-start = ((bf16[64,6,2048]{2,1,0:T(8,128)(2,1)}), bf16[64,6,2048]{2,1,0:T(8,128)(2,1)S(1)}, u32[]{:S(2)}, u32[]{:S(2)}) async-start(bf16[64,6,2048]{2,1,0:T(8,128)(2,1)} %get-tuple-element.11), calls=%async_computation | async-start | bytes 4194304 | tf_op jit(solution)/shard_map/all_to_all | solution.py:78
  146.8 51.2 %all-to-all-done = bf16[64,6,2048]{2,1,0:T(8,128)(2,1)S(1)} async-done(((bf16[64,6,2048]{2,1,0:T(8,128)(2,1)}), bf16[64,6,2048]{2,1,0:T(8,128)(2,1)S(1)}, u32[]{:S(2)}, u32[]{:S(2)}) %all-to-all-start) | async-done | bytes 1572896 | tf_op jit(solution)/shard_map/all_to_all | solution.py:78
  202.5 5.0 reshape.165
  207.5 4.4 copy.24
  211.9 8.3 %all-to-all-start.1 = ((bf16[64,32,2,352]{3,1,2,0:T(8,128)(2,1)}), bf16[64,32,2,352]{3,1,2,0:T(8,128)(2,1)}, u32[]{:S(2)}, u32[]{:S(2)}) async-start(bf16[64,32,2,352]{3,1,2,0:T(8,128)(2,1)} %bitcast.36), calls=%async_computation.1 | async-start | bytes 6291456 | tf_op jit(solution)/shard_map/all_to_all | solution.py:56
  222.2 45.1 %all-to-all-done.1 = bf16[64,32,2,352]{3,1,2,0:T(8,128)(2,1)} async-done(((bf16[64,32,2,352]{3,1,2,0:T(8,128)(2,1)}), bf16[64,32,2,352]{3,1,2,0:T(8,128)(2,1)}, u32[]{:S(2)}, u32[]{:S(2)}) %all-to-all-start.1) | async-done | bytes 2883616 | tf_op jit(solution)/shard_map/all_to_all | solution.py:56
  267.3 9.4 %all-to-all-start.2 = ((bf16[64,32,352]{2,1,0:T(8,128)(2,1)}), bf16[64,32,352]{2,1,0:T(8,128)(2,1)S(1)}, u32[]{:S(2)}, u32[]{:S(2)}) async-start(bf16[64,32,352]{2,1,0:T(8,128)(2,1)} %bitcast.5), calls=%async_computation.2 | async-start | bytes 3145728 | tf_op jit(solution)/shard_map/all_to_all | solution.py:57
  276.8 6.9 %copy.25 = bf16[64,32,2,352]{3,2,1,0:T(2,128)(2,1)} copy(bf16[64,32,2,352]{3,1,2,0:T(8,128)(2,1)} %all-to-all-done.1) | data formatting | bytes 5767168 | tf_op jit(solution)/shard_map/all_to_all | solution.py:56
  283.6 7.6 %reshape.167 = bf16[2048,704]{1,0:T(8,128)(2,1)} reshape(bf16[64,32,2,352]{3,2,1,0:T(2,128)(2,1)} %copy.25) | data formatting | bytes 5767168 | tf_op jit(solution)/shard_map/reshape | solution.py:59
  291.2 10.6 %fusion.50 = f32[1536,704]{0,1:T(8,128)} fusion(bf16[1536,2048]{1,0:T(8,128)(2,1)} %all-gather.12.cloned.1.call-done, bf16[2048,704]{1,0:T(8,128)(2,1)} %reshape.167), kind=kOutput, calls=%fused_computation.75 | convolution fusion | flops 4429185024 | bytes 13500416 | tf_op jit(solution)/shard_map/dot_general | solution.py:15
  301.8 4.1 all-to-all-done.2
  305.9 7.7 %convolution_convert_fusion = bf16[1536,2048]{1,0:T(8,128)(2,1)} fusion(bf16[2048,352]{1,0:T(8,128)(2,1)S(1)} %bitcast.39, f32[1536,704]{0,1:T(8,128)} %fusion.50), kind=kOutput, calls=%fused_computation.3 | convolution fusion | flops 2220982272 | bytes 12058624 | tf_op jit(solution)/shard_map/dot_general | solution.py:17
  313.9 11.1 %all-gather.10.cloned.1.call-done = bf16[1536,2048]{1,0:T(8,128)(2,1)} async-done(((bf16[384,2048]{1,0:T(8,128)(2,1)}), bf16[1536,2048]{1,0:T(8,128)(2,1)}) %all-gather.10.cloned.1.call-update) | async-done | bytes 6291472 | tf_op jit(solution)/shard_map/all_gather | solution.py:99
  325.0 8.0 %fusion.49 = f32[1536,704]{0,1:T(8,128)S(1)} fusion(bf16[1536,2048]{1,0:T(8,128)(2,1)} %all-gather.10.cloned.1.call-done, bf16[2048,704]{1,0:T(8,128)(2,1)} %reshape.167), kind=kOutput, calls=%fused_computation.74 | convolution fusion | flops 4429185024 | bytes 13500416 | tf_op jit(solution)/shard_map/dot_general | solution.py:15
  333.1 5.5 convolution_convert_fusion.1
  338.6 50.9 %reduce-scatter.6.cloned.1.call-done = bf16[384,2048]{1,0:T(8,128)(2,1)} async-done(((bf16[1536,2048]{1,0:T(8,128)(2,1)}), bf16[384,2048]{1,0:T(8,128)(2,1)}) %reduce-scatter.6.cloned.1.call-update) | async-done | bytes 1572880 | tf_op jit(solution)/shard_map/reduce_scatter | solution.py:100
  393.2 10.6 %all-to-all-start.5 = ((bf16[64,6,2048]{2,1,0:T(8,128)(2,1)}), bf16[64,6,2048]{2,1,0:T(8,128)(2,1)S(1)}, u32[]{:S(2)}, u32[]{:S(2)}) async-start(bf16[64,6,2048]{2,1,0:T(8,128)(2,1)} %reshape.172), calls=%async_computation.7 | async-start | bytes 4194304 | tf_op jit(solution)/shard_map/all_to_all | solution.py:107
  403.8 3.8 fusion.4
  407.6 9.0 %fusion = f32[256,2048]{1,0:T(8,128)} fusion(bf16[2048,2112]{1,0:T(8,128)(2,1)} %bitcast.43, bf16[256,2048]{1,0:T(8,128)(2,1)} %all-gather.8.cloned.1.call-done, f32[256,704]{0,1:T(8,128)S(1)} %fusion.4), kind=kOutput, calls=%fused_computation.7 | convolution fusion | flops 1477476352 | bytes 10158080 | tf_op jit(solution)/shard_map/dot_general | solution.py:126
  416.6 41.6 %reduce-scatter.4.cloned.1.call-done = bf16[384,2048]{1,0:T(8,128)(2,1)} async-done(((bf16[1536,2048]{1,0:T(8,128)(2,1)}), bf16[384,2048]{1,0:T(8,128)(2,1)}) %reduce-scatter.4.cloned.1.call-update) | async-done | bytes 1572880 | tf_op jit(solution)/shard_map/reduce_scatter | solution.py:100
  461.9 10.7 %all-to-all-start.3 = ((bf16[64,6,2048]{2,1,0:T(8,128)(2,1)}), bf16[64,6,2048]{2,1,0:T(8,128)(2,1)}, u32[]{:S(2)}, u32[]{:S(2)}) async-start(bf16[64,6,2048]{2,1,0:T(8,128)(2,1)} %reshape.170), calls=%async_computation.4 | async-start | bytes 4194304 | tf_op jit(solution)/shard_map/all_to_all | solution.py:107
  473.1 50.8 %all-to-all-done.3 = bf16[64,6,2048]{2,1,0:T(8,128)(2,1)} async-done(((bf16[64,6,2048]{2,1,0:T(8,128)(2,1)}), bf16[64,6,2048]{2,1,0:T(8,128)(2,1)}, u32[]{:S(2)}, u32[]{:S(2)}) %all-to-all-start.3) | async-done | bytes 1572896 | tf_op jit(solution)/shard_map/all_to_all | solution.py:107
  523.9 5.1 pad_maximum_fusion
  528.9 6.2 %reshape.173 = bf16[768,2048]{1,0:T(8,128)(2,1)} reshape(bf16[64,12,2048]{2,1,0:T(8,128)(2,1)} %pad_maximum_fusion) | data formatting | bytes 6291456 | tf_op jit(solution)/shard_map/reshape | solution.py:115
  535.1 6.7 %gather_fusion = bf16[384,2048]{1,0:T(8,128)(2,1)S(1)} fusion(bf16[768,2048]{1,0:T(8,128)(2,1)} %reshape.173, s32[1024]{0:T(1024)S(1)} %pad_clamp_fusion), kind=kCustom, calls=%fused_computation.1 | custom fusion | bytes 3147264 | tf_op jit(solution)/shard_map/gather | solution.py:116
  543.9 3.8 multiply_reduce_fusion
  549.9 21.3 %all-gather.14.cloned.1.call-done = bf16[256,2048]{1,0:T(8,128)(2,1)} async-done(((bf16[64,2048]{1,0:T(8,128)(2,1)}), bf16[256,2048]{1,0:T(8,128)(2,1)}) %all-gather.14.cloned.1.call-update) | async-done | bytes 1048592 | tf_op jit(solution)/shard_map/all_gather | solution.py:133
  (68 shorter events, 30.1 us)
Async XLA Ops:
  7.2 564.0 %copy-start = (bf16[2048,144]{0,1:T(8,128)(2,1)S(1)}, bf16[2048,144]{0,1:T(8,128)(2,1)}, u32[]{:S(2)}) copy-start(bf16[2048,144]{0,1:T(8,128)(2,1)} %param.21) | copy-start | bytes 1769476
  7.2 139.6 %all-gather.8.cloned.1.call-start = ((), (), s32[]{:S(2)}) async-start(), calls=%async_computation.9 | async-start | bytes 1310720 | tf_op jit(solution)/shard_map/all_gather | solution.py:92
  10.2 187.8 %all-gather.16.cloned.1.call-start = ((), (), s32[]{:S(2)}) async-start(), calls=%async_computation.16 | async-start | bytes 9469952 | tf_op jit(solution)/shard_map/all_gather | solution.py:90
  32.5 258.8 %all-gather.12.cloned.1.call-start = ((), (), s32[]{:S(2)}) async-start(), calls=%async_computation.12 | async-start | bytes 7864320 | tf_op jit(solution)/shard_map/all_gather | solution.py:99
  136.7 61.3 %all-to-all-start = ((bf16[64,6,2048]{2,1,0:T(8,128)(2,1)}), bf16[64,6,2048]{2,1,0:T(8,128)(2,1)S(1)}, u32[]{:S(2)}, u32[]{:S(2)}) async-start(bf16[64,6,2048]{2,1,0:T(8,128)(2,1)} %get-tuple-element.11), calls=%async_computation | async-start | bytes 4194304 | tf_op jit(solution)/shard_map/all_to_all | solution.py:78
  146.7 178.3 %all-gather.10.cloned.1.call-start = ((), (), s32[]{:S(2)}) async-start(), calls=%async_computation.10 | async-start | bytes 7864320 | tf_op jit(solution)/shard_map/all_gather | solution.py:99
  211.9 8.3 %copy-start.1 = (f32[16,32,1408]{2,1,0:T(8,128)S(1)}, f32[16,32,1408]{2,1,0:T(8,128)}, u32[]{:S(2)}) copy-start(f32[16,32,1408]{2,1,0:T(8,128)} %param.14) | copy-start | bytes 8650756
  211.9 55.5 %all-to-all-start.1 = ((bf16[64,32,2,352]{3,1,2,0:T(8,128)(2,1)}), bf16[64,32,2,352]{3,1,2,0:T(8,128)(2,1)}, u32[]{:S(2)}, u32[]{:S(2)}) async-start(bf16[64,32,2,352]{3,1,2,0:T(8,128)(2,1)} %bitcast.36), calls=%async_computation.1 | async-start | bytes 6291456 | tf_op jit(solution)/shard_map/all_to_all | solution.py:56
  267.3 38.6 %all-to-all-start.2 = ((bf16[64,32,352]{2,1,0:T(8,128)(2,1)}), bf16[64,32,352]{2,1,0:T(8,128)(2,1)S(1)}, u32[]{:S(2)}, u32[]{:S(2)}) async-start(bf16[64,32,352]{2,1,0:T(8,128)(2,1)} %bitcast.5), calls=%async_computation.2 | async-start | bytes 3145728 | tf_op jit(solution)/shard_map/all_to_all | solution.py:57
  276.7 112.8 %reduce-scatter.6.cloned.1.call-start = ((), (), s32[]{:S(2)}) async-start(), calls=%async_computation.13 | async-start | bytes 7864320 | tf_op jit(solution)/shard_map/reduce_scatter | solution.py:100
  313.7 144.6 %reduce-scatter.4.cloned.1.call-start = ((), (), s32[]{:S(2)}) async-start(), calls=%async_computation.11 | async-start | bytes 7864320 | tf_op jit(solution)/shard_map/reduce_scatter | solution.py:100
  393.2 68.7 %all-to-all-start.5 = ((bf16[64,6,2048]{2,1,0:T(8,128)(2,1)}), bf16[64,6,2048]{2,1,0:T(8,128)(2,1)S(1)}, u32[]{:S(2)}, u32[]{:S(2)}) async-start(bf16[64,6,2048]{2,1,0:T(8,128)(2,1)} %reshape.172), calls=%async_computation.7 | async-start | bytes 4194304 | tf_op jit(solution)/shard_map/all_to_all | solution.py:107
  403.8 144.0 %reduce-scatter.8.cloned.1.call-start = ((), (), s32[]{:S(2)}) async-start(), calls=%async_computation.14 | async-start | bytes 2621440 | tf_op jit(solution)/shard_map/reduce_scatter | solution.py:125
  416.6 56.3 %copy-start.4 = (s32[64,6]{0,1:T(8,128)S(1)}, s32[64,6]{0,1:T(8,128)}, u32[]{:S(2)}) copy-start(s32[64,6]{0,1:T(8,128)} %param.16) | copy-start | bytes 4612
  461.9 61.9 %all-to-all-start.3 = ((bf16[64,6,2048]{2,1,0:T(8,128)(2,1)}), bf16[64,6,2048]{2,1,0:T(8,128)(2,1)}, u32[]{:S(2)}, u32[]{:S(2)}) async-start(bf16[64,6,2048]{2,1,0:T(8,128)(2,1)} %reshape.170), calls=%async_computation.4 | async-start | bytes 4194304 | tf_op jit(solution)/shard_map/all_to_all | solution.py:107
  472.7 98.5 %all-gather.14.cloned.1.call-start = ((), (), s32[]{:S(2)}) async-start(), calls=%async_computation.15 | async-start | bytes 1310720 | tf_op jit(solution)/shard_map/all_gather | solution.py:133
  543.9 3.8 copy-start.2
  543.9 5.1 copy-start.5
  549.0 24.6 %copy-start.3 = (bf16[64,2048]{1,0:T(8,128)(2,1)}, bf16[64,2048]{1,0:T(8,128)(2,1)S(1)}, u32[]{:S(2)}) copy-start(bf16[64,2048]{1,0:T(8,128)(2,1)S(1)} %get-tuple-element.9) | copy-start | bytes 786436
Sparse Core Ops, SparseCore 0:
  10.4 29.3 all-gather.7
  41.6 99.7 all-gather.15
  143.2 71.0 all-gather.11
  215.9 109.0 all-gather.9
  327.4 62.0 reduce-scatter.5
  392.0 66.2 reduce-scatter.3
  460.8 31.9 reduce-scatter.7
  550.0 21.1 all-gather.13

commit v4 on v3

--- a/solution.py
+++ b/solution.py
@@ -68,9 +68,12 @@
     slot_of_pair = jnp.sum(before * onehot, axis=1)
     target = flat_ids * capacity + slot_of_pair
     token_of_pair = jnp.arange(pairs, dtype=jnp.int32) // top
-    send = (
-        jnp.zeros((n_groups * capacity, width), jnp.bfloat16).at[target].set(normed[token_of_pair])
-    )
+    slot_ids = jnp.arange(n_groups * capacity, dtype=jnp.int32)
+    token_slot = target.reshape(tok_rows, top)[:, :, None] == slot_ids[None, None, :]
+    slot_token = jnp.any(token_slot, axis=1).astype(jnp.bfloat16)
+    send = lax.dot_general(
+        slot_token, normed, (((0,), (0,)), ((), ())), preferred_element_type=jnp.float32
+    ).astype(jnp.bfloat16)
     n_chunks = 2 if capacity % 2 == 0 else 1
     chunk = capacity // n_chunks
     send = send.reshape(n_groups, capacity, width)
@@ -113,8 +116,13 @@
             )
         )
     back = jnp.concatenate(back, axis=1).reshape(n_groups * capacity, width)
-    picked = back[target].reshape(tok_rows, top, width)
-    routed = jnp.sum(picked.astype(jnp.float32) * gate_weights[:, :, None], axis=1)
+    slot_weight = jnp.sum(jnp.where(token_slot, gate_weights[:, :, None], 0.0), axis=1)
+    routed = jnp.dot(
+        slot_weight,
+        back.astype(jnp.float32),
+        precision=lax.Precision.HIGHEST,
+        preferred_element_type=jnp.float32,
+    )
     gate_w = shared_cat[:, :shared_cols]
     up_w = shared_cat[:, shared_cols : 2 * shared_cols]
     down_s = shared_cat[:, 2 * shared_cols :]

time: 591 us -> 589 us (level)
  local copies, waits for them, and re-layouts: 74.4 us -> 55 us
  waiting for transfers between devices: 276 us -> 293 us
  matrix products: 47 us -> 54.7 us
    all_gather x2, waiting for transfers between devices: 11.1 us -> 35.8 us  [on_device(): rows = lax.all_gather(slots_here, 'mp', axis=0, tiled=True)]
    scatter x1 -> x0, local copies, waits for them, and re-layouts: 10.6 us -> none  [on_device(): jnp.zeros((n_groups * capacity, width), jnp.bfloat16).at[target]]
    all_to_all x1, waiting for transfers between devices: 45.1 us -> 36.6 us  [on_device(): lax.all_to_all(in_send, ('expert', 'mp'), split_axis=0, concat_axis=1, ti...]
    dot_general x0 -> x2, matrix products: none -> 7.5 us  [the longest x1 3.87 us: on_device(): jnp.dot(slot_weight, back.astype(jnp.float32), precision=lax.Precision.HI...]
    gather x1 -> x0, local copies, waits for them, and re-layouts: 6.69 us -> none  [on_device(): picked = back[target].reshape(tok_rows, top, width)]
  transfers between devices with their start and end apart: 13 -> 13, of which waited for: 8 -> 8; matrix products, arithmetic and copies ran while one was open for 23% -> 20% of each run, Pallas kernels for 0% -> 0%
where the time goes in v4:
time: 589 us; the launch traced here: 580 us
  waiting for transfers between devices  293 us (50%)
  blocking collectives  98.7 us (17%)
  local copies, waits for them, and re-layouts  55 us (9%)
  matrix products  54.7 us (9%)
  starting transfers between devices  49 us (8%)
  other arithmetic  15 us (3%)
  between operations  14.8 us (3%)
    reduce_scatter x2, waiting for transfers between devices, on_device(): lax.psum_scatter(expert_part(rows, gate_up_w, down_w).astype(jnp.bfloat16...  95.4 us
    all_to_all x1, blocking collectives, on_device(): lax.all_to_all(send[:, c * chunk:(c + 1) * chunk], ('dp', 'expert'), spli...  77.5 us
    all_to_all x1, waiting for transfers between devices, on_device(): lax.all_to_all(send[:, c * chunk:(c + 1) * chunk], ('dp', 'expert'), spli...  51.2 us
    all_to_all x2, waiting for transfers between devices, on_device(): lax.all_to_all(summed.reshape(n_groups, chunk, width), ('dp', 'expert'),...  50.7 us
    all_to_all x1, waiting for transfers between devices, on_device(): lax.all_to_all(in_send, ('expert', 'mp'), split_axis=0, concat_axis=1, ti...  36.6 us
    all_gather x2, waiting for transfers between devices, on_device(): rows = lax.all_gather(slots_here, 'mp', axis=0, tiled=True)  35.8 us
    all_gather x1, waiting for transfers between devices, on_device(): next_group = lax.all_gather(next_rows, 'mp', axis=0, tiled=True)  21.3 us
    all_to_all x2, starting transfers between devices, on_device(): lax.all_to_all(summed.reshape(n_groups, chunk, width), ('dp', 'expert'),...  21.3 us
  transfers between devices with their start and end apart: 13, of which 8 were waited for; matrix products, arithmetic and copies ran while one was open for 20% of the time, Pallas kernels for 0%

profile of v4, /device:TPU:8, one launch (start us, length us, event | category | flops | bytes accessed | tf_op | source)
XLA Modules:
  0.0 580.3 jit_solution(5109590462637843734)
XLA Ops:
  11.2 21.2 %all-gather = bf16[128,2112]{1,0:T(8,128)(2,1)} all-gather(bf16[32,2112]{1,0:T(8,128)(2,1)S(1)} %concatenate.9), channel_id=2, replica_groups=mesh['dp'=4,'expert'=16,'mp'=4] {'dp'}, dimensions={0}, use_global_device_ids=true | all-gather | bytes 675840 | tf_op jit(solution)/shard_map/all_gather | solution.py:92
  35.4 3.6 convolution_convert_fusion.2
  39.0 6.1 %reshape.94 = bf16[64,12,2048]{2,1,0:T(8,128)(2,1)} reshape(bf16[768,2048]{1,0:T(8,128)(2,1)} %convolution_convert_fusion.2) | data formatting | bytes 6291456 | tf_op jit(solution)/shard_map/reshape | solution.py:79
  45.1 5.2 fusion.42
  50.3 77.5 %all_to_all.38 = bf16[64,6,2048]{2,1,0:T(8,128)(2,1)S(1)} all-to-all(bf16[64,6,2048]{2,1,0:T(8,128)(2,1)S(1)} %get-tuple-element.8), channel_id=1, replica_groups=mesh['dp'=4,'expert'=16,'mp'=4] {'dp','expert'}, dimensions={0} | all-to-all | bytes 3145728 | tf_op jit(solution)/shard_map/all_to_all | solution.py:81
  129.3 10.0 %all-to-all-start = ((bf16[64,6,2048]{2,1,0:T(8,128)(2,1)}), bf16[64,6,2048]{2,1,0:T(8,128)(2,1)S(1)}, u32[]{:S(2)}, u32[]{:S(2)}) async-start(bf16[64,6,2048]{2,1,0:T(8,128)(2,1)} %get-tuple-element.9), calls=%async_computation | async-start | bytes 4194304 | tf_op jit(solution)/shard_map/all_to_all | solution.py:81
  139.3 51.2 %all-to-all-done = bf16[64,6,2048]{2,1,0:T(8,128)(2,1)S(1)} async-done(((bf16[64,6,2048]{2,1,0:T(8,128)(2,1)}), bf16[64,6,2048]{2,1,0:T(8,128)(2,1)S(1)}, u32[]{:S(2)}, u32[]{:S(2)}) %all-to-all-start) | async-done | bytes 1572896 | tf_op jit(solution)/shard_map/all_to_all | solution.py:81
  195.1 5.0 reshape.97
  200.1 4.4 copy.42
  204.5 9.0 %all-to-all-start.1 = ((bf16[64,32,2,352]{3,1,2,0:T(8,128)(2,1)}), bf16[64,32,2,352]{3,1,2,0:T(8,128)(2,1)}, u32[]{:S(2)}, u32[]{:S(2)}) async-start(bf16[64,32,2,352]{3,1,2,0:T(8,128)(2,1)} %bitcast.40), calls=%async_computation.1 | async-start | bytes 6291456 | tf_op jit(solution)/shard_map/all_to_all | solution.py:56
  215.5 36.6 %all-to-all-done.1 = bf16[64,32,2,352]{3,1,2,0:T(8,128)(2,1)} async-done(((bf16[64,32,2,352]{3,1,2,0:T(8,128)(2,1)}), bf16[64,32,2,352]{3,1,2,0:T(8,128)(2,1)}, u32[]{:S(2)}, u32[]{:S(2)}) %all-to-all-start.1) | async-done | bytes 2883616 | tf_op jit(solution)/shard_map/all_to_all | solution.py:56
  252.2 7.8 %all-to-all-start.2 = ((bf16[64,32,352]{2,1,0:T(8,128)(2,1)}), bf16[64,32,352]{2,1,0:T(8,128)(2,1)S(1)}, u32[]{:S(2)}, u32[]{:S(2)}) async-start(bf16[64,32,352]{2,1,0:T(8,128)(2,1)} %bitcast.5), calls=%async_computation.2 | async-start | bytes 3145728 | tf_op jit(solution)/shard_map/all_to_all | solution.py:57
  260.2 7.3 %copy.43 = bf16[64,32,2,352]{3,2,1,0:T(2,128)(2,1)} copy(bf16[64,32,2,352]{3,1,2,0:T(8,128)(2,1)} %all-to-all-done.1) | data formatting | bytes 5767168 | tf_op jit(solution)/shard_map/all_to_all | solution.py:56
  267.5 7.6 %reshape.99 = bf16[2048,704]{1,0:T(8,128)(2,1)} reshape(bf16[64,32,2,352]{3,2,1,0:T(2,128)(2,1)} %copy.43) | data formatting | bytes 5767168 | tf_op jit(solution)/shard_map/reshape | solution.py:59
  275.1 10.5 %fusion.45 = f32[1536,704]{0,1:T(8,128)} fusion(bf16[1536,2048]{1,0:T(8,128)(2,1)} %all-gather.12.cloned.1.call-done, bf16[2048,704]{1,0:T(8,128)(2,1)} %reshape.99), kind=kOutput, calls=%fused_computation.62 | convolution fusion | flops 4429185024 | bytes 13500416 | tf_op jit(solution)/shard_map/dot_general | solution.py:15
  287.4 7.7 %convolution_convert_fusion = bf16[1536,2048]{1,0:T(8,128)(2,1)} fusion(bf16[2048,352]{1,0:T(8,128)(2,1)S(1)} %bitcast.43, f32[1536,704]{0,1:T(8,128)} %fusion.45), kind=kOutput, calls=%fused_computation | convolution fusion | flops 2220982272 | bytes 12058624 | tf_op jit(solution)/shard_map/dot_general | solution.py:17
  295.5 35.8 %all-gather.10.cloned.1.call-done = bf16[1536,2048]{1,0:T(8,128)(2,1)} async-done(((bf16[384,2048]{1,0:T(8,128)(2,1)}), bf16[1536,2048]{1,0:T(8,128)(2,1)}) %all-gather.10.cloned.1.call-update) | async-done | bytes 6291472 | tf_op jit(solution)/shard_map/all_gather | solution.py:102
  331.3 8.0 %fusion.44 = f32[1536,704]{0,1:T(8,128)S(1)} fusion(bf16[1536,2048]{1,0:T(8,128)(2,1)} %all-gather.10.cloned.1.call-done, bf16[2048,704]{1,0:T(8,128)(2,1)} %reshape.99), kind=kOutput, calls=%fused_computation.61 | convolution fusion | flops 4429185024 | bytes 13500416 | tf_op jit(solution)/shard_map/dot_general | solution.py:15
  339.3 5.9 %convolution_convert_fusion.1 = bf16[1536,2048]{1,0:T(8,128)(2,1)} fusion(bf16[2048,352]{1,0:T(8,128)(2,1)S(1)} %bitcast.44, f32[1536,704]{0,1:T(8,128)S(1)} %fusion.44), kind=kOutput, calls=%fused_computation.1 | convolution fusion | flops 2220982272 | bytes 12058624 | tf_op jit(solution)/shard_map/dot_general | solution.py:17
  345.2 53.8 %reduce-scatter.6.cloned.1.call-done = bf16[384,2048]{1,0:T(8,128)(2,1)} async-done(((bf16[1536,2048]{1,0:T(8,128)(2,1)}), bf16[384,2048]{1,0:T(8,128)(2,1)}) %reduce-scatter.6.cloned.1.call-update) | async-done | bytes 1572880 | tf_op jit(solution)/shard_map/reduce_scatter | solution.py:103
  399.0 3.7 reshape.104
  402.6 10.5 %all-to-all-start.5 = ((bf16[64,6,2048]{2,1,0:T(8,128)(2,1)}), bf16[64,6,2048]{2,1,0:T(8,128)(2,1)S(1)}, u32[]{:S(2)}, u32[]{:S(2)}) async-start(bf16[64,6,2048]{2,1,0:T(8,128)(2,1)} %reshape.104), calls=%async_computation.7 | async-start | bytes 4194304 | tf_op jit(solution)/shard_map/all_to_all | solution.py:110
  413.2 3.8 fusion.4
  417.1 9.0 %fusion = f32[256,2048]{1,0:T(8,128)} fusion(bf16[2048,2112]{1,0:T(8,128)(2,1)} %bitcast.47, bf16[256,2048]{1,0:T(8,128)(2,1)} %all-gather.8.cloned.1.call-done, f32[256,704]{0,1:T(8,128)S(1)} %fusion.4), kind=kOutput, calls=%fused_computation.4 | convolution fusion | flops 1477476352 | bytes 10158080 | tf_op jit(solution)/shard_map/dot_general | solution.py:134
  426.1 41.6 %reduce-scatter.4.cloned.1.call-done = bf16[384,2048]{1,0:T(8,128)(2,1)} async-done(((bf16[1536,2048]{1,0:T(8,128)(2,1)}), bf16[384,2048]{1,0:T(8,128)(2,1)}) %reduce-scatter.4.cloned.1.call-update) | async-done | bytes 1572880 | tf_op jit(solution)/shard_map/reduce_scatter | solution.py:103
  467.7 3.7 reshape.102
  471.4 10.7 %all-to-all-start.3 = ((bf16[64,6,2048]{2,1,0:T(8,128)(2,1)}), bf16[64,6,2048]{2,1,0:T(8,128)(2,1)}, u32[]{:S(2)}, u32[]{:S(2)}) async-start(bf16[64,6,2048]{2,1,0:T(8,128)(2,1)} %reshape.102), calls=%async_computation.4 | async-start | bytes 4194304 | tf_op jit(solution)/shard_map/all_to_all | solution.py:110
  482.6 50.6 %all-to-all-done.3 = bf16[64,6,2048]{2,1,0:T(8,128)(2,1)} async-done(((bf16[64,6,2048]{2,1,0:T(8,128)(2,1)}), bf16[64,6,2048]{2,1,0:T(8,128)(2,1)}, u32[]{:S(2)}, u32[]{:S(2)}) %all-to-all-start.3) | async-done | bytes 1572896 | tf_op jit(solution)/shard_map/all_to_all | solution.py:110
  533.3 5.1 pad_maximum_fusion
  538.3 6.2 %reshape.105 = bf16[768,2048]{1,0:T(8,128)(2,1)} reshape(bf16[64,12,2048]{2,1,0:T(8,128)(2,1)} %pad_maximum_fusion) | data formatting | bytes 6291456 | tf_op jit(solution)/shard_map/reshape | solution.py:118
  544.5 3.9 fusion.28
  549.3 21.3 %all-gather.14.cloned.1.call-done = bf16[256,2048]{1,0:T(8,128)(2,1)} async-done(((bf16[64,2048]{1,0:T(8,128)(2,1)}), bf16[256,2048]{1,0:T(8,128)(2,1)}) %all-gather.14.cloned.1.call-update) | async-done | bytes 1048592 | tf_op jit(solution)/shard_map/all_gather | solution.py:141
  (64 shorter events, 21.1 us)
Async XLA Ops:
  7.2 563.5 %copy-start = (bf16[2048,144]{0,1:T(8,128)(2,1)S(1)}, bf16[2048,144]{0,1:T(8,128)(2,1)}, u32[]{:S(2)}) copy-start(bf16[2048,144]{0,1:T(8,128)(2,1)} %param.21) | copy-start | bytes 1769476
  7.2 27.9 %copy-start.4 = (s32[64,6]{0,1:T(8,128)S(1)}, s32[64,6]{0,1:T(8,128)}, u32[]{:S(2)}) copy-start(s32[64,6]{0,1:T(8,128)} %param.15) | copy-start | bytes 4612
  7.2 132.1 %all-gather.8.cloned.1.call-start = ((), (), s32[]{:S(2)}) async-start(), calls=%async_computation.9 | async-start | bytes 1310720 | tf_op jit(solution)/shard_map/all_gather | solution.py:95
  10.2 180.3 %all-gather.16.cloned.1.call-start = ((), (), s32[]{:S(2)}) async-start(), calls=%async_computation.16 | async-start | bytes 9469952 | tf_op jit(solution)/shard_map/all_gather | solution.py:93
  32.5 242.6 %all-gather.12.cloned.1.call-start = ((), (), s32[]{:S(2)}) async-start(), calls=%async_computation.12 | async-start | bytes 7864320 | tf_op jit(solution)/shard_map/all_gather | solution.py:102
  129.3 61.3 %all-to-all-start = ((bf16[64,6,2048]{2,1,0:T(8,128)(2,1)}), bf16[64,6,2048]{2,1,0:T(8,128)(2,1)S(1)}, u32[]{:S(2)}, u32[]{:S(2)}) async-start(bf16[64,6,2048]{2,1,0:T(8,128)(2,1)} %get-tuple-element.9), calls=%async_computation | async-start | bytes 4194304 | tf_op jit(solution)/shard_map/all_to_all | solution.py:81
  139.2 192.0 %all-gather.10.cloned.1.call-start = ((), (), s32[]{:S(2)}) async-start(), calls=%async_computation.10 | async-start | bytes 7864320 | tf_op jit(solution)/shard_map/all_gather | solution.py:102
  204.5 9.0 %copy-start.1 = (f32[16,32,1408]{2,1,0:T(8,128)S(1)}, f32[16,32,1408]{2,1,0:T(8,128)}, u32[]{:S(2)}) copy-start(f32[16,32,1408]{2,1,0:T(8,128)} %param.14) | copy-start | bytes 8650756
  204.5 47.7 %all-to-all-start.1 = ((bf16[64,32,2,352]{3,1,2,0:T(8,128)(2,1)}), bf16[64,32,2,352]{3,1,2,0:T(8,128)(2,1)}, u32[]{:S(2)}, u32[]{:S(2)}) async-start(bf16[64,32,2,352]{3,1,2,0:T(8,128)(2,1)} %bitcast.40), calls=%async_computation.1 | async-start | bytes 6291456 | tf_op jit(solution)/shard_map/all_to_all | solution.py:56
  252.2 35.3 %all-to-all-start.2 = ((bf16[64,32,352]{2,1,0:T(8,128)(2,1)}), bf16[64,32,352]{2,1,0:T(8,128)(2,1)S(1)}, u32[]{:S(2)}, u32[]{:S(2)}) async-start(bf16[64,32,352]{2,1,0:T(8,128)(2,1)} %bitcast.5), calls=%async_computation.2 | async-start | bytes 3145728 | tf_op jit(solution)/shard_map/all_to_all | solution.py:57
  260.0 139.0 %reduce-scatter.6.cloned.1.call-start = ((), (), s32[]{:S(2)}) async-start(), calls=%async_computation.13 | async-start | bytes 7864320 | tf_op jit(solution)/shard_map/reduce_scatter | solution.py:103
  295.2 172.5 %reduce-scatter.4.cloned.1.call-start = ((), (), s32[]{:S(2)}) async-start(), calls=%async_computation.11 | async-start | bytes 7864320 | tf_op jit(solution)/shard_map/reduce_scatter | solution.py:103
  402.6 68.7 %all-to-all-start.5 = ((bf16[64,6,2048]{2,1,0:T(8,128)(2,1)}), bf16[64,6,2048]{2,1,0:T(8,128)(2,1)S(1)}, u32[]{:S(2)}, u32[]{:S(2)}) async-start(bf16[64,6,2048]{2,1,0:T(8,128)(2,1)} %reshape.104), calls=%async_computation.7 | async-start | bytes 4194304 | tf_op jit(solution)/shard_map/all_to_all | solution.py:110
  413.2 131.3 %reduce-scatter.8.cloned.1.call-start = ((), (), s32[]{:S(2)}) async-start(), calls=%async_computation.14 | async-start | bytes 2621440 | tf_op jit(solution)/shard_map/reduce_scatter | solution.py:133
  426.0 56.3 %copy-start.5 = (s32[64,6]{0,1:T(8,128)S(1)}, s32[64,6]{0,1:T(8,128)}, u32[]{:S(2)}) copy-start(s32[64,6]{0,1:T(8,128)} %param.16) | copy-start | bytes 4612
  471.4 61.9 %all-to-all-start.3 = ((bf16[64,6,2048]{2,1,0:T(8,128)(2,1)}), bf16[64,6,2048]{2,1,0:T(8,128)(2,1)}, u32[]{:S(2)}, u32[]{:S(2)}) async-start(bf16[64,6,2048]{2,1,0:T(8,128)(2,1)} %reshape.102), calls=%async_computation.4 | async-start | bytes 4194304 | tf_op jit(solution)/shard_map/all_to_all | solution.py:110
  482.1 88.5 %all-gather.14.cloned.1.call-start = ((), (), s32[]{:S(2)}) async-start(), calls=%async_computation.15 | async-start | bytes 1310720 | tf_op jit(solution)/shard_map/all_gather | solution.py:141
  538.3 6.2 %copy-start.2 = (bf16[64,2048]{1,0:T(8,128)(2,1)S(1)}, bf16[64,2048]{1,0:T(8,128)(2,1)}, u32[]{:S(2)}) copy-start(bf16[64,2048]{1,0:T(8,128)(2,1)} %param.11) | copy-start | bytes 786436
  544.5 3.9 copy-start.6
  548.4 24.6 %copy-start.3 = (bf16[64,2048]{1,0:T(8,128)(2,1)}, bf16[64,2048]{1,0:T(8,128)(2,1)S(1)}, u32[]{:S(2)}) copy-start(bf16[64,2048]{1,0:T(8,128)(2,1)S(1)} %get-tuple-element.15) | copy-start | bytes 786436
Sparse Core Ops, SparseCore 0:
  10.4 29.3 all-gather.7
  41.6 99.9 all-gather.15
  143.4 77.4 all-gather.11
  222.6 108.6 all-gather.9
  333.7 65.2 reduce-scatter.5
  401.4 66.2 reduce-scatter.3
  470.2 31.9 reduce-scatter.7
  549.4 21.1 all-gather.13

commit v5 on v4

--- a/solution.py
+++ b/solution.py
@@ -74,7 +74,7 @@
     send = lax.dot_general(
         slot_token, normed, (((0,), (0,)), ((), ())), preferred_element_type=jnp.float32
     ).astype(jnp.bfloat16)
-    n_chunks = 2 if capacity % 2 == 0 else 1
+    n_chunks = 3 if capacity % 3 == 0 else 1
     chunk = capacity // n_chunks
     send = send.reshape(n_groups, capacity, width)
     received = [

time: 589 us -> 598 us (1.015)
  waiting for transfers between devices: 293 us -> 275 us
  blocking collectives: 98.7 us -> 112 us
  starting transfers between devices: 49 us -> 58.3 us
    all_to_all x1, waiting for transfers between devices: 51.2 us -> 16.3 us  [on_device(): lax.all_to_all(send[:, c * chunk:(c + 1) * chunk], ('dp', 'expert'), spli...]
    all_gather x2 -> x3, waiting for transfers between devices: 35.8 us -> 63.3 us  [on_device(): rows = lax.all_gather(slots_here, 'mp', axis=0, tiled=True)]
    all_to_all x2 -> x3, waiting for transfers between devices: 50.7 us -> 28.4 us  [on_device(): lax.all_to_all(summed.reshape(n_groups, chunk, width), ('dp', 'expert'),...]
    all_to_all x1 -> x2, blocking collectives: 77.5 us -> 90.4 us  [on_device(): lax.all_to_all(send[:, c * chunk:(c + 1) * chunk], ('dp', 'expert'), spli...]
    all_to_all x2 -> x3, starting transfers between devices: 21.3 us -> 31.9 us  [on_device(): lax.all_to_all(summed.reshape(n_groups, chunk, width), ('dp', 'expert'),...]
    reduce_scatter x2 -> x3, waiting for transfers between devices: 95.4 us -> 106 us  [on_device(): lax.psum_scatter(expert_part(rows, gate_up_w, down_w).astype(jnp.bfloat16...]
    dot_general x2 -> x3, matrix products: 13.6 us -> 15.2 us  [expert_part(): lax.dot_general(act, down_w, (((1,), (1,)), ((), ())), preferred_element_...]
    dot_general x2 -> x3, matrix products: 18.5 us -> 19.8 us  [expert_part(): gate_up = jnp.dot(rows, gate_up_w, preferred_element_type=jnp.float32)]
  transfers between devices with their start and end apart: 13 -> 16, of which waited for: 8 -> 10; matrix products, arithmetic and copies ran while one was open for 20% -> 20% of each run, Pallas kernels for 0% -> 0%
where the time goes in v5:
time: 598 us; the launch traced here: 588 us
  waiting for transfers between devices  275 us (46%)
  blocking collectives  112 us (19%)
  starting transfers between devices  58.3 us (10%)
  matrix products  58.3 us (10%)
  local copies, waits for them, and re-layouts  55.7 us (9%)
  between operations  14.9 us (2%)
  other arithmetic  14.6 us (2%)
    reduce_scatter x3, waiting for transfers between devices, on_device(): lax.psum_scatter(expert_part(rows, gate_up_w, down_w).astype(jnp.bfloat16...  106 us
    all_to_all x2, blocking collectives, on_device(): lax.all_to_all(send[:, c * chunk:(c + 1) * chunk], ('dp', 'expert'), spli...  90.4 us
    all_gather x3, waiting for transfers between devices, on_device(): rows = lax.all_gather(slots_here, 'mp', axis=0, tiled=True)  63.3 us
    all_to_all x1, waiting for transfers between devices, on_device(): lax.all_to_all(in_send, ('expert', 'mp'), split_axis=0, concat_axis=1, ti...  36.3 us
    all_to_all x3, starting transfers between devices, on_device(): lax.all_to_all(summed.reshape(n_groups, chunk, width), ('dp', 'expert'),...  31.9 us
    all_to_all x3, waiting for transfers between devices, on_device(): lax.all_to_all(summed.reshape(n_groups, chunk, width), ('dp', 'expert'),...  28.4 us
    all_gather x1, waiting for transfers between devices, on_device(): next_group = lax.all_gather(next_rows, 'mp', axis=0, tiled=True)  21.7 us
    all_gather x1, blocking collectives, on_device(): shared_cat = lax.all_gather(shared_cat, 'dp', axis=0, tiled=False)  21.2 us
  transfers between devices with their start and end apart: 16, of which 10 were waited for; matrix products, arithmetic and copies ran while one was open for 20% of the time, Pallas kernels for 0%

profile of v5, /device:TPU:8, one launch (start us, length us, event | category | flops | bytes accessed | tf_op | source)
XLA Modules:
  0.0 588.5 jit_solution(11390816934777583834)
XLA Ops:
  11.2 21.2 %all-gather = bf16[128,2112]{1,0:T(8,128)(2,1)} all-gather(bf16[32,2112]{1,0:T(8,128)(2,1)S(1)} %concatenate.9), channel_id=2, replica_groups=mesh['dp'=4,'expert'=16,'mp'=4] {'dp'}, dimensions={0}, use_global_device_ids=true | all-gather | bytes 675840 | tf_op jit(solution)/shard_map/all_gather | solution.py:92
  39.0 6.1 %reshape.100 = bf16[64,12,2048]{2,1,0:T(8,128)(2,1)} reshape(bf16[768,2048]{1,0:T(8,128)(2,1)} %convolution_convert_fusion.3) | data formatting | bytes 6291456 | tf_op jit(solution)/shard_map/reshape | solution.py:79
  45.1 5.4 fusion.46
  50.5 44.8 %all_to_all.48 = bf16[64,4,2048]{2,1,0:T(4,128)(2,1)S(1)} all-to-all(bf16[64,4,2048]{2,1,0:T(4,128)(2,1)S(1)} %get-tuple-element.9), channel_id=1, replica_groups=mesh['dp'=4,'expert'=16,'mp'=4] {'dp','expert'}, dimensions={0} | all-to-all | bytes 2097152 | tf_op jit(solution)/shard_map/all_to_all | solution.py:81
  96.5 45.6 %all_to_all.49 = bf16[64,4,2048]{2,1,0:T(4,128)(2,1)S(1)} all-to-all(bf16[64,4,2048]{2,1,0:T(4,128)(2,1)S(1)} %get-tuple-element.8), channel_id=1, replica_groups=mesh['dp'=4,'expert'=16,'mp'=4] {'dp','expert'}, dimensions={0} | all-to-all | bytes 2097152 | tf_op jit(solution)/shard_map/all_to_all | solution.py:81
  143.2 9.4 %all-to-all-start = ((bf16[64,4,2048]{2,1,0:T(4,128)(2,1)}), bf16[64,4,2048]{2,1,0:T(4,128)(2,1)}, u32[]{:S(2)}, u32[]{:S(2)}) async-start(bf16[64,4,2048]{2,1,0:T(4,128)(2,1)} %get-tuple-element.10), calls=%async_computation | async-start | bytes 2097152 | tf_op jit(solution)/shard_map/all_to_all | solution.py:81
  155.7 5.0 reshape.103
  165.0 16.3 %all-to-all-done = bf16[64,4,2048]{2,1,0:T(4,128)(2,1)} async-done(((bf16[64,4,2048]{2,1,0:T(4,128)(2,1)}), bf16[64,4,2048]{2,1,0:T(4,128)(2,1)}, u32[]{:S(2)}, u32[]{:S(2)}) %all-to-all-start) | async-done | bytes 1048608 | tf_op jit(solution)/shard_map/all_to_all | solution.py:81
  181.4 8.0 %all-to-all-start.1 = ((bf16[64,32,2,352]{3,1,2,0:T(8,128)(2,1)}), bf16[64,32,2,352]{3,1,2,0:T(8,128)(2,1)}, u32[]{:S(2)}, u32[]{:S(2)}) async-start(bf16[64,32,2,352]{3,1,2,0:T(8,128)(2,1)} %bitcast.43), calls=%async_computation.1 | async-start | bytes 6291456 | tf_op jit(solution)/shard_map/all_to_all | solution.py:56
  194.0 36.3 %all-to-all-done.1 = bf16[64,32,2,352]{3,1,2,0:T(8,128)(2,1)} async-done(((bf16[64,32,2,352]{3,1,2,0:T(8,128)(2,1)}), bf16[64,32,2,352]{3,1,2,0:T(8,128)(2,1)}, u32[]{:S(2)}, u32[]{:S(2)}) %all-to-all-start.1) | async-done | bytes 2883616 | tf_op jit(solution)/shard_map/all_to_all | solution.py:56
  230.3 8.1 %all-to-all-start.2 = ((bf16[64,32,352]{2,1,0:T(8,128)(2,1)}), bf16[64,32,352]{2,1,0:T(8,128)(2,1)S(1)}, u32[]{:S(2)}, u32[]{:S(2)}) async-start(bf16[64,32,352]{2,1,0:T(8,128)(2,1)} %bitcast.5), calls=%async_computation.2 | async-start | bytes 3145728 | tf_op jit(solution)/shard_map/all_to_all | solution.py:57
  238.4 6.8 %copy.43 = bf16[64,32,2,352]{3,2,1,0:T(2,128)(2,1)} copy(bf16[64,32,2,352]{3,1,2,0:T(8,128)(2,1)} %all-to-all-done.1) | data formatting | bytes 5767168 | tf_op jit(solution)/shard_map/all_to_all | solution.py:56
  245.2 7.6 %reshape.105 = bf16[2048,704]{1,0:T(8,128)(2,1)} reshape(bf16[64,32,2,352]{3,2,1,0:T(2,128)(2,1)} %copy.43) | data formatting | bytes 5767168 | tf_op jit(solution)/shard_map/reshape | solution.py:59
  252.8 8.0 %fusion.50 = f32[1024,704]{0,1:T(8,128)} fusion(bf16[1024,2048]{1,0:T(8,128)(2,1)} %all-gather.15.cloned.1.call-done, bf16[2048,704]{1,0:T(8,128)(2,1)} %reshape.105), kind=kOutput, calls=%fused_computation.68 | convolution fusion | flops 2952790016 | bytes 9961472 | tf_op jit(solution)/shard_map/dot_general | solution.py:15
  263.9 6.2 %convolution_convert_fusion = bf16[1024,2048]{1,0:T(8,128)(2,1)} fusion(bf16[2048,352]{1,0:T(8,128)(2,1)S(1)} %bitcast.46, f32[1024,704]{0,1:T(8,128)} %fusion.50), kind=kOutput, calls=%fused_computation.1 | convolution fusion | flops 1480654848 | bytes 8519680 | tf_op jit(solution)/shard_map/dot_general | solution.py:17
  270.3 22.5 %all-gather.13.cloned.1.call-done = bf16[1024,2048]{1,0:T(8,128)(2,1)} async-done(((bf16[256,2048]{1,0:T(8,128)(2,1)}), bf16[1024,2048]{1,0:T(8,128)(2,1)}) %all-gather.13.cloned.1.call-update) | async-done | bytes 4194320 | tf_op jit(solution)/shard_map/all_gather | solution.py:102
  292.8 5.9 %fusion.49 = f32[1024,704]{0,1:T(8,128)S(1)} fusion(bf16[1024,2048]{1,0:T(8,128)(2,1)} %all-gather.13.cloned.1.call-done, bf16[2048,704]{1,0:T(8,128)(2,1)} %reshape.105), kind=kOutput, calls=%fused_computation.67 | convolution fusion | flops 2952790016 | bytes 9961472 | tf_op jit(solution)/shard_map/dot_general | solution.py:15
  298.8 4.5 convolution_convert_fusion.1
  303.4 40.8 %all-gather.11.cloned.1.call-done = bf16[1024,2048]{1,0:T(8,128)(2,1)} async-done(((bf16[256,2048]{1,0:T(8,128)(2,1)}), bf16[1024,2048]{1,0:T(8,128)(2,1)}) %all-gather.11.cloned.1.call-update) | async-done | bytes 4194320 | tf_op jit(solution)/shard_map/all_gather | solution.py:102
  344.1 5.9 %fusion.48 = f32[1024,704]{0,1:T(8,128)S(1)} fusion(bf16[1024,2048]{1,0:T(8,128)(2,1)} %all-gather.11.cloned.1.call-done, bf16[2048,704]{1,0:T(8,128)(2,1)} %reshape.105), kind=kOutput, calls=%fused_computation.66 | convolution fusion | flops 2952790016 | bytes 9961472 | tf_op jit(solution)/shard_map/dot_general | solution.py:15
  350.1 4.5 convolution_convert_fusion.2
  354.6 41.6 %reduce-scatter.9.cloned.1.call-done = bf16[256,2048]{1,0:T(8,128)(2,1)} async-done(((bf16[1024,2048]{1,0:T(8,128)(2,1)}), bf16[256,2048]{1,0:T(8,128)(2,1)}) %reduce-scatter.9.cloned.1.call-update) | async-done | bytes 1048592 | tf_op jit(solution)/shard_map/reduce_scatter | solution.py:103
  398.5 10.6 %all-to-all-start.7 = ((bf16[64,4,2048]{2,1,0:T(4,128)(2,1)}), bf16[64,4,2048]{2,1,0:T(4,128)(2,1)S(1)}, u32[]{:S(2)}, u32[]{:S(2)}) async-start(bf16[64,4,2048]{2,1,0:T(4,128)(2,1)} %reshape.112), calls=%async_computation.10 | async-start | bytes 2097152 | tf_op jit(solution)/shard_map/all_to_all | solution.py:110
  413.0 35.1 %reduce-scatter.7.cloned.1.call-done = bf16[256,2048]{1,0:T(8,128)(2,1)} async-done(((bf16[1024,2048]{1,0:T(8,128)(2,1)}), bf16[256,2048]{1,0:T(8,128)(2,1)}) %reduce-scatter.7.cloned.1.call-update) | async-done | bytes 1048592 | tf_op jit(solution)/shard_map/reduce_scatter | solution.py:103
  450.4 10.6 %all-to-all-start.5 = ((bf16[64,4,2048]{2,1,0:T(4,128)(2,1)}), bf16[64,4,2048]{2,1,0:T(4,128)(2,1)S(1)}, u32[]{:S(2)}, u32[]{:S(2)}) async-start(bf16[64,4,2048]{2,1,0:T(4,128)(2,1)} %reshape.110), calls=%async_computation.7 | async-start | bytes 2097152 | tf_op jit(solution)/shard_map/all_to_all | solution.py:110
  461.3 9.5 %fusion = f32[256,2048]{1,0:T(8,128)} fusion(bf16[2048,2112]{1,0:T(8,128)(2,1)} %bitcast.51, bf16[256,2048]{1,0:T(8,128)(2,1)} %all-gather.9.cloned.1.call-done, f32[256,704]{0,1:T(8,128)S(1)} %fusion.4), kind=kOutput, calls=%fused_computation.5 | convolution fusion | flops 1477476352 | bytes 10158080 | tf_op jit(solution)/shard_map/dot_general | solution.py:134
  470.8 29.0 %reduce-scatter.5.cloned.1.call-done = bf16[256,2048]{1,0:T(8,128)(2,1)} async-done(((bf16[1024,2048]{1,0:T(8,128)(2,1)}), bf16[256,2048]{1,0:T(8,128)(2,1)}) %reduce-scatter.5.cloned.1.call-update) | async-done | bytes 1048592 | tf_op jit(solution)/shard_map/reduce_scatter | solution.py:103
  502.0 10.7 %all-to-all-start.3 = ((bf16[64,4,2048]{2,1,0:T(4,128)(2,1)}), bf16[64,4,2048]{2,1,0:T(4,128)(2,1)}, u32[]{:S(2)}, u32[]{:S(2)}) async-start(bf16[64,4,2048]{2,1,0:T(4,128)(2,1)} %reshape.108), calls=%async_computation.4 | async-start | bytes 2097152 | tf_op jit(solution)/shard_map/all_to_all | solution.py:110
  513.1 28.4 %all-to-all-done.3 = bf16[64,4,2048]{2,1,0:T(4,128)(2,1)} async-done(((bf16[64,4,2048]{2,1,0:T(4,128)(2,1)}), bf16[64,4,2048]{2,1,0:T(4,128)(2,1)}, u32[]{:S(2)}, u32[]{:S(2)}) %all-to-all-start.3) | async-done | bytes 1048608 | tf_op jit(solution)/shard_map/all_to_all | solution.py:110
  541.5 4.6 pad_maximum_fusion
  546.1 6.2 %reshape.113 = bf16[768,2048]{1,0:T(8,128)(2,1)} reshape(bf16[64,12,2048]{2,1,0:T(8,128)(2,1)} %pad_maximum_fusion) | data formatting | bytes 6291456 | tf_op jit(solution)/shard_map/reshape | solution.py:118
  557.1 21.7 %all-gather.17.cloned.1.call-done = bf16[256,2048]{1,0:T(8,128)(2,1)} async-done(((bf16[64,2048]{1,0:T(8,128)(2,1)}), bf16[256,2048]{1,0:T(8,128)(2,1)}) %all-gather.17.cloned.1.call-update) | async-done | bytes 1048592 | tf_op jit(solution)/shard_map/all_gather | solution.py:141
  (79 shorter events, 46.5 us)
Async XLA Ops:
  7.2 571.6 %copy-start = (bf16[2048,144]{0,1:T(8,128)(2,1)S(1)}, bf16[2048,144]{0,1:T(8,128)(2,1)}, u32[]{:S(2)}) copy-start(bf16[2048,144]{0,1:T(8,128)(2,1)} %param.21) | copy-start | bytes 1769476
  7.2 27.9 %copy-start.4 = (s32[64,6]{0,1:T(8,128)S(1)}, s32[64,6]{0,1:T(8,128)}, u32[]{:S(2)}) copy-start(s32[64,6]{0,1:T(8,128)} %param.15) | copy-start | bytes 4612
  7.2 182.3 %all-gather.9.cloned.1.call-start = ((), (), s32[]{:S(2)}) async-start(), calls=%async_computation.12 | async-start | bytes 1310720 | tf_op jit(solution)/shard_map/all_gather | solution.py:95
  10.2 179.3 %all-gather.19.cloned.1.call-start = ((), (), s32[]{:S(2)}) async-start(), calls=%async_computation.21 | async-start | bytes 9469952 | tf_op jit(solution)/shard_map/all_gather | solution.py:93
  32.5 220.3 %all-gather.15.cloned.1.call-start = ((), (), s32[]{:S(2)}) async-start(), calls=%async_computation.17 | async-start | bytes 5242880 | tf_op jit(solution)/shard_map/all_gather | solution.py:102
  96.5 196.4 %all-gather.13.cloned.1.call-start = ((), (), s32[]{:S(2)}) async-start(), calls=%async_computation.15 | async-start | bytes 5242880 | tf_op jit(solution)/shard_map/all_gather | solution.py:102
  143.2 38.2 %all-to-all-start = ((bf16[64,4,2048]{2,1,0:T(4,128)(2,1)}), bf16[64,4,2048]{2,1,0:T(4,128)(2,1)}, u32[]{:S(2)}, u32[]{:S(2)}) async-start(bf16[64,4,2048]{2,1,0:T(4,128)(2,1)} %get-tuple-element.10), calls=%async_computation | async-start | bytes 2097152 | tf_op jit(solution)/shard_map/all_to_all | solution.py:81
  181.4 48.9 %all-to-all-start.1 = ((bf16[64,32,2,352]{3,1,2,0:T(8,128)(2,1)}), bf16[64,32,2,352]{3,1,2,0:T(8,128)(2,1)}, u32[]{:S(2)}, u32[]{:S(2)}) async-start(bf16[64,32,2,352]{3,1,2,0:T(8,128)(2,1)} %bitcast.43), calls=%async_computation.1 | async-start | bytes 6291456 | tf_op jit(solution)/shard_map/all_to_all | solution.py:56
  189.4 2.5 copy-start.1
  189.4 154.7 %all-gather.11.cloned.1.call-start = ((), (), s32[]{:S(2)}) async-start(), calls=%async_computation.13 | async-start | bytes 5242880 | tf_op jit(solution)/shard_map/all_gather | solution.py:102
  230.3 33.6 %all-to-all-start.2 = ((bf16[64,32,352]{2,1,0:T(8,128)(2,1)}), bf16[64,32,352]{2,1,0:T(8,128)(2,1)S(1)}, u32[]{:S(2)}, u32[]{:S(2)}) async-start(bf16[64,32,352]{2,1,0:T(8,128)(2,1)} %bitcast.5), calls=%async_computation.2 | async-start | bytes 3145728 | tf_op jit(solution)/shard_map/all_to_all | solution.py:57
  238.3 157.9 %reduce-scatter.9.cloned.1.call-start = ((), (), s32[]{:S(2)}) async-start(), calls=%async_computation.18 | async-start | bytes 5242880 | tf_op jit(solution)/shard_map/reduce_scatter | solution.py:103
  270.0 178.1 %reduce-scatter.7.cloned.1.call-start = ((), (), s32[]{:S(2)}) async-start(), calls=%async_computation.16 | async-start | bytes 5242880 | tf_op jit(solution)/shard_map/reduce_scatter | solution.py:103
  303.3 196.5 %reduce-scatter.5.cloned.1.call-start = ((), (), s32[]{:S(2)}) async-start(), calls=%async_computation.14 | async-start | bytes 5242880 | tf_op jit(solution)/shard_map/reduce_scatter | solution.py:103
  354.6 54.4 %copy-start.7 = (bf16[256,2048]{1,0:T(8,128)(2,1)S(1)}, bf16[256,2048]{1,0:T(8,128)(2,1)}, u32[]{:S(2)}) copy-start(bf16[256,2048]{1,0:T(8,128)(2,1)} %all-gather.9.cloned.1.call-done) | copy-start | bytes 3145732
  398.5 51.9 %all-to-all-start.7 = ((bf16[64,4,2048]{2,1,0:T(4,128)(2,1)}), bf16[64,4,2048]{2,1,0:T(4,128)(2,1)S(1)}, u32[]{:S(2)}, u32[]{:S(2)}) async-start(bf16[64,4,2048]{2,1,0:T(4,128)(2,1)} %reshape.112), calls=%async_computation.10 | async-start | bytes 2097152 | tf_op jit(solution)/shard_map/all_to_all | solution.py:110
  450.4 51.6 %all-to-all-start.5 = ((bf16[64,4,2048]{2,1,0:T(4,128)(2,1)}), bf16[64,4,2048]{2,1,0:T(4,128)(2,1)S(1)}, u32[]{:S(2)}, u32[]{:S(2)}) async-start(bf16[64,4,2048]{2,1,0:T(4,128)(2,1)} %reshape.110), calls=%async_computation.7 | async-start | bytes 2097152 | tf_op jit(solution)/shard_map/all_to_all | solution.py:110
  461.0 91.3 %reduce-scatter.11.cloned.1.call-start = ((), (), s32[]{:S(2)}) async-start(), calls=%async_computation.19 | async-start | bytes 2621440 | tf_op jit(solution)/shard_map/reduce_scatter | solution.py:133
  470.8 42.1 %copy-start.5 = (s32[64,6]{0,1:T(8,128)S(1)}, s32[64,6]{0,1:T(8,128)}, u32[]{:S(2)}) copy-start(s32[64,6]{0,1:T(8,128)} %param.16) | copy-start | bytes 4612
  502.0 39.5 %all-to-all-start.3 = ((bf16[64,4,2048]{2,1,0:T(4,128)(2,1)}), bf16[64,4,2048]{2,1,0:T(4,128)(2,1)}, u32[]{:S(2)}, u32[]{:S(2)}) async-start(bf16[64,4,2048]{2,1,0:T(4,128)(2,1)} %reshape.108), calls=%async_computation.4 | async-start | bytes 2097152 | tf_op jit(solution)/shard_map/all_to_all | solution.py:110
  512.8 66.0 %all-gather.17.cloned.1.call-start = ((), (), s32[]{:S(2)}) async-start(), calls=%async_computation.20 | async-start | bytes 1310720 | tf_op jit(solution)/shard_map/all_gather | solution.py:141
  546.1 6.2 %copy-start.2 = (bf16[64,2048]{1,0:T(8,128)(2,1)S(1)}, bf16[64,2048]{1,0:T(8,128)(2,1)}, u32[]{:S(2)}) copy-start(bf16[64,2048]{1,0:T(8,128)(2,1)} %param.11) | copy-start | bytes 786436
  552.3 3.9 copy-start.6
  556.2 25.0 %copy-start.3 = (bf16[64,2048]{1,0:T(8,128)(2,1)}, bf16[64,2048]{1,0:T(8,128)(2,1)S(1)}, u32[]{:S(2)}) copy-start(bf16[64,2048]{1,0:T(8,128)(2,1)S(1)} %get-tuple-element.16) | copy-start | bytes 786436
Sparse Core Ops, SparseCore 0:
  10.4 29.3 all-gather.8
  41.6 91.9 all-gather.18
  135.5 78.2 all-gather.14
  215.5 77.2 all-gather.12
  294.5 49.5 all-gather.10
  346.5 49.7 reduce-scatter.8
  399.0 49.0 reduce-scatter.6
  450.7 49.0 reduce-scatter.4
  502.5 31.9 reduce-scatter.10
  557.2 21.5 all-gather.16

commit v6 on v4

--- a/solution.py
+++ b/solution.py
@@ -93,8 +93,12 @@
     shared_cat = lax.all_gather(shared_cat, "expert", axis=1, tiled=False)
     shared_cat = shared_cat.reshape(width, 3 * shared_cols)
     group_rows = lax.all_gather(normed, "mp", axis=0, tiled=True)
-    received[0], shared_cat, group_rows = lax.optimization_barrier(
-        (received[0], shared_cat, group_rows)
+    kv_cols = kv_weight.shape[1]
+    kv_full = lax.all_to_all(
+        jnp.broadcast_to(kv_weight[None], (n_mp,) + kv_weight.shape), "mp", 0, 0, tiled=True
+    )
+    received[0], shared_cat, group_rows, kv_full = lax.optimization_barrier(
+        (received[0], shared_cat, group_rows, kv_full)
     )
     back = []
     for c in range(n_chunks):
@@ -138,9 +142,13 @@
     )
     layer_out = (hidden.astype(jnp.float32) + routed + shared_out).astype(jnp.bfloat16)
     next_rows = rms_scale(layer_out, next_gain)
-    next_group = lax.all_gather(next_rows, "mp", axis=0, tiled=True)
-    kv_latent = jnp.dot(next_group, kv_weight, preferred_element_type=jnp.float32).astype(
+    kv_full = kv_full.transpose(1, 0, 2).reshape(width, n_mp * kv_cols)
+    kv_local = jnp.dot(next_rows, kv_full, preferred_element_type=jnp.float32).astype(
         jnp.bfloat16
+    )
+    kv_send = kv_local.reshape(tok_rows, n_mp, kv_cols).transpose(1, 0, 2)
+    kv_latent = lax.all_to_all(kv_send, "mp", 0, 0, tiled=True).reshape(
+        n_mp * tok_rows, kv_cols
     )
     return (layer_out, kv_latent)
 

time: 589 us -> 580 us (0.985)
  waiting for transfers between devices: 293 us -> 250 us
  blocking collectives: 98.7 us -> 137 us
  local copies, waits for them, and re-layouts: 55 us -> 48.2 us
    all_to_all x0 -> x2, blocking collectives: none -> 38.2 us  [the longest x1 29.7 us: on_device(): lax.all_to_all(jnp.broadcast_to(kv_weight[None], (n_mp,) + kv_weight.shap...]
    all_gather x2, waiting for transfers between devices: 35.8 us -> 0.04 us  [on_device(): rows = lax.all_gather(slots_here, 'mp', axis=0, tiled=True)]
    all_gather x1 -> x0, waiting for transfers between devices: 21.3 us -> none  [on_device(): next_group = lax.all_gather(next_rows, 'mp', axis=0, tiled=True)]
    all_to_all x1, waiting for transfers between devices: 36.6 us -> 48.5 us  [on_device(): lax.all_to_all(in_send, ('expert', 'mp'), split_axis=0, concat_axis=1, ti...]
    all_to_all x1, waiting for transfers between devices: 1.86 us -> 7.99 us  [on_device(): lax.all_to_all(out_send, ('expert', 'mp'), split_axis=0, concat_axis=1, t...]
  transfers between devices with their start and end apart: 13 -> 12, of which waited for: 8 -> 6; matrix products, arithmetic and copies ran while one was open for 20% -> 19% of each run, Pallas kernels for 0% -> 0%
where the time goes in v6:
time: 580 us; the launch traced here: 571 us
  waiting for transfers between devices  250 us (43%)
  blocking collectives  137 us (24%)
  matrix products  51.8 us (9%)
  starting transfers between devices  50.7 us (9%)
  local copies, waits for them, and re-layouts  48.2 us (8%)
  other arithmetic  18.2 us (3%)
  between operations  14.9 us (3%)
    reduce_scatter x2, waiting for transfers between devices, on_device(): lax.psum_scatter(expert_part(rows, gate_up_w, down_w).astype(jnp.bfloat16...  92.2 us
    all_to_all x1, blocking collectives, on_device(): lax.all_to_all(send[:, c * chunk:(c + 1) * chunk], ('dp', 'expert'), spli...  77.5 us
    all_to_all x1, waiting for transfers between devices, on_device(): lax.all_to_all(send[:, c * chunk:(c + 1) * chunk], ('dp', 'expert'), spli...  51.2 us
    all_to_all x2, waiting for transfers between devices, on_device(): lax.all_to_all(summed.reshape(n_groups, chunk, width), ('dp', 'expert'),...  50.1 us
    all_to_all x1, waiting for transfers between devices, on_device(): lax.all_to_all(in_send, ('expert', 'mp'), split_axis=0, concat_axis=1, ti...  48.5 us
    all_to_all x1, blocking collectives, on_device(): lax.all_to_all(jnp.broadcast_to(kv_weight[None], (n_mp,) + kv_weight.shap...  29.7 us
    all_to_all x2, starting transfers between devices, on_device(): lax.all_to_all(summed.reshape(n_groups, chunk, width), ('dp', 'expert'),...  21.8 us
    all_gather x1, blocking collectives, on_device(): shared_cat = lax.all_gather(shared_cat, 'dp', axis=0, tiled=False)  21.2 us
  transfers between devices with their start and end apart: 12, of which 6 were waited for; matrix products, arithmetic and copies ran while one was open for 19% of the time, Pallas kernels for 0%

profile of v6, /device:TPU:8, one launch (start us, length us, event | category | flops | bytes accessed | tf_op | source)
XLA Modules:
  0.0 570.9 jit_solution(1515567700657391225)
XLA Ops:
  11.2 21.2 %all-gather = bf16[128,2112]{1,0:T(8,128)(2,1)} all-gather(bf16[32,2112]{1,0:T(8,128)(2,1)S(1)} %concatenate.9), channel_id=2, replica_groups=mesh['dp'=4,'expert'=16,'mp'=4] {'dp'}, dimensions={0}, use_global_device_ids=true | all-gather | bytes 675840 | tf_op jit(solution)/shard_map/all_gather | solution.py:92
  37.3 2.8 reshape.104
  40.1 5.2 fusion.45
  45.3 77.5 %all_to_all.48 = bf16[64,6,2048]{2,1,0:T(8,128)(2,1)S(1)} all-to-all(bf16[64,6,2048]{2,1,0:T(8,128)(2,1)S(1)} %get-tuple-element.10), channel_id=1, replica_groups=mesh['dp'=4,'expert'=16,'mp'=4] {'dp','expert'}, dimensions={0} | all-to-all | bytes 3145728 | tf_op jit(solution)/shard_map/all_to_all | solution.py:81
  124.5 29.7 %all_to_all.49 = bf16[4,2048,144]{1,2,0:T(8,128)(2,1)} all-to-all(bf16[4,2048,144]{1,2,0:T(8,128)(2,1)S(1)} %broadcast_in_dim.12), channel_id=1, replica_groups=mesh['dp'=4,'expert'=16,'mp'=4] {'mp'}, dimensions={0} | all-to-all | bytes 4718592 | tf_op jit(solution)/shard_map/all_to_all | solution.py:97
  154.2 13.5 %all-to-all-start = ((bf16[64,6,2048]{2,1,0:T(8,128)(2,1)}), bf16[64,6,2048]{2,1,0:T(8,128)(2,1)S(1)}, u32[]{:S(2)}, u32[]{:S(2)}) async-start(bf16[64,6,2048]{2,1,0:T(8,128)(2,1)} %get-tuple-element.11), calls=%async_computation | async-start | bytes 4194304 | tf_op jit(solution)/shard_map/all_to_all | solution.py:81
  167.8 51.2 %all-to-all-done = bf16[64,6,2048]{2,1,0:T(8,128)(2,1)S(1)} async-done(((bf16[64,6,2048]{2,1,0:T(8,128)(2,1)}), bf16[64,6,2048]{2,1,0:T(8,128)(2,1)S(1)}, u32[]{:S(2)}, u32[]{:S(2)}) %all-to-all-start) | async-done | bytes 1572896 | tf_op jit(solution)/shard_map/all_to_all | solution.py:81
  220.5 4.6 convert_element_type.61
  225.1 6.8 %reshape.107 = bf16[16,32,2,4,352]{4,3,2,1,0:T(4,128)(2,1)S(1)} reshape(bf16[16,32,2816]{2,1,0:T(8,128)(2,1)} %convert_element_type.61) | data formatting | bytes 5767168 | tf_op jit(solution)/shard_map/reshape | solution.py:45
  234.3 5.9 %all-to-all-start.2 = ((bf16[64,32,2,352]{3,1,2,0:T(8,128)(2,1)}), bf16[64,32,2,352]{3,1,2,0:T(8,128)(2,1)S(1)}, u32[]{:S(2)}, u32[]{:S(2)}) async-start(bf16[64,32,2,352]{3,1,2,0:T(8,128)(2,1)} %bitcast.46), calls=%async_computation.2 | async-start | bytes 6291456 | tf_op jit(solution)/shard_map/all_to_all | solution.py:56
  244.1 48.5 %all-to-all-done.2 = bf16[64,32,2,352]{3,1,2,0:T(8,128)(2,1)S(1)} async-done(((bf16[64,32,2,352]{3,1,2,0:T(8,128)(2,1)}), bf16[64,32,2,352]{3,1,2,0:T(8,128)(2,1)S(1)}, u32[]{:S(2)}, u32[]{:S(2)}) %all-to-all-start.2) | async-done | bytes 2883616 | tf_op jit(solution)/shard_map/all_to_all | solution.py:56
  292.5 9.1 %all-to-all-start.3 = ((bf16[64,32,352]{2,1,0:T(8,128)(2,1)}), bf16[64,32,352]{2,1,0:T(8,128)(2,1)}, u32[]{:S(2)}, u32[]{:S(2)}) async-start(bf16[64,32,352]{2,1,0:T(8,128)(2,1)} %bitcast.49), calls=%async_computation.3 | async-start | bytes 3145728 | tf_op jit(solution)/shard_map/all_to_all | solution.py:57
  301.8 4.9 copy.59
  306.8 6.4 %reshape.109 = bf16[2048,704]{1,0:T(8,128)(2,1)S(1)} reshape(bf16[64,32,2,352]{3,2,1,0:T(2,128)(2,1)} %copy.59) | data formatting | bytes 5767168 | tf_op jit(solution)/shard_map/reshape | solution.py:59
  313.2 9.5 %fusion.48 = f32[1536,704]{0,1:T(8,128)} fusion(bf16[1536,2048]{1,0:T(8,128)(2,1)} %all-gather.11.cloned.1.call-done, bf16[2048,704]{1,0:T(8,128)(2,1)S(1)} %reshape.109), kind=kOutput, calls=%fused_computation.65 | convolution fusion | flops 4429185024 | bytes 13500416 | tf_op jit(solution)/shard_map/dot_general | solution.py:15
  322.8 8.0 %all-to-all-done.3 = bf16[64,32,352]{2,1,0:T(8,128)(2,1)} async-done(((bf16[64,32,352]{2,1,0:T(8,128)(2,1)}), bf16[64,32,352]{2,1,0:T(8,128)(2,1)}, u32[]{:S(2)}, u32[]{:S(2)}) %all-to-all-start.3) | async-done | bytes 1441824 | tf_op jit(solution)/shard_map/all_to_all | solution.py:57
  330.8 8.8 %convolution_convert_fusion = bf16[1536,2048]{1,0:T(8,128)(2,1)} fusion(bf16[2048,352]{1,0:T(8,128)(2,1)} %bitcast.6, f32[1536,704]{0,1:T(8,128)} %fusion.48), kind=kOutput, calls=%fused_computation | convolution fusion | flops 2220982272 | bytes 12058624 | tf_op jit(solution)/shard_map/dot_general | solution.py:17
  339.7 7.3 %fusion.47 = f32[1536,704]{0,1:T(8,128)S(1)} fusion(bf16[1536,2048]{1,0:T(8,128)(2,1)} %all-gather.9.cloned.1.call-done, bf16[2048,704]{1,0:T(8,128)(2,1)S(1)} %reshape.109), kind=kOutput, calls=%fused_computation.64 | convolution fusion | flops 4429185024 | bytes 13500416 | tf_op jit(solution)/shard_map/dot_general | solution.py:15
  347.0 7.0 %convolution_convert_fusion.1 = bf16[1536,2048]{1,0:T(8,128)(2,1)} fusion(bf16[2048,352]{1,0:T(8,128)(2,1)} %bitcast.6, f32[1536,704]{0,1:T(8,128)S(1)} %fusion.47), kind=kOutput, calls=%fused_computation.1 | convolution fusion | flops 2220982272 | bytes 12058624 | tf_op jit(solution)/shard_map/dot_general | solution.py:17
  354.0 51.0 %reduce-scatter.6.cloned.1.call-done = bf16[384,2048]{1,0:T(8,128)(2,1)} async-done(((bf16[1536,2048]{1,0:T(8,128)(2,1)}), bf16[384,2048]{1,0:T(8,128)(2,1)}) %reduce-scatter.6.cloned.1.call-update) | async-done | bytes 1572880 | tf_op jit(solution)/shard_map/reduce_scatter | solution.py:107
  405.0 3.7 reshape.114
  408.7 10.6 %all-to-all-start.6 = ((bf16[64,6,2048]{2,1,0:T(8,128)(2,1)}), bf16[64,6,2048]{2,1,0:T(8,128)(2,1)S(1)}, u32[]{:S(2)}, u32[]{:S(2)}) async-start(bf16[64,6,2048]{2,1,0:T(8,128)(2,1)} %reshape.114), calls=%async_computation.8 | async-start | bytes 4194304 | tf_op jit(solution)/shard_map/all_to_all | solution.py:114
  419.3 4.3 fusion.4
  423.6 8.9 %fusion = f32[256,2048]{1,0:T(8,128)} fusion(bf16[2048,2112]{1,0:T(8,128)(2,1)} %bitcast.55, bf16[256,2048]{1,0:T(8,128)(2,1)S(1)} %copy-done.7, f32[256,704]{0,1:T(8,128)} %fusion.4), kind=kOutput, calls=%fused_computation.4 | convolution fusion | flops 1477476352 | bytes 10158080 | tf_op jit(solution)/shard_map/dot_general | solution.py:138
  432.5 41.2 %reduce-scatter.4.cloned.1.call-done = bf16[384,2048]{1,0:T(8,128)(2,1)} async-done(((bf16[1536,2048]{1,0:T(8,128)(2,1)}), bf16[384,2048]{1,0:T(8,128)(2,1)}) %reduce-scatter.4.cloned.1.call-update) | async-done | bytes 1572880 | tf_op jit(solution)/shard_map/reduce_scatter | solution.py:107
  473.7 3.7 reshape.112
  477.4 11.2 %all-to-all-start.4 = ((bf16[64,6,2048]{2,1,0:T(8,128)(2,1)}), bf16[64,6,2048]{2,1,0:T(8,128)(2,1)}, u32[]{:S(2)}, u32[]{:S(2)}) async-start(bf16[64,6,2048]{2,1,0:T(8,128)(2,1)} %reshape.112), calls=%async_computation.5 | async-start | bytes 4194304 | tf_op jit(solution)/shard_map/all_to_all | solution.py:114
  489.5 50.1 %all-to-all-done.4 = bf16[64,6,2048]{2,1,0:T(8,128)(2,1)} async-done(((bf16[64,6,2048]{2,1,0:T(8,128)(2,1)}), bf16[64,6,2048]{2,1,0:T(8,128)(2,1)}, u32[]{:S(2)}, u32[]{:S(2)}) %all-to-all-start.4) | async-done | bytes 1572896 | tf_op jit(solution)/shard_map/all_to_all | solution.py:114
  539.6 5.1 pad_maximum_fusion
  544.6 4.8 reshape.115
  549.5 3.2 fusion.28
  554.4 8.5 %all_to_all.50 = bf16[4,64,144]{2,1,0:T(8,128)(2,1)S(1)} all-to-all(bf16[4,64,144]{2,1,0:T(8,128)(2,1)S(1)} %bitcast.51), channel_id=1, replica_groups=mesh['dp'=4,'expert'=16,'mp'=4] {'mp'}, dimensions={0} | all-to-all | bytes 147456 | tf_op jit(solution)/shard_map/all_to_all | solution.py:150
  (68 shorter events, 22.1 us)
Async XLA Ops:
  7.2 27.9 %copy-start.4 = (s32[64,6]{0,1:T(8,128)S(1)}, s32[64,6]{0,1:T(8,128)}, u32[]{:S(2)}) copy-start(s32[64,6]{0,1:T(8,128)} %param.15) | copy-start | bytes 4612
  7.2 160.7 %all-gather.7.cloned.1.call-start = ((), (), s32[]{:S(2)}) async-start(), calls=%async_computation.11 | async-start | bytes 1310720 | tf_op jit(solution)/shard_map/all_gather | solution.py:95
  10.2 208.9 %all-gather.13.cloned.1.call-start = ((), (), s32[]{:S(2)}) async-start(), calls=%async_computation.17 | async-start | bytes 9469952 | tf_op jit(solution)/shard_map/all_gather | solution.py:93
  32.4 280.8 %all-gather.11.cloned.1.call-start = ((), (), s32[]{:S(2)}) async-start(), calls=%async_computation.14 | async-start | bytes 7864320 | tf_op jit(solution)/shard_map/all_gather | solution.py:106
  122.8 1.5 copy-start.3
  154.2 64.8 %all-to-all-start = ((bf16[64,6,2048]{2,1,0:T(8,128)(2,1)}), bf16[64,6,2048]{2,1,0:T(8,128)(2,1)S(1)}, u32[]{:S(2)}, u32[]{:S(2)}) async-start(bf16[64,6,2048]{2,1,0:T(8,128)(2,1)} %get-tuple-element.11), calls=%async_computation | async-start | bytes 4194304 | tf_op jit(solution)/shard_map/all_to_all | solution.py:81
  167.8 171.9 %all-gather.9.cloned.1.call-start = ((), (), s32[]{:S(2)}) async-start(), calls=%async_computation.12 | async-start | bytes 7864320 | tf_op jit(solution)/shard_map/all_gather | solution.py:106
  234.3 58.3 %all-to-all-start.2 = ((bf16[64,32,2,352]{3,1,2,0:T(8,128)(2,1)}), bf16[64,32,2,352]{3,1,2,0:T(8,128)(2,1)S(1)}, u32[]{:S(2)}, u32[]{:S(2)}) async-start(bf16[64,32,2,352]{3,1,2,0:T(8,128)(2,1)} %bitcast.46), calls=%async_computation.2 | async-start | bytes 6291456 | tf_op jit(solution)/shard_map/all_to_all | solution.py:56
  292.5 38.2 %all-to-all-start.3 = ((bf16[64,32,352]{2,1,0:T(8,128)(2,1)}), bf16[64,32,352]{2,1,0:T(8,128)(2,1)}, u32[]{:S(2)}, u32[]{:S(2)}) async-start(bf16[64,32,352]{2,1,0:T(8,128)(2,1)} %bitcast.49), calls=%async_computation.3 | async-start | bytes 3145728 | tf_op jit(solution)/shard_map/all_to_all | solution.py:57
  301.6 103.4 %reduce-scatter.6.cloned.1.call-start = ((), (), s32[]{:S(2)}) async-start(), calls=%async_computation.15 | async-start | bytes 7864320 | tf_op jit(solution)/shard_map/reduce_scatter | solution.py:107
  339.6 134.1 %reduce-scatter.4.cloned.1.call-start = ((), (), s32[]{:S(2)}) async-start(), calls=%async_computation.13 | async-start | bytes 7864320 | tf_op jit(solution)/shard_map/reduce_scatter | solution.py:107
  354.0 65.3 %copy-start.7 = (bf16[256,2048]{1,0:T(8,128)(2,1)S(1)}, bf16[256,2048]{1,0:T(8,128)(2,1)}, u32[]{:S(2)}) copy-start(bf16[256,2048]{1,0:T(8,128)(2,1)} %all-gather.7.cloned.1.call-done) | copy-start | bytes 3145732
  408.7 68.7 %all-to-all-start.6 = ((bf16[64,6,2048]{2,1,0:T(8,128)(2,1)}), bf16[64,6,2048]{2,1,0:T(8,128)(2,1)S(1)}, u32[]{:S(2)}, u32[]{:S(2)}) async-start(bf16[64,6,2048]{2,1,0:T(8,128)(2,1)} %reshape.114), calls=%async_computation.8 | async-start | bytes 4194304 | tf_op jit(solution)/shard_map/all_to_all | solution.py:114
  419.3 130.2 %reduce-scatter.8.cloned.1.call-start = ((), (), s32[]{:S(2)}) async-start(), calls=%async_computation.16 | async-start | bytes 2621440 | tf_op jit(solution)/shard_map/reduce_scatter | solution.py:137
  432.5 56.0 %copy-start.5 = (s32[64,6]{0,1:T(8,128)S(1)}, s32[64,6]{0,1:T(8,128)}, u32[]{:S(2)}) copy-start(s32[64,6]{0,1:T(8,128)} %param.16) | copy-start | bytes 4612
  477.4 62.2 %all-to-all-start.4 = ((bf16[64,6,2048]{2,1,0:T(8,128)(2,1)}), bf16[64,6,2048]{2,1,0:T(8,128)(2,1)}, u32[]{:S(2)}, u32[]{:S(2)}) async-start(bf16[64,6,2048]{2,1,0:T(8,128)(2,1)} %reshape.112), calls=%async_computation.5 | async-start | bytes 4194304 | tf_op jit(solution)/shard_map/all_to_all | solution.py:114
  544.6 4.8 copy-start.1
  549.4 3.9 copy-start.6
  549.5 3.9 copy-start
  552.6 0.7 copy-start.2
Sparse Core Ops, SparseCore 0:
  10.4 29.3 all-gather.6
  41.6 99.8 all-gather.12
  143.4 70.8 all-gather.10
  220.6 114.7 all-gather.8
  339.8 65.2 reduce-scatter.5
  407.4 66.2 reduce-scatter.3
  476.2 31.9 reduce-scatter.7

commit v7 on v6

--- a/solution.py
+++ b/solution.py
@@ -56,8 +56,6 @@
         lax.all_to_all(in_send, ("expert", "mp"), split_axis=0, concat_axis=1, tiled=True),
         lax.all_to_all(out_send, ("expert", "mp"), split_axis=0, concat_axis=1, tiled=True),
     )
-    gate_up_w = in_recv.reshape(width, 2 * quarter)
-    down_w = out_recv.reshape(width, quarter)
     normed = rms_scale(hidden, norm_gain)
     levels = gate_levels.astype(jnp.float32)
     gate_weights = levels / jnp.sum(levels, axis=1, keepdims=True)
@@ -97,9 +95,11 @@
     kv_full = lax.all_to_all(
         jnp.broadcast_to(kv_weight[None], (n_mp,) + kv_weight.shape), "mp", 0, 0, tiled=True
     )
-    received[0], shared_cat, group_rows, kv_full = lax.optimization_barrier(
-        (received[0], shared_cat, group_rows, kv_full)
+    received[0], shared_cat, group_rows, kv_full, in_recv, out_recv = lax.optimization_barrier(
+        (received[0], shared_cat, group_rows, kv_full, in_recv, out_recv)
     )
+    gate_up_w = in_recv.reshape(width, 2 * quarter)
+    down_w = out_recv.reshape(width, quarter)
     back = []
     for c in range(n_chunks):
         slots_here = received[c].reshape(n_groups * chunk, width)

time: 580 us -> 602 us (1.038); the launches traced: 571 us -> 600 us
  waiting for transfers between devices: 250 us -> 330 us
  blocking collectives: 137 us -> 91.7 us
    all_to_all x1 -> x2, waiting for transfers between devices: 51.2 us -> 113 us  [on_device(): lax.all_to_all(send[:, c * chunk:(c + 1) * chunk], ('dp', 'expert'), spli...]
    all_gather x2, waiting for transfers between devices: 0.04 us -> 46.5 us  [on_device(): rows = lax.all_gather(slots_here, 'mp', axis=0, tiled=True)]
    all_to_all x2 -> x1, blocking collectives: 107 us -> 62 us  [on_device(): lax.all_to_all(in_send, ('expert', 'mp'), split_axis=0, concat_axis=1, ti...]
    all_to_all x1, waiting for transfers between devices: 48.5 us -> 14.1 us  [on_device(): lax.all_to_all(jnp.broadcast_to(kv_weight[None], (n_mp,) + kv_weight.shap...]
    reshape x1 -> x0, local copies, waits for them, and re-layouts: 6.44 us -> none  [on_device(): gate_up_w = in_recv.reshape(width, 2 * quarter)]
    all_to_all x1 -> x2, starting transfers between devices: 13.5 us -> 16 us  [on_device(): lax.all_to_all(send[:, c * chunk:(c + 1) * chunk], ('dp', 'expert'), spli...]
  transfers between devices with their start and end apart: 12 -> 13, of which waited for: 6 -> 8; matrix products, arithmetic and copies ran while one was open for 19% -> 17% of each run, Pallas kernels for 0% -> 0%
where the time goes in v7:
time: 602 us; the launch traced here: 600 us
  waiting for transfers between devices  330 us (55%)
  blocking collectives  91.7 us (15%)
  starting transfers between devices  54.4 us (9%)
  matrix products  48.2 us (8%)
  local copies, waits for them, and re-layouts  44.4 us (7%)
  other arithmetic  16.7 us (3%)
  between operations  14.4 us (2%)
    all_to_all x2, waiting for transfers between devices, on_device(): lax.all_to_all(send[:, c * chunk:(c + 1) * chunk], ('dp', 'expert'), spli...  113 us
    reduce_scatter x2, waiting for transfers between devices, on_device(): lax.psum_scatter(expert_part(rows, gate_up_w, down_w).astype(jnp.bfloat16...  96.8 us
    all_to_all x1, blocking collectives, on_device(): lax.all_to_all(in_send, ('expert', 'mp'), split_axis=0, concat_axis=1, ti...  62 us
    all_to_all x2, waiting for transfers between devices, on_device(): lax.all_to_all(summed.reshape(n_groups, chunk, width), ('dp', 'expert'),...  50.3 us
    all_gather x2, waiting for transfers between devices, on_device(): rows = lax.all_gather(slots_here, 'mp', axis=0, tiled=True)  46.5 us
    all_to_all x2, starting transfers between devices, on_device(): lax.all_to_all(summed.reshape(n_groups, chunk, width), ('dp', 'expert'),...  21.6 us
    all_gather x1, blocking collectives, on_device(): shared_cat = lax.all_gather(shared_cat, 'dp', axis=0, tiled=False)  21.2 us
    all_to_all x2, starting transfers between devices, on_device(): lax.all_to_all(send[:, c * chunk:(c + 1) * chunk], ('dp', 'expert'), spli...  16 us
  transfers between devices with their start and end apart: 13, of which 8 were waited for; matrix products, arithmetic and copies ran while one was open for 17% of the time, Pallas kernels for 0%

profile of v7, /device:TPU:8, one launch (start us, length us, event | category | flops | bytes accessed | tf_op | source)
XLA Modules:
  0.0 600.0 jit_solution(17300808137075616118)
XLA Ops:
  11.2 21.2 %all-gather = bf16[128,2112]{1,0:T(8,128)(2,1)} all-gather(bf16[32,2112]{1,0:T(8,128)(2,1)S(1)} %concatenate.9), channel_id=2, replica_groups=mesh['dp'=4,'expert'=16,'mp'=4] {'dp'}, dimensions={0}, use_global_device_ids=true | all-gather | bytes 675840 | tf_op jit(solution)/shard_map/all_gather | solution.py:90
  34.2 4.6 all-to-all-start.1
  44.8 5.9 fusion.47
  50.7 14.1 %all-to-all-done.1 = bf16[4,2048,144]{1,2,0:T(8,128)(2,1)} async-done(((bf16[4,2048,144]{1,2,0:T(8,128)(2,1)}), bf16[4,2048,144]{1,2,0:T(8,128)(2,1)}, u32[]{:S(2)}, u32[]{:S(2)}) %all-to-all-start.1) | async-done | bytes 2359328 | tf_op jit(solution)/shard_map/all_to_all | solution.py:95
  64.9 9.7 %all-to-all-start.5 = ((bf16[64,6,2048]{2,1,0:T(8,128)(2,1)}), bf16[64,6,2048]{2,1,0:T(8,128)(2,1)S(1)}, u32[]{:S(2)}, u32[]{:S(2)}) async-start(bf16[64,6,2048]{2,1,0:T(8,128)(2,1)} %get-tuple-element.14), calls=%async_computation.6 | async-start | bytes 4194304 | tf_op jit(solution)/shard_map/all_to_all | solution.py:79
  78.5 65.2 %all-to-all-done.5 = bf16[64,6,2048]{2,1,0:T(8,128)(2,1)S(1)} async-done(((bf16[64,6,2048]{2,1,0:T(8,128)(2,1)}), bf16[64,6,2048]{2,1,0:T(8,128)(2,1)S(1)}, u32[]{:S(2)}, u32[]{:S(2)}) %all-to-all-start.5) | async-done | bytes 1572896 | tf_op jit(solution)/shard_map/all_to_all | solution.py:79
  143.7 11.5 %all-to-all-start.3 = ((bf16[64,32,352]{2,1,0:T(8,128)(2,1)}), bf16[64,32,352]{2,1,0:T(8,128)(2,1)}, u32[]{:S(2)}, u32[]{:S(2)}) async-start(bf16[64,32,352]{2,1,0:T(8,128)(2,1)} %bitcast.54), calls=%async_computation.3 | async-start | bytes 3145728 | tf_op jit(solution)/shard_map/all_to_all | solution.py:57
  156.7 3.0 convert_element_type.61
  159.7 5.1 reshape.104
  167.6 9.2 %all-to-all-done.3 = bf16[64,32,352]{2,1,0:T(8,128)(2,1)} async-done(((bf16[64,32,352]{2,1,0:T(8,128)(2,1)}), bf16[64,32,352]{2,1,0:T(8,128)(2,1)}, u32[]{:S(2)}, u32[]{:S(2)}) %all-to-all-start.3) | async-done | bytes 1441824 | tf_op jit(solution)/shard_map/all_to_all | solution.py:57
  176.8 62.0 %all_to_all.54 = bf16[64,32,2,352]{3,1,2,0:T(8,128)(2,1)} all-to-all(bf16[64,32,2,352]{3,1,2,0:T(8,128)(2,1)S(1)} %bitcast.52), channel_id=1, replica_groups=mesh['dp'=4,'expert'=16,'mp'=4] {'expert','mp'}, dimensions={0} | all-to-all | bytes 5767168 | tf_op jit(solution)/shard_map/all_to_all | solution.py:56
  238.8 6.3 %all-to-all-start = ((bf16[64,6,2048]{2,1,0:T(8,128)(2,1)}), bf16[64,6,2048]{2,1,0:T(8,128)(2,1)}, u32[]{:S(2)}, u32[]{:S(2)}) async-start(bf16[64,6,2048]{2,1,0:T(8,128)(2,1)} %get-tuple-element.15), calls=%async_computation | async-start | bytes 4194304 | tf_op jit(solution)/shard_map/all_to_all | solution.py:79
  247.4 47.9 %all-to-all-done = bf16[64,6,2048]{2,1,0:T(8,128)(2,1)} async-done(((bf16[64,6,2048]{2,1,0:T(8,128)(2,1)}), bf16[64,6,2048]{2,1,0:T(8,128)(2,1)}, u32[]{:S(2)}, u32[]{:S(2)}) %all-to-all-start) | async-done | bytes 1572896 | tf_op jit(solution)/shard_map/all_to_all | solution.py:79
  295.3 3.7 reshape.107
  302.1 7.7 %fusion.50 = f32[1536,704]{0,1:T(8,128)S(1)} fusion(bf16[1536,2048]{1,0:T(8,128)(2,1)} %all-gather.11.cloned.1.call-done, bf16[2048,704]{0,1:T(8,128)(2,1)} %bitcast.55), kind=kOutput, calls=%fused_computation.67 | convolution fusion | flops 4429185024 | bytes 13500416 | tf_op jit(solution)/shard_map/dot_general | solution.py:15
  309.8 7.2 %convolution_convert_fusion = bf16[1536,2048]{1,0:T(8,128)(2,1)} fusion(bf16[1,2048,352]{2,1,0:T(8,128)(2,1)} %bitcast.7, f32[1536,704]{0,1:T(8,128)S(1)} %fusion.50), kind=kOutput, calls=%fused_computation | convolution fusion | flops 2220982272 | bytes 12058624 | tf_op jit(solution)/shard_map/dot_general | solution.py:17
  317.1 46.5 %all-gather.9.cloned.1.call-done = bf16[1536,2048]{1,0:T(8,128)(2,1)} async-done(((bf16[384,2048]{1,0:T(8,128)(2,1)}), bf16[1536,2048]{1,0:T(8,128)(2,1)}) %all-gather.9.cloned.1.call-update) | async-done | bytes 6291472 | tf_op jit(solution)/shard_map/all_gather | solution.py:106
  363.6 6.8 %fusion.49 = f32[1536,704]{0,1:T(8,128)S(1)} fusion(bf16[1536,2048]{1,0:T(8,128)(2,1)} %all-gather.9.cloned.1.call-done, bf16[2048,704]{0,1:T(8,128)(2,1)S(1)} %bitcast.56), kind=kOutput, calls=%fused_computation.66 | convolution fusion | flops 4429185024 | bytes 13500416 | tf_op jit(solution)/shard_map/dot_general | solution.py:15
  370.3 6.9 %convolution_convert_fusion.1 = bf16[1536,2048]{1,0:T(8,128)(2,1)} fusion(bf16[1,2048,352]{2,1,0:T(8,128)(2,1)} %bitcast.7, f32[1536,704]{0,1:T(8,128)S(1)} %fusion.49), kind=kOutput, calls=%fused_computation.1 | convolution fusion | flops 2220982272 | bytes 12058624 | tf_op jit(solution)/shard_map/dot_general | solution.py:17
  377.3 55.9 %reduce-scatter.6.cloned.1.call-done = bf16[384,2048]{1,0:T(8,128)(2,1)} async-done(((bf16[1536,2048]{1,0:T(8,128)(2,1)}), bf16[384,2048]{1,0:T(8,128)(2,1)}) %reduce-scatter.6.cloned.1.call-update) | async-done | bytes 1572880 | tf_op jit(solution)/shard_map/reduce_scatter | solution.py:107
  433.2 3.7 reshape.112
  436.8 10.7 %all-to-all-start.6 = ((bf16[64,6,2048]{2,1,0:T(8,128)(2,1)}), bf16[64,6,2048]{2,1,0:T(8,128)(2,1)S(1)}, u32[]{:S(2)}, u32[]{:S(2)}) async-start(bf16[64,6,2048]{2,1,0:T(8,128)(2,1)} %reshape.112), calls=%async_computation.8 | async-start | bytes 4194304 | tf_op jit(solution)/shard_map/all_to_all | solution.py:114
  447.8 4.2 fusion.4
  452.1 8.9 %fusion = f32[256,2048]{1,0:T(8,128)} fusion(bf16[2048,2112]{1,0:T(8,128)(2,1)} %bitcast.62, bf16[256,2048]{1,0:T(8,128)(2,1)S(1)} %copy-done.8, f32[256,704]{0,1:T(8,128)} %fusion.4), kind=kOutput, calls=%fused_computation.4 | convolution fusion | flops 1477476352 | bytes 10158080 | tf_op jit(solution)/shard_map/dot_general | solution.py:138
  461.0 40.9 %reduce-scatter.4.cloned.1.call-done = bf16[384,2048]{1,0:T(8,128)(2,1)} async-done(((bf16[1536,2048]{1,0:T(8,128)(2,1)}), bf16[384,2048]{1,0:T(8,128)(2,1)}) %reduce-scatter.4.cloned.1.call-update) | async-done | bytes 1572880 | tf_op jit(solution)/shard_map/reduce_scatter | solution.py:107
  501.9 3.7 reshape.110
  505.5 10.9 %all-to-all-start.4 = ((bf16[64,6,2048]{2,1,0:T(8,128)(2,1)}), bf16[64,6,2048]{2,1,0:T(8,128)(2,1)}, u32[]{:S(2)}, u32[]{:S(2)}) async-start(bf16[64,6,2048]{2,1,0:T(8,128)(2,1)} %reshape.110), calls=%async_computation.5 | async-start | bytes 4194304 | tf_op jit(solution)/shard_map/all_to_all | solution.py:114
  517.3 50.3 %all-to-all-done.4 = bf16[64,6,2048]{2,1,0:T(8,128)(2,1)} async-done(((bf16[64,6,2048]{2,1,0:T(8,128)(2,1)}), bf16[64,6,2048]{2,1,0:T(8,128)(2,1)}, u32[]{:S(2)}, u32[]{:S(2)}) %all-to-all-start.4) | async-done | bytes 1572896 | tf_op jit(solution)/shard_map/all_to_all | solution.py:114
  567.6 5.1 pad_maximum_fusion
  572.7 4.8 reshape.113
  577.5 3.0 fusion.30
  583.9 8.5 %all_to_all.55 = bf16[4,64,144]{2,1,0:T(8,128)(2,1)S(1)} all-to-all(bf16[4,64,144]{2,1,0:T(8,128)(2,1)S(1)} %bitcast.58), channel_id=1, replica_groups=mesh['dp'=4,'expert'=16,'mp'=4] {'mp'}, dimensions={0} | all-to-all | bytes 147456 | tf_op jit(solution)/shard_map/all_to_all | solution.py:150
  (71 shorter events, 30.6 us)
Async XLA Ops:
  7.2 25.3 %copy-start.4 = (bf16[2048,144]{0,1:T(8,128)(2,1)S(1)}, bf16[2048,144]{0,1:T(8,128)(2,1)}, u32[]{:S(2)}) copy-start(bf16[2048,144]{0,1:T(8,128)(2,1)} %param.21) | copy-start | bytes 1769476
  7.2 240.2 %all-gather.7.cloned.1.call-start = ((), (), s32[]{:S(2)}) async-start(), calls=%async_computation.11 | async-start | bytes 1310720 | tf_op jit(solution)/shard_map/all_gather | solution.py:93
  10.2 285.1 %all-gather.13.cloned.1.call-start = ((), (), s32[]{:S(2)}) async-start(), calls=%async_computation.17 | async-start | bytes 9469952 | tf_op jit(solution)/shard_map/all_gather | solution.py:91
  34.2 4.6 copy-start.5
  34.2 6.8 %copy-start.2 = (bf16[64,2048]{1,0:T(8,128)(2,1)S(1)}, bf16[64,2048]{1,0:T(8,128)(2,1)}, u32[]{:S(2)}) copy-start(bf16[64,2048]{1,0:T(8,128)(2,1)} %fusion.35) | copy-start | bytes 786436
  34.2 30.7 %all-to-all-start.1 = ((bf16[4,2048,144]{1,2,0:T(8,128)(2,1)}), bf16[4,2048,144]{1,2,0:T(8,128)(2,1)}, u32[]{:S(2)}, u32[]{:S(2)}) async-start(bf16[4,2048,144]{1,2,0:T(8,128)(2,1)} %broadcast_in_dim.12), calls=%async_computation.1 | async-start | bytes 4718592 | tf_op jit(solution)/shard_map/all_to_all | solution.py:95
  64.9 78.8 %all-to-all-start.5 = ((bf16[64,6,2048]{2,1,0:T(8,128)(2,1)}), bf16[64,6,2048]{2,1,0:T(8,128)(2,1)S(1)}, u32[]{:S(2)}, u32[]{:S(2)}) async-start(bf16[64,6,2048]{2,1,0:T(8,128)(2,1)} %get-tuple-element.14), calls=%async_computation.6 | async-start | bytes 4194304 | tf_op jit(solution)/shard_map/all_to_all | solution.py:79
  143.7 33.1 %all-to-all-start.3 = ((bf16[64,32,352]{2,1,0:T(8,128)(2,1)}), bf16[64,32,352]{2,1,0:T(8,128)(2,1)}, u32[]{:S(2)}, u32[]{:S(2)}) async-start(bf16[64,32,352]{2,1,0:T(8,128)(2,1)} %bitcast.54), calls=%async_computation.3 | async-start | bytes 3145728 | tf_op jit(solution)/shard_map/all_to_all | solution.py:57
  155.2 146.9 %all-gather.11.cloned.1.call-start = ((), (), s32[]{:S(2)}) async-start(), calls=%async_computation.14 | async-start | bytes 7864320 | tf_op jit(solution)/shard_map/all_gather | solution.py:106
  238.8 56.5 %all-to-all-start = ((bf16[64,6,2048]{2,1,0:T(8,128)(2,1)}), bf16[64,6,2048]{2,1,0:T(8,128)(2,1)}, u32[]{:S(2)}, u32[]{:S(2)}) async-start(bf16[64,6,2048]{2,1,0:T(8,128)(2,1)} %get-tuple-element.15), calls=%async_computation | async-start | bytes 4194304 | tf_op jit(solution)/shard_map/all_to_all | solution.py:79
  245.1 118.5 %all-gather.9.cloned.1.call-start = ((), (), s32[]{:S(2)}) async-start(), calls=%async_computation.12 | async-start | bytes 7864320 | tf_op jit(solution)/shard_map/all_gather | solution.py:106
  299.0 134.1 %reduce-scatter.6.cloned.1.call-start = ((), (), s32[]{:S(2)}) async-start(), calls=%async_computation.15 | async-start | bytes 7864320 | tf_op jit(solution)/shard_map/reduce_scatter | solution.py:107
  317.0 46.5 %copy-start = (bf16[1,2048,2,352]{1,3,2,0:T(8,128)(2,1)S(1)}, bf16[1,2048,2,352]{1,3,2,0:T(8,128)(2,1)}, u32[]{:S(2)}) copy-start(bf16[1,2048,2,352]{1,3,2,0:T(8,128)(2,1)} %copy.62) | copy-start | bytes 8650756
  317.0 184.8 %reduce-scatter.4.cloned.1.call-start = ((), (), s32[]{:S(2)}) async-start(), calls=%async_computation.13 | async-start | bytes 7864320 | tf_op jit(solution)/shard_map/reduce_scatter | solution.py:107
  436.8 11.0 %copy-start.8 = (bf16[256,2048]{1,0:T(8,128)(2,1)S(1)}, bf16[256,2048]{1,0:T(8,128)(2,1)}, u32[]{:S(2)}) copy-start(bf16[256,2048]{1,0:T(8,128)(2,1)} %all-gather.7.cloned.1.call-done) | copy-start | bytes 3145732
  436.8 68.7 %all-to-all-start.6 = ((bf16[64,6,2048]{2,1,0:T(8,128)(2,1)}), bf16[64,6,2048]{2,1,0:T(8,128)(2,1)S(1)}, u32[]{:S(2)}, u32[]{:S(2)}) async-start(bf16[64,6,2048]{2,1,0:T(8,128)(2,1)} %reshape.112), calls=%async_computation.8 | async-start | bytes 4194304 | tf_op jit(solution)/shard_map/all_to_all | solution.py:114
  447.5 129.9 %reduce-scatter.8.cloned.1.call-start = ((), (), s32[]{:S(2)}) async-start(), calls=%async_computation.16 | async-start | bytes 2621440 | tf_op jit(solution)/shard_map/reduce_scatter | solution.py:137
  505.5 10.9 %copy-start.6 = (s32[64,6]{0,1:T(8,128)S(1)}, s32[64,6]{0,1:T(8,128)}, u32[]{:S(2)}) copy-start(s32[64,6]{0,1:T(8,128)} %param.16) | copy-start | bytes 4612
  505.5 62.1 %all-to-all-start.4 = ((bf16[64,6,2048]{2,1,0:T(8,128)(2,1)}), bf16[64,6,2048]{2,1,0:T(8,128)(2,1)}, u32[]{:S(2)}, u32[]{:S(2)}) async-start(bf16[64,6,2048]{2,1,0:T(8,128)(2,1)} %reshape.110), calls=%async_computation.5 | async-start | bytes 4194304 | tf_op jit(solution)/shard_map/all_to_all | solution.py:114
  572.7 4.8 copy-start.1
  577.4 3.8 copy-start.7
  580.5 0.7 copy-start.3
Sparse Core Ops, SparseCore 0:
  10.4 29.7 all-gather.6
  42.0 89.8 all-gather.12
  157.9 102.1 all-gather.10
  299.2 64.3 all-gather.8
  366.0 67.1 reduce-scatter.5
  435.6 66.2 reduce-scatter.3
  504.4 31.9 reduce-scatter.7

commit v8 on v6

--- a/solution.py
+++ b/solution.py
@@ -74,18 +74,18 @@
     send = lax.dot_general(
         slot_token, normed, (((0,), (0,)), ((), ())), preferred_element_type=jnp.float32
     ).astype(jnp.bfloat16)
-    n_chunks = 2 if capacity % 2 == 0 else 1
-    chunk = capacity // n_chunks
+    bounds = (0, 2 * capacity // 3, capacity) if capacity >= 3 else (0, capacity)
+    spans = list(zip(bounds[:-1], bounds[1:]))
     send = send.reshape(n_groups, capacity, width)
     received = [
         lax.all_to_all(
-            send[:, c * chunk : (c + 1) * chunk],
+            send[:, lo:hi],
             ("dp", "expert"),
             split_axis=0,
             concat_axis=0,
             tiled=True,
         )
-        for c in range(n_chunks)
+        for lo, hi in spans
     ]
     shared_cols = shared_gate.shape[1]
     shared_cat = jnp.concatenate([shared_gate, shared_up, shared_down], axis=1)
@@ -101,7 +101,8 @@
         (received[0], shared_cat, group_rows, kv_full)
     )
     back = []
-    for c in range(n_chunks):
+    for c, (lo, hi) in enumerate(spans):
+        chunk = hi - lo
         slots_here = received[c].reshape(n_groups * chunk, width)
         rows = lax.all_gather(slots_here, "mp", axis=0, tiled=True)
         summed = lax.psum_scatter(

time: 580 us -> 551 us (0.950)
  blocking collectives: 137 us -> 72.3 us
  waiting for transfers between devices: 250 us -> 294 us
    all_to_all x2 -> x1, blocking collectives: 107 us -> 42.6 us  [on_device(): lax.all_to_all(send[:, lo:hi], ('dp', 'expert'), split_axis=0, concat_axi...]
    all_to_all x1 -> x2, waiting for transfers between devices: 51.2 us -> 77.3 us  [the longest x1 51.1 us: on_device(): lax.all_to_all(send[:, lo:hi], ('dp', 'expert'), split_axis=0, concat_axi...]
    all_to_all x2, waiting for transfers between devices: 50.1 us -> 64.8 us  [on_device(): lax.all_to_all(summed.reshape(n_groups, chunk, width), ('dp', 'expert'),...]
    all_gather x2, waiting for transfers between devices: 0.04 us -> 13.4 us  [on_device(): rows = lax.all_gather(slots_here, 'mp', axis=0, tiled=True)]
    reduce_scatter x2, waiting for transfers between devices: 92.2 us -> 79.4 us  [on_device(): lax.psum_scatter(expert_part(rows, gate_up_w, down_w).astype(jnp.bfloat16...]
    all_to_all x1 -> x2, starting transfers between devices: 13.5 us -> 14.1 us  [the longest x1 9.81 us: on_device(): lax.all_to_all(send[:, lo:hi], ('dp', 'expert'), split_axis=0, concat_axi...]
  transfers between devices with their start and end apart: 12 -> 13, of which waited for: 6 -> 9; matrix products, arithmetic and copies ran while one was open for 19% -> 19% of each run, Pallas kernels for 0% -> 0%
where the time goes in v8:
time: 551 us; the launch traced here: 542 us
  waiting for transfers between devices  294 us (53%)
  blocking collectives  72.3 us (13%)
  starting transfers between devices  51.2 us (9%)
  matrix products  50.9 us (9%)
  local copies, waits for them, and re-layouts  42.9 us (8%)
  other arithmetic  15.9 us (3%)
  between operations  14.9 us (3%)
    reduce_scatter x2, waiting for transfers between devices, on_device(): lax.psum_scatter(expert_part(rows, gate_up_w, down_w).astype(jnp.bfloat16...  79.4 us
    all_to_all x2, waiting for transfers between devices, on_device(): lax.all_to_all(summed.reshape(n_groups, chunk, width), ('dp', 'expert'),...  64.8 us
    all_to_all x1, waiting for transfers between devices, on_device(): lax.all_to_all(send[:, lo:hi], ('dp', 'expert'), split_axis=0, concat_axi...  51.1 us
    all_to_all x1, waiting for transfers between devices, on_device(): lax.all_to_all(in_send, ('expert', 'mp'), split_axis=0, concat_axis=1, ti...  48.5 us
    all_to_all x1, blocking collectives, on_device(): lax.all_to_all(send[:, lo:hi], ('dp', 'expert'), split_axis=0, concat_axi...  42.6 us
    all_to_all x1, waiting for transfers between devices, on_device(): lax.all_to_all(jnp.broadcast_to(kv_weight[None], (n_mp,) + kv_weight.shap...  26.2 us
    all_gather x1, blocking collectives, on_device(): shared_cat = lax.all_gather(shared_cat, 'dp', axis=0, tiled=False)  21.2 us
    all_to_all x2, starting transfers between devices, on_device(): lax.all_to_all(summed.reshape(n_groups, chunk, width), ('dp', 'expert'),...  21.1 us
  transfers between devices with their start and end apart: 13, of which 9 were waited for; matrix products, arithmetic and copies ran while one was open for 19% of the time, Pallas kernels for 0%

profile of v8, /device:TPU:8, one launch (start us, length us, event | category | flops | bytes accessed | tf_op | source)
XLA Modules:
  0.0 542.1 jit_solution(3544073971727459353)
XLA Ops:
  11.2 21.2 %all-gather = bf16[128,2112]{1,0:T(8,128)(2,1)} all-gather(bf16[32,2112]{1,0:T(8,128)(2,1)S(1)} %concatenate.9), channel_id=2, replica_groups=mesh['dp'=4,'expert'=16,'mp'=4] {'dp'}, dimensions={0}, use_global_device_ids=true | all-gather | bytes 675840 | tf_op jit(solution)/shard_map/all_gather | solution.py:92
  37.3 2.8 reshape.104
  42.2 42.6 %all_to_all.48 = bf16[64,4,2048]{2,1,0:T(4,128)(2,1)S(1)} all-to-all(bf16[64,4,2048]{2,1,0:T(4,128)(2,1)S(1)} %slice.68), channel_id=1, replica_groups=mesh['dp'=4,'expert'=16,'mp'=4] {'dp','expert'}, dimensions={0} | all-to-all | bytes 2097152 | tf_op jit(solution)/shard_map/all_to_all | solution.py:81
  87.6 4.3 all-to-all-start.1
  91.9 3.2 slice.61
  95.1 26.2 %all-to-all-done.1 = bf16[4,2048,144]{1,2,0:T(8,128)(2,1)S(1)} async-done(((bf16[4,2048,144]{1,2,0:T(8,128)(2,1)}), bf16[4,2048,144]{1,2,0:T(8,128)(2,1)S(1)}, u32[]{:S(2)}, u32[]{:S(2)}) %all-to-all-start.1) | async-done | bytes 2359328 | tf_op jit(solution)/shard_map/all_to_all | solution.py:97
  121.3 9.8 %all-to-all-start = ((bf16[64,8,2048]{2,1,0:T(8,128)(2,1)}), bf16[64,8,2048]{2,1,0:T(8,128)(2,1)}, u32[]{:S(2)}, u32[]{:S(2)}) async-start(bf16[64,8,2048]{2,1,0:T(8,128)(2,1)} %slice.61), calls=%async_computation | async-start | bytes 4194304 | tf_op jit(solution)/shard_map/all_to_all | solution.py:81
  131.2 51.1 %all-to-all-done = bf16[64,8,2048]{2,1,0:T(8,128)(2,1)} async-done(((bf16[64,8,2048]{2,1,0:T(8,128)(2,1)}), bf16[64,8,2048]{2,1,0:T(8,128)(2,1)}, u32[]{:S(2)}, u32[]{:S(2)}) %all-to-all-start) | async-done | bytes 2097184 | tf_op jit(solution)/shard_map/all_to_all | solution.py:81
  182.3 4.6 convert_element_type.61
  186.9 6.8 %reshape.107 = bf16[16,32,2,4,352]{4,3,2,1,0:T(4,128)(2,1)S(1)} reshape(bf16[16,32,2816]{2,1,0:T(8,128)(2,1)} %convert_element_type.61) | data formatting | bytes 5767168 | tf_op jit(solution)/shard_map/reshape | solution.py:45
  196.1 6.0 %all-to-all-start.2 = ((bf16[64,32,2,352]{3,1,2,0:T(8,128)(2,1)}), bf16[64,32,2,352]{3,1,2,0:T(8,128)(2,1)S(1)}, u32[]{:S(2)}, u32[]{:S(2)}) async-start(bf16[64,32,2,352]{3,1,2,0:T(8,128)(2,1)} %bitcast.48), calls=%async_computation.2 | async-start | bytes 6291456 | tf_op jit(solution)/shard_map/all_to_all | solution.py:56
  205.9 48.5 %all-to-all-done.2 = bf16[64,32,2,352]{3,1,2,0:T(8,128)(2,1)S(1)} async-done(((bf16[64,32,2,352]{3,1,2,0:T(8,128)(2,1)}), bf16[64,32,2,352]{3,1,2,0:T(8,128)(2,1)S(1)}, u32[]{:S(2)}, u32[]{:S(2)}) %all-to-all-start.2) | async-done | bytes 2883616 | tf_op jit(solution)/shard_map/all_to_all | solution.py:56
  254.4 9.1 %all-to-all-start.3 = ((bf16[64,32,352]{2,1,0:T(8,128)(2,1)}), bf16[64,32,352]{2,1,0:T(8,128)(2,1)}, u32[]{:S(2)}, u32[]{:S(2)}) async-start(bf16[64,32,352]{2,1,0:T(8,128)(2,1)} %bitcast.51), calls=%async_computation.3 | async-start | bytes 3145728 | tf_op jit(solution)/shard_map/all_to_all | solution.py:57
  263.7 4.9 copy.59
  268.6 6.4 %reshape.109 = bf16[2048,704]{1,0:T(8,128)(2,1)S(1)} reshape(bf16[64,32,2,352]{3,2,1,0:T(2,128)(2,1)} %copy.59) | data formatting | bytes 5767168 | tf_op jit(solution)/shard_map/reshape | solution.py:59
  275.1 7.0 %fusion.47 = f32[1024,704]{0,1:T(8,128)} fusion(bf16[1024,2048]{1,0:T(8,128)(2,1)} %all-gather.11.cloned.1.call-done, bf16[2048,704]{1,0:T(8,128)(2,1)S(1)} %reshape.109), kind=kOutput, calls=%fused_computation.64 | convolution fusion | flops 2952790016 | bytes 9961472 | tf_op jit(solution)/shard_map/dot_general | solution.py:15
  282.1 10.5 %all-to-all-done.3 = bf16[64,32,352]{2,1,0:T(8,128)(2,1)} async-done(((bf16[64,32,352]{2,1,0:T(8,128)(2,1)}), bf16[64,32,352]{2,1,0:T(8,128)(2,1)}, u32[]{:S(2)}, u32[]{:S(2)}) %all-to-all-start.3) | async-done | bytes 1441824 | tf_op jit(solution)/shard_map/all_to_all | solution.py:57
  292.6 6.7 %convolution_convert_fusion.1 = bf16[1024,2048]{1,0:T(8,128)(2,1)} fusion(bf16[2048,352]{1,0:T(8,128)(2,1)} %bitcast.7, f32[1024,704]{0,1:T(8,128)} %fusion.47), kind=kOutput, calls=%fused_computation.2 | convolution fusion | flops 1480654848 | bytes 8519680 | tf_op jit(solution)/shard_map/dot_general | solution.py:17
  299.6 13.4 %all-gather.9.cloned.1.call-done = bf16[2048,2048]{1,0:T(8,128)(2,1)} async-done(((bf16[512,2048]{1,0:T(8,128)(2,1)}), bf16[2048,2048]{1,0:T(8,128)(2,1)}) %all-gather.9.cloned.1.call-update) | async-done | bytes 8388624 | tf_op jit(solution)/shard_map/all_gather | solution.py:107
  313.0 8.8 %fusion.46 = f32[2048,704]{0,1:T(8,128)S(1)} fusion(bf16[2048,2048]{1,0:T(8,128)(2,1)} %all-gather.9.cloned.1.call-done, bf16[2048,704]{1,0:T(8,128)(2,1)S(1)} %reshape.109), kind=kOutput, calls=%fused_computation.63 | convolution fusion | flops 5905580032 | bytes 17039360 | tf_op jit(solution)/shard_map/dot_general | solution.py:15
  321.8 8.3 %convolution_convert_fusion = bf16[2048,2048]{1,0:T(8,128)(2,1)} fusion(bf16[2048,352]{1,0:T(8,128)(2,1)} %bitcast.7, f32[2048,704]{0,1:T(8,128)S(1)} %fusion.46), kind=kOutput, calls=%fused_computation | convolution fusion | flops 2961309696 | bytes 15597568 | tf_op jit(solution)/shard_map/dot_general | solution.py:17
  330.2 35.6 %reduce-scatter.6.cloned.1.call-done = bf16[256,2048]{1,0:T(8,128)(2,1)} async-done(((bf16[1024,2048]{1,0:T(8,128)(2,1)}), bf16[256,2048]{1,0:T(8,128)(2,1)}) %reduce-scatter.6.cloned.1.call-update) | async-done | bytes 1048592 | tf_op jit(solution)/shard_map/reduce_scatter | solution.py:108
  368.0 10.6 %all-to-all-start.6 = ((bf16[64,4,2048]{2,1,0:T(4,128)(2,1)}), bf16[64,4,2048]{2,1,0:T(4,128)(2,1)S(1)}, u32[]{:S(2)}, u32[]{:S(2)}) async-start(bf16[64,4,2048]{2,1,0:T(4,128)(2,1)} %reshape.114), calls=%async_computation.8 | async-start | bytes 2097152 | tf_op jit(solution)/shard_map/all_to_all | solution.py:115
  378.6 4.8 fusion.4
  383.4 24.0 %all-to-all-done.6 = bf16[64,4,2048]{2,1,0:T(4,128)(2,1)S(1)} async-done(((bf16[64,4,2048]{2,1,0:T(4,128)(2,1)}), bf16[64,4,2048]{2,1,0:T(4,128)(2,1)S(1)}, u32[]{:S(2)}, u32[]{:S(2)}) %all-to-all-start.6) | async-done | bytes 1048608 | tf_op jit(solution)/shard_map/all_to_all | solution.py:115
  407.4 43.8 %reduce-scatter.4.cloned.1.call-done = bf16[512,2048]{1,0:T(8,128)(2,1)} async-done(((bf16[2048,2048]{1,0:T(8,128)(2,1)}), bf16[512,2048]{1,0:T(8,128)(2,1)}) %reduce-scatter.4.cloned.1.call-update) | async-done | bytes 2097168 | tf_op jit(solution)/shard_map/reduce_scatter | solution.py:108
  451.2 10.6 %all-to-all-start.4 = ((bf16[64,8,2048]{2,1,0:T(8,128)(2,1)}), bf16[64,8,2048]{2,1,0:T(8,128)(2,1)S(1)}, u32[]{:S(2)}, u32[]{:S(2)}) async-start(bf16[64,8,2048]{2,1,0:T(8,128)(2,1)} %bitcast.53), calls=%async_computation.5 | async-start | bytes 4194304 | tf_op jit(solution)/shard_map/all_to_all | solution.py:115
  462.1 9.2 %fusion = f32[256,2048]{1,0:T(8,128)} fusion(bf16[2048,2112]{1,0:T(8,128)(2,1)} %bitcast.58, bf16[256,2048]{1,0:T(8,128)(2,1)} %all-gather.7.cloned.1.call-done, f32[256,704]{0,1:T(8,128)} %fusion.4), kind=kOutput, calls=%fused_computation.4 | convolution fusion | flops 1477476352 | bytes 10158080 | tf_op jit(solution)/shard_map/dot_general | solution.py:139
  472.3 40.8 %all-to-all-done.4 = bf16[64,8,2048]{2,1,0:T(8,128)(2,1)S(1)} async-done(((bf16[64,8,2048]{2,1,0:T(8,128)(2,1)}), bf16[64,8,2048]{2,1,0:T(8,128)(2,1)S(1)}, u32[]{:S(2)}, u32[]{:S(2)}) %all-to-all-start.4) | async-done | bytes 2097184 | tf_op jit(solution)/shard_map/all_to_all | solution.py:115
  515.8 4.8 reshape.115
  520.6 3.2 fusion.28
  525.5 8.5 %all_to_all.49 = bf16[4,64,144]{2,1,0:T(8,128)(2,1)S(1)} all-to-all(bf16[4,64,144]{2,1,0:T(8,128)(2,1)S(1)} %bitcast.54), channel_id=1, replica_groups=mesh['dp'=4,'expert'=16,'mp'=4] {'mp'}, dimensions={0} | all-to-all | bytes 147456 | tf_op jit(solution)/shard_map/all_to_all | solution.py:151
  (70 shorter events, 29.2 us)
Async XLA Ops:
  7.2 27.9 %copy-start.5 = (s32[64,6]{0,1:T(8,128)S(1)}, s32[64,6]{0,1:T(8,128)}, u32[]{:S(2)}) copy-start(s32[64,6]{0,1:T(8,128)} %param.15) | copy-start | bytes 4612
  7.2 124.0 %all-gather.7.cloned.1.call-start = ((), (), s32[]{:S(2)}) async-start(), calls=%async_computation.11 | async-start | bytes 1310720 | tf_op jit(solution)/shard_map/all_gather | solution.py:95
  10.2 172.1 %all-gather.13.cloned.1.call-start = ((), (), s32[]{:S(2)}) async-start(), calls=%async_computation.17 | async-start | bytes 9469952 | tf_op jit(solution)/shard_map/all_gather | solution.py:93
  32.4 242.7 %all-gather.11.cloned.1.call-start = ((), (), s32[]{:S(2)}) async-start(), calls=%async_computation.14 | async-start | bytes 5242880 | tf_op jit(solution)/shard_map/all_gather | solution.py:107
  42.2 43.7 %copy-start.4 = (bf16[2048,144]{0,1:T(8,128)(2,1)S(1)}, bf16[2048,144]{0,1:T(8,128)(2,1)}, u32[]{:S(2)}) copy-start(bf16[2048,144]{0,1:T(8,128)(2,1)} %param.21) | copy-start | bytes 1769476
  87.6 33.7 %all-to-all-start.1 = ((bf16[4,2048,144]{1,2,0:T(8,128)(2,1)}), bf16[4,2048,144]{1,2,0:T(8,128)(2,1)S(1)}, u32[]{:S(2)}, u32[]{:S(2)}) async-start(bf16[4,2048,144]{1,2,0:T(8,128)(2,1)} %broadcast_in_dim.12), calls=%async_computation.1 | async-start | bytes 4718592 | tf_op jit(solution)/shard_map/all_to_all | solution.py:97
  121.3 61.0 %copy-start = (bf16[4,2048,144]{1,2,0:T(8,128)(2,1)}, bf16[4,2048,144]{1,2,0:T(8,128)(2,1)S(1)}, u32[]{:S(2)}) copy-start(bf16[4,2048,144]{1,2,0:T(8,128)(2,1)S(1)} %all-to-all-done.1) | copy-start | bytes 7077892
  121.3 61.0 %all-to-all-start = ((bf16[64,8,2048]{2,1,0:T(8,128)(2,1)}), bf16[64,8,2048]{2,1,0:T(8,128)(2,1)}, u32[]{:S(2)}, u32[]{:S(2)}) async-start(bf16[64,8,2048]{2,1,0:T(8,128)(2,1)} %slice.61), calls=%async_computation | async-start | bytes 4194304 | tf_op jit(solution)/shard_map/all_to_all | solution.py:81
  131.1 181.9 %all-gather.9.cloned.1.call-start = ((), (), s32[]{:S(2)}) async-start(), calls=%async_computation.12 | async-start | bytes 10485760 | tf_op jit(solution)/shard_map/all_gather | solution.py:107
  196.1 58.3 %all-to-all-start.2 = ((bf16[64,32,2,352]{3,1,2,0:T(8,128)(2,1)}), bf16[64,32,2,352]{3,1,2,0:T(8,128)(2,1)S(1)}, u32[]{:S(2)}, u32[]{:S(2)}) async-start(bf16[64,32,2,352]{3,1,2,0:T(8,128)(2,1)} %bitcast.48), calls=%async_computation.2 | async-start | bytes 6291456 | tf_op jit(solution)/shard_map/all_to_all | solution.py:56
  254.4 38.2 %all-to-all-start.3 = ((bf16[64,32,352]{2,1,0:T(8,128)(2,1)}), bf16[64,32,352]{2,1,0:T(8,128)(2,1)}, u32[]{:S(2)}, u32[]{:S(2)}) async-start(bf16[64,32,352]{2,1,0:T(8,128)(2,1)} %bitcast.51), calls=%async_computation.3 | async-start | bytes 3145728 | tf_op jit(solution)/shard_map/all_to_all | solution.py:57
  263.5 102.3 %reduce-scatter.6.cloned.1.call-start = ((), (), s32[]{:S(2)}) async-start(), calls=%async_computation.15 | async-start | bytes 5242880 | tf_op jit(solution)/shard_map/reduce_scatter | solution.py:108
  299.3 151.9 %reduce-scatter.4.cloned.1.call-start = ((), (), s32[]{:S(2)}) async-start(), calls=%async_computation.13 | async-start | bytes 10485760 | tf_op jit(solution)/shard_map/reduce_scatter | solution.py:108
  330.2 48.4 %copy-start.8 = (bf16[256,2048]{1,0:T(8,128)(2,1)S(1)}, bf16[256,2048]{1,0:T(8,128)(2,1)}, u32[]{:S(2)}) copy-start(bf16[256,2048]{1,0:T(8,128)(2,1)} %all-gather.7.cloned.1.call-done) | copy-start | bytes 3145732
  368.0 39.4 %all-to-all-start.6 = ((bf16[64,4,2048]{2,1,0:T(4,128)(2,1)}), bf16[64,4,2048]{2,1,0:T(4,128)(2,1)S(1)}, u32[]{:S(2)}, u32[]{:S(2)}) async-start(bf16[64,4,2048]{2,1,0:T(4,128)(2,1)} %reshape.114), calls=%async_computation.8 | async-start | bytes 2097152 | tf_op jit(solution)/shard_map/all_to_all | solution.py:115
  451.2 61.8 %all-to-all-start.4 = ((bf16[64,8,2048]{2,1,0:T(8,128)(2,1)}), bf16[64,8,2048]{2,1,0:T(8,128)(2,1)S(1)}, u32[]{:S(2)}, u32[]{:S(2)}) async-start(bf16[64,8,2048]{2,1,0:T(8,128)(2,1)} %bitcast.53), calls=%async_computation.5 | async-start | bytes 4194304 | tf_op jit(solution)/shard_map/all_to_all | solution.py:115
  461.8 9.6 %copy-start.6 = (s32[64,6]{0,1:T(8,128)S(1)}, s32[64,6]{0,1:T(8,128)}, u32[]{:S(2)}) copy-start(s32[64,6]{0,1:T(8,128)} %param.16) | copy-start | bytes 4612
  461.8 58.8 %reduce-scatter.8.cloned.1.call-start = ((), (), s32[]{:S(2)}) async-start(), calls=%async_computation.16 | async-start | bytes 2621440 | tf_op jit(solution)/shard_map/reduce_scatter | solution.py:138
  515.8 4.8 copy-start.2
  520.6 3.9 copy-start.7
  520.6 3.9 copy-start.1
  523.8 0.7 copy-start.3
Sparse Core Ops, SparseCore 0:
  10.4 29.3 all-gather.6
  41.6 74.7 all-gather.12
  118.2 53.2 all-gather.10
  182.4 130.5 all-gather.8
  315.4 50.3 reduce-scatter.5
  368.4 82.7 reduce-scatter.3
  471.5 31.7 reduce-scatter.7

commit v9 on v8

--- a/solution.py
+++ b/solution.py
@@ -74,7 +74,7 @@
     send = lax.dot_general(
         slot_token, normed, (((0,), (0,)), ((), ())), preferred_element_type=jnp.float32
     ).astype(jnp.bfloat16)
-    bounds = (0, 2 * capacity // 3, capacity) if capacity >= 3 else (0, capacity)
+    bounds = (0, 3 * capacity // 4, capacity) if capacity >= 4 else (0, capacity)
     spans = list(zip(bounds[:-1], bounds[1:]))
     send = send.reshape(n_groups, capacity, width)
     received = [

time: 551 us -> 663 us (1.20)
  waiting for transfers between devices: 294 us -> 396 us
  local copies, waits for them, and re-layouts: 42.9 us -> 51.9 us
    all_to_all x1, waiting for transfers between devices: 51.1 us -> 96 us  [on_device(): lax.all_to_all(send[:, lo:hi], ('dp', 'expert'), split_axis=0, concat_axi...]
    reduce_scatter x2, waiting for transfers between devices: 79.4 us -> 105 us  [on_device(): lax.psum_scatter(expert_part(rows, gate_up_w, down_w).astype(jnp.bfloat16...]
    all_to_all x2, waiting for transfers between devices: 64.8 us -> 83 us  [on_device(): lax.all_to_all(summed.reshape(n_groups, chunk, width), ('dp', 'expert'),...]
    all_gather x2, waiting for transfers between devices: 13.4 us -> 23.4 us  [on_device(): rows = lax.all_gather(slots_here, 'mp', axis=0, tiled=True)]
  transfers between devices with their start and end apart: 13 -> 13, of which waited for: 9 -> 8; matrix products, arithmetic and copies ran while one was open for 19% -> 17% of each run, Pallas kernels for 0% -> 0%
where the time goes in v9:
time: 663 us; the launch traced here: 653 us
  waiting for transfers between devices  396 us (60%)
  blocking collectives  72.2 us (11%)
  local copies, waits for them, and re-layouts  51.9 us (8%)
  starting transfers between devices  51.4 us (8%)
  matrix products  47.9 us (7%)
  other arithmetic  18.8 us (3%)
  between operations  14.8 us (2%)
    reduce_scatter x2, waiting for transfers between devices, on_device(): lax.psum_scatter(expert_part(rows, gate_up_w, down_w).astype(jnp.bfloat16...  105 us
    all_to_all x1, waiting for transfers between devices, on_device(): lax.all_to_all(send[:, lo:hi], ('dp', 'expert'), split_axis=0, concat_axi...  96 us
    all_to_all x2, waiting for transfers between devices, on_device(): lax.all_to_all(summed.reshape(n_groups, chunk, width), ('dp', 'expert'),...  83 us
    all_to_all x1, waiting for transfers between devices, on_device(): lax.all_to_all(in_send, ('expert', 'mp'), split_axis=0, concat_axis=1, ti...  48.5 us
    all_to_all x1, blocking collectives, on_device(): lax.all_to_all(send[:, lo:hi], ('dp', 'expert'), split_axis=0, concat_axi...  42.4 us
    all_to_all x1, waiting for transfers between devices, on_device(): lax.all_to_all(jnp.broadcast_to(kv_weight[None], (n_mp,) + kv_weight.shap...  28 us
    all_gather x2, waiting for transfers between devices, on_device(): rows = lax.all_gather(slots_here, 'mp', axis=0, tiled=True)  23.4 us
    all_to_all x2, starting transfers between devices, on_device(): lax.all_to_all(summed.reshape(n_groups, chunk, width), ('dp', 'expert'),...  21.4 us
  transfers between devices with their start and end apart: 13, of which 8 were waited for; matrix products, arithmetic and copies ran while one was open for 17% of the time, Pallas kernels for 0%

profile of v9, /device:TPU:8, one launch (start us, length us, event | category | flops | bytes accessed | tf_op | source)
XLA Modules:
  0.0 653.3 jit_solution(10739740823751758865)
XLA Ops:
  11.2 21.2 %all-gather = bf16[128,2112]{1,0:T(8,128)(2,1)} all-gather(bf16[32,2112]{1,0:T(8,128)(2,1)S(1)} %concatenate.9), channel_id=2, replica_groups=mesh['dp'=4,'expert'=16,'mp'=4] {'dp'}, dimensions={0}, use_global_device_ids=true | all-gather | bytes 675840 | tf_op jit(solution)/shard_map/all_gather | solution.py:92
  42.2 42.4 %all_to_all.48 = bf16[64,3,2048]{2,1,0:T(4,128)(2,1)S(1)} all-to-all(bf16[64,3,2048]{2,1,0:T(4,128)(2,1)S(1)} %slice.68), channel_id=1, replica_groups=mesh['dp'=4,'expert'=16,'mp'=4] {'dp','expert'}, dimensions={0} | all-to-all | bytes 1572864 | tf_op jit(solution)/shard_map/all_to_all | solution.py:81
  86.4 4.3 all-to-all-start.1
  92.1 28.0 %all-to-all-done.1 = bf16[4,2048,144]{1,2,0:T(8,128)(2,1)S(1)} async-done(((bf16[4,2048,144]{1,2,0:T(8,128)(2,1)}), bf16[4,2048,144]{1,2,0:T(8,128)(2,1)S(1)}, u32[]{:S(2)}, u32[]{:S(2)}) %all-to-all-start.1) | async-done | bytes 2359328 | tf_op jit(solution)/shard_map/all_to_all | solution.py:97
  121.6 9.7 %all-to-all-start = ((bf16[64,9,2048]{2,1,0:T(8,128)(2,1)}), bf16[64,9,2048]{2,1,0:T(8,128)(2,1)}, u32[]{:S(2)}, u32[]{:S(2)}) async-start(bf16[64,9,2048]{2,1,0:T(8,128)(2,1)} %bitcast.47), calls=%async_computation | async-start | bytes 8388608 | tf_op jit(solution)/shard_map/all_to_all | solution.py:81
  131.4 96.0 %all-to-all-done = bf16[64,9,2048]{2,1,0:T(8,128)(2,1)} async-done(((bf16[64,9,2048]{2,1,0:T(8,128)(2,1)}), bf16[64,9,2048]{2,1,0:T(8,128)(2,1)}, u32[]{:S(2)}, u32[]{:S(2)}) %all-to-all-start) | async-done | bytes 2359328 | tf_op jit(solution)/shard_map/all_to_all | solution.py:81
  227.4 4.7 reshape.106
  232.2 4.6 convert_element_type.61
  236.8 6.8 %reshape.107 = bf16[16,32,2,4,352]{4,3,2,1,0:T(4,128)(2,1)S(1)} reshape(bf16[16,32,2816]{2,1,0:T(8,128)(2,1)} %convert_element_type.61) | data formatting | bytes 5767168 | tf_op jit(solution)/shard_map/reshape | solution.py:45
  245.9 6.0 all-to-all-start.2
  255.8 48.5 %all-to-all-done.2 = bf16[64,32,2,352]{3,1,2,0:T(8,128)(2,1)S(1)} async-done(((bf16[64,32,2,352]{3,1,2,0:T(8,128)(2,1)}), bf16[64,32,2,352]{3,1,2,0:T(8,128)(2,1)S(1)}, u32[]{:S(2)}, u32[]{:S(2)}) %all-to-all-start.2) | async-done | bytes 2883616 | tf_op jit(solution)/shard_map/all_to_all | solution.py:56
  304.2 9.1 %all-to-all-start.3 = ((bf16[64,32,352]{2,1,0:T(8,128)(2,1)}), bf16[64,32,352]{2,1,0:T(8,128)(2,1)}, u32[]{:S(2)}, u32[]{:S(2)}) async-start(bf16[64,32,352]{2,1,0:T(8,128)(2,1)} %bitcast.51), calls=%async_computation.3 | async-start | bytes 3145728 | tf_op jit(solution)/shard_map/all_to_all | solution.py:57
  313.6 4.9 copy.59
  318.5 6.4 reshape.109
  324.9 5.7 fusion.47
  330.7 11.8 %all-to-all-done.3 = bf16[64,32,352]{2,1,0:T(8,128)(2,1)} async-done(((bf16[64,32,352]{2,1,0:T(8,128)(2,1)}), bf16[64,32,352]{2,1,0:T(8,128)(2,1)}, u32[]{:S(2)}, u32[]{:S(2)}) %all-to-all-start.3) | async-done | bytes 1441824 | tf_op jit(solution)/shard_map/all_to_all | solution.py:57
  342.5 5.6 convolution_convert_fusion.1
  348.3 23.4 %all-gather.9.cloned.1.call-done = bf16[2304,2048]{1,0:T(8,128)(2,1)} async-done(((bf16[576,2048]{1,0:T(8,128)(2,1)}), bf16[2304,2048]{1,0:T(8,128)(2,1)}) %all-gather.9.cloned.1.call-update) | async-done | bytes 9437200 | tf_op jit(solution)/shard_map/all_gather | solution.py:107
  371.7 9.6 %fusion.46 = f32[2304,704]{0,1:T(8,128)S(1)} fusion(bf16[2304,2048]{1,0:T(8,128)(2,1)} %all-gather.9.cloned.1.call-done, bf16[2048,704]{1,0:T(8,128)(2,1)S(1)} %reshape.109), kind=kOutput, calls=%fused_computation.63 | convolution fusion | flops 6643777536 | bytes 18808832 | tf_op jit(solution)/shard_map/dot_general | solution.py:15
  381.4 9.1 %convolution_convert_fusion = bf16[2304,2048]{1,0:T(8,128)(2,1)} fusion(bf16[2048,352]{1,0:T(8,128)(2,1)} %bitcast.6, f32[2304,704]{0,1:T(8,128)S(1)} %fusion.46), kind=kOutput, calls=%fused_computation | convolution fusion | flops 3331473408 | bytes 17367040 | tf_op jit(solution)/shard_map/dot_general | solution.py:17
  390.4 25.5 %reduce-scatter.6.cloned.1.call-done = bf16[192,2048]{1,0:T(8,128)(2,1)} async-done(((bf16[768,2048]{1,0:T(8,128)(2,1)}), bf16[192,2048]{1,0:T(8,128)(2,1)}) %reduce-scatter.6.cloned.1.call-update) | async-done | bytes 786448 | tf_op jit(solution)/shard_map/reduce_scatter | solution.py:108
  416.0 3.3 reshape.114
  419.2 10.6 %all-to-all-start.6 = ((bf16[64,3,2048]{2,1,0:T(4,128)(2,1)}), bf16[64,3,2048]{2,1,0:T(4,128)(2,1)S(1)}, u32[]{:S(2)}, u32[]{:S(2)}) async-start(bf16[64,3,2048]{2,1,0:T(4,128)(2,1)} %reshape.114), calls=%async_computation.8 | async-start | bytes 2097152 | tf_op jit(solution)/shard_map/all_to_all | solution.py:115
  429.8 79.9 %reduce-scatter.4.cloned.1.call-done = bf16[576,2048]{1,0:T(8,128)(2,1)} async-done(((bf16[2304,2048]{1,0:T(8,128)(2,1)}), bf16[576,2048]{1,0:T(8,128)(2,1)}) %reduce-scatter.4.cloned.1.call-update) | async-done | bytes 2359312 | tf_op jit(solution)/shard_map/reduce_scatter | solution.py:108
  509.7 4.6 reshape.112
  514.3 10.9 %all-to-all-start.4 = ((bf16[64,9,2048]{2,1,0:T(8,128)(2,1)}), bf16[64,9,2048]{2,1,0:T(8,128)(2,1)}, u32[]{:S(2)}, u32[]{:S(2)}) async-start(bf16[64,9,2048]{2,1,0:T(8,128)(2,1)} %reshape.112), calls=%async_computation.5 | async-start | bytes 8388608 | tf_op jit(solution)/shard_map/all_to_all | solution.py:115
  525.5 3.2 fusion.5
  528.8 8.7 %fusion.1 = f32[256,2048]{1,0:T(8,128)} fusion(bf16[2048,2112]{1,0:T(8,128)(2,1)} %bitcast.57, bf16[256,2048]{1,0:T(8,128)(2,1)S(1)} %copy-done.8, f32[256,704]{0,1:T(8,128)S(1)} %fusion.5), kind=kOutput, calls=%fused_computation.6 | convolution fusion | flops 1477476352 | bytes 10158080 | tf_op jit(solution)/shard_map/dot_general | solution.py:139
  538.4 83.0 %all-to-all-done.4 = bf16[64,9,2048]{2,1,0:T(8,128)(2,1)} async-done(((bf16[64,9,2048]{2,1,0:T(8,128)(2,1)}), bf16[64,9,2048]{2,1,0:T(8,128)(2,1)}, u32[]{:S(2)}, u32[]{:S(2)}) %all-to-all-start.4) | async-done | bytes 2359328 | tf_op jit(solution)/shard_map/all_to_all | solution.py:115
  621.3 5.7 pad_maximum_fusion
  627.0 4.8 reshape.115
  636.7 8.5 %all_to_all.49 = bf16[4,64,144]{2,1,0:T(8,128)(2,1)S(1)} all-to-all(bf16[4,64,144]{2,1,0:T(8,128)(2,1)S(1)} %bitcast.53), channel_id=1, replica_groups=mesh['dp'=4,'expert'=16,'mp'=4] {'mp'}, dimensions={0} | all-to-all | bytes 147456 | tf_op jit(solution)/shard_map/all_to_all | solution.py:151
  (71 shorter events, 32.0 us)
Async XLA Ops:
  7.2 27.8 %copy-start.5 = (s32[64,6]{0,1:T(8,128)S(1)}, s32[64,6]{0,1:T(8,128)}, u32[]{:S(2)}) copy-start(s32[64,6]{0,1:T(8,128)} %param.15) | copy-start | bytes 4612
  7.2 124.2 %all-gather.7.cloned.1.call-start = ((), (), s32[]{:S(2)}) async-start(), calls=%async_computation.11 | async-start | bytes 1310720 | tf_op jit(solution)/shard_map/all_gather | solution.py:95
  10.2 217.3 %all-gather.13.cloned.1.call-start = ((), (), s32[]{:S(2)}) async-start(), calls=%async_computation.17 | async-start | bytes 9469952 | tf_op jit(solution)/shard_map/all_gather | solution.py:93
  40.0 44.7 %copy-start.4 = (bf16[2048,144]{0,1:T(8,128)(2,1)S(1)}, bf16[2048,144]{0,1:T(8,128)(2,1)}, u32[]{:S(2)}) copy-start(bf16[2048,144]{0,1:T(8,128)(2,1)} %param.21) | copy-start | bytes 1769476
  86.4 33.7 %all-to-all-start.1 = ((bf16[4,2048,144]{1,2,0:T(8,128)(2,1)}), bf16[4,2048,144]{1,2,0:T(8,128)(2,1)S(1)}, u32[]{:S(2)}, u32[]{:S(2)}) async-start(bf16[4,2048,144]{1,2,0:T(8,128)(2,1)} %broadcast_in_dim.12), calls=%async_computation.1 | async-start | bytes 4718592 | tf_op jit(solution)/shard_map/all_to_all | solution.py:97
  90.7 234.3 %all-gather.11.cloned.1.call-start = ((), (), s32[]{:S(2)}) async-start(), calls=%async_computation.14 | async-start | bytes 3932160 | tf_op jit(solution)/shard_map/all_gather | solution.py:107
  120.1 1.5 copy-start
  121.6 105.9 %all-to-all-start = ((bf16[64,9,2048]{2,1,0:T(8,128)(2,1)}), bf16[64,9,2048]{2,1,0:T(8,128)(2,1)}, u32[]{:S(2)}, u32[]{:S(2)}) async-start(bf16[64,9,2048]{2,1,0:T(8,128)(2,1)} %bitcast.47), calls=%async_computation | async-start | bytes 8388608 | tf_op jit(solution)/shard_map/all_to_all | solution.py:81
  131.3 240.4 %all-gather.9.cloned.1.call-start = ((), (), s32[]{:S(2)}) async-start(), calls=%async_computation.12 | async-start | bytes 11796480 | tf_op jit(solution)/shard_map/all_gather | solution.py:107
  245.9 58.3 %all-to-all-start.2 = ((bf16[64,32,2,352]{3,1,2,0:T(8,128)(2,1)}), bf16[64,32,2,352]{3,1,2,0:T(8,128)(2,1)S(1)}, u32[]{:S(2)}, u32[]{:S(2)}) async-start(bf16[64,32,2,352]{3,1,2,0:T(8,128)(2,1)} %bitcast.48), calls=%async_computation.2 | async-start | bytes 6291456 | tf_op jit(solution)/shard_map/all_to_all | solution.py:56
  304.2 38.2 %all-to-all-start.3 = ((bf16[64,32,352]{2,1,0:T(8,128)(2,1)}), bf16[64,32,352]{2,1,0:T(8,128)(2,1)}, u32[]{:S(2)}, u32[]{:S(2)}) async-start(bf16[64,32,352]{2,1,0:T(8,128)(2,1)} %bitcast.51), calls=%async_computation.3 | async-start | bytes 3145728 | tf_op jit(solution)/shard_map/all_to_all | solution.py:57
  313.3 102.6 %reduce-scatter.6.cloned.1.call-start = ((), (), s32[]{:S(2)}) async-start(), calls=%async_computation.15 | async-start | bytes 3932160 | tf_op jit(solution)/shard_map/reduce_scatter | solution.py:108
  348.1 161.7 %reduce-scatter.4.cloned.1.call-start = ((), (), s32[]{:S(2)}) async-start(), calls=%async_computation.13 | async-start | bytes 11796480 | tf_op jit(solution)/shard_map/reduce_scatter | solution.py:108
  419.2 95.1 %all-to-all-start.6 = ((bf16[64,3,2048]{2,1,0:T(4,128)(2,1)}), bf16[64,3,2048]{2,1,0:T(4,128)(2,1)S(1)}, u32[]{:S(2)}, u32[]{:S(2)}) async-start(bf16[64,3,2048]{2,1,0:T(4,128)(2,1)} %reshape.114), calls=%async_computation.8 | async-start | bytes 2097152 | tf_op jit(solution)/shard_map/all_to_all | solution.py:115
  514.3 11.2 %copy-start.8 = (bf16[256,2048]{1,0:T(8,128)(2,1)S(1)}, bf16[256,2048]{1,0:T(8,128)(2,1)}, u32[]{:S(2)}) copy-start(bf16[256,2048]{1,0:T(8,128)(2,1)} %all-gather.7.cloned.1.call-done) | copy-start | bytes 3145732
  514.3 107.0 %all-to-all-start.4 = ((bf16[64,9,2048]{2,1,0:T(8,128)(2,1)}), bf16[64,9,2048]{2,1,0:T(8,128)(2,1)}, u32[]{:S(2)}, u32[]{:S(2)}) async-start(bf16[64,9,2048]{2,1,0:T(8,128)(2,1)} %reshape.112), calls=%async_computation.5 | async-start | bytes 8388608 | tf_op jit(solution)/shard_map/all_to_all | solution.py:115
  525.2 106.6 %reduce-scatter.8.cloned.1.call-start = ((), (), s32[]{:S(2)}) async-start(), calls=%async_computation.16 | async-start | bytes 2621440 | tf_op jit(solution)/shard_map/reduce_scatter | solution.py:138
  528.8 8.7 %copy-start.6 = (s32[64,6]{0,1:T(8,128)S(1)}, s32[64,6]{0,1:T(8,128)}, u32[]{:S(2)}) copy-start(s32[64,6]{0,1:T(8,128)} %param.16) | copy-start | bytes 4612
  627.0 4.8 copy-start.2
  631.8 3.9 copy-start.7
  631.8 3.9 copy-start.1
  635.0 0.7 copy-start.3
Sparse Core Ops, SparseCore 0:
  10.4 29.3 all-gather.6
  41.6 74.6 all-gather.12
  118.1 44.5 all-gather.10
  232.3 139.4 all-gather.8
  374.1 41.7 reduce-scatter.5
  418.4 91.2 reduce-scatter.3
  537.6 31.7 reduce-scatter.7

commit v10 on v9

--- a/solution.py
+++ b/solution.py
@@ -74,7 +74,7 @@
     send = lax.dot_general(
         slot_token, normed, (((0,), (0,)), ((), ())), preferred_element_type=jnp.float32
     ).astype(jnp.bfloat16)
-    bounds = (0, 3 * capacity // 4, capacity) if capacity >= 4 else (0, capacity)
+    bounds = (0, 5 * capacity // 12, capacity) if capacity >= 3 else (0, capacity)
     spans = list(zip(bounds[:-1], bounds[1:]))
     send = send.reshape(n_groups, capacity, width)
     received = [

time: 663 us -> 559 us (0.84)
  waiting for transfers between devices: 396 us -> 256 us
  blocking collectives: 72.2 us -> 105 us
    all_to_all x1, waiting for transfers between devices: 96 us -> 37.5 us  [on_device(): lax.all_to_all(send[:, lo:hi], ('dp', 'expert'), split_axis=0, concat_axi...]
    all_to_all x1, blocking collectives: 42.4 us -> 75 us  [on_device(): lax.all_to_all(send[:, lo:hi], ('dp', 'expert'), split_axis=0, concat_axi...]
    all_to_all x2, waiting for transfers between devices: 83 us -> 52.3 us  [on_device(): lax.all_to_all(summed.reshape(n_groups, chunk, width), ('dp', 'expert'),...]
    all_gather x2, waiting for transfers between devices: 23.4 us -> 3.45 us  [on_device(): rows = lax.all_gather(slots_here, 'mp', axis=0, tiled=True)]
    reduce_scatter x2, waiting for transfers between devices: 105 us -> 93.1 us  [on_device(): lax.psum_scatter(expert_part(rows, gate_up_w, down_w).astype(jnp.bfloat16...]
    all_to_all x1, waiting for transfers between devices: 48.5 us -> 37.4 us  [on_device(): lax.all_to_all(in_send, ('expert', 'mp'), split_axis=0, concat_axis=1, ti...]
  transfers between devices with their start and end apart: 13 -> 13, of which waited for: 8 -> 9; matrix products, arithmetic and copies ran while one was open for 17% -> 21% of each run, Pallas kernels for 0% -> 0%
where the time goes in v10:
time: 559 us; the launch traced here: 550 us
  waiting for transfers between devices  256 us (46%)
  blocking collectives  105 us (19%)
  matrix products  52.6 us (9%)
  local copies, waits for them, and re-layouts  52.5 us (9%)
  starting transfers between devices  51.4 us (9%)
  other arithmetic  18.2 us (3%)
  between operations  14.6 us (3%)
    reduce_scatter x2, waiting for transfers between devices, on_device(): lax.psum_scatter(expert_part(rows, gate_up_w, down_w).astype(jnp.bfloat16...  93.1 us
    all_to_all x1, blocking collectives, on_device(): lax.all_to_all(send[:, lo:hi], ('dp', 'expert'), split_axis=0, concat_axi...  75 us
    all_to_all x2, waiting for transfers between devices, on_device(): lax.all_to_all(summed.reshape(n_groups, chunk, width), ('dp', 'expert'),...  52.3 us
    all_to_all x1, waiting for transfers between devices, on_device(): lax.all_to_all(send[:, lo:hi], ('dp', 'expert'), split_axis=0, concat_axi...  37.5 us
    all_to_all x1, waiting for transfers between devices, on_device(): lax.all_to_all(in_send, ('expert', 'mp'), split_axis=0, concat_axis=1, ti...  37.4 us
    all_to_all x1, waiting for transfers between devices, on_device(): lax.all_to_all(jnp.broadcast_to(kv_weight[None], (n_mp,) + kv_weight.shap...  24.9 us
    all_gather x1, blocking collectives, on_device(): shared_cat = lax.all_gather(shared_cat, 'dp', axis=0, tiled=False)  21.2 us
    all_to_all x2, starting transfers between devices, on_device(): lax.all_to_all(summed.reshape(n_groups, chunk, width), ('dp', 'expert'),...  19.3 us
  transfers between devices with their start and end apart: 13, of which 9 were waited for; matrix products, arithmetic and copies ran while one was open for 21% of the time, Pallas kernels for 0%

profile of v10, /device:TPU:8, one launch (start us, length us, event | category | flops | bytes accessed | tf_op | source)
XLA Modules:
  0.0 549.6 jit_solution(16665083584550809228)
XLA Ops:
  11.2 21.2 %all-gather = bf16[128,2112]{1,0:T(8,128)(2,1)} all-gather(bf16[32,2112]{1,0:T(8,128)(2,1)S(1)} %concatenate.9), channel_id=2, replica_groups=mesh['dp'=4,'expert'=16,'mp'=4] {'dp'}, dimensions={0}, use_global_device_ids=true | all-gather | bytes 675840 | tf_op jit(solution)/shard_map/all_gather | solution.py:92
  42.9 75.0 %all_to_all.48 = bf16[64,7,2048]{2,1,0:T(8,128)(2,1)S(1)} all-to-all(bf16[64,7,2048]{2,1,0:T(8,128)(2,1)S(1)} %slice.68), channel_id=1, replica_groups=mesh['dp'=4,'expert'=16,'mp'=4] {'dp','expert'}, dimensions={0} | all-to-all | bytes 3670016 | tf_op jit(solution)/shard_map/all_to_all | solution.py:81
  121.3 4.3 all-to-all-start.1
  128.9 24.9 %all-to-all-done.1 = bf16[4,2048,144]{1,2,0:T(8,128)(2,1)S(1)} async-done(((bf16[4,2048,144]{1,2,0:T(8,128)(2,1)}), bf16[4,2048,144]{1,2,0:T(8,128)(2,1)S(1)}, u32[]{:S(2)}, u32[]{:S(2)}) %all-to-all-start.1) | async-done | bytes 2359328 | tf_op jit(solution)/shard_map/all_to_all | solution.py:97
  153.7 12.2 %all-to-all-start = ((bf16[64,5,2048]{2,1,0:T(8,128)(2,1)}), bf16[64,5,2048]{2,1,0:T(8,128)(2,1)}, u32[]{:S(2)}, u32[]{:S(2)}) async-start(bf16[64,5,2048]{2,1,0:T(8,128)(2,1)} %slice.61), calls=%async_computation | async-start | bytes 4194304 | tf_op jit(solution)/shard_map/all_to_all | solution.py:81
  166.0 4.6 convert_element_type.61
  170.6 6.6 %reshape.107 = bf16[16,32,2,4,352]{4,3,2,1,0:T(4,128)(2,1)S(1)} reshape(bf16[16,32,2816]{2,1,0:T(8,128)(2,1)} %convert_element_type.61) | data formatting | bytes 5767168 | tf_op jit(solution)/shard_map/reshape | solution.py:45
  179.6 37.5 %all-to-all-done = bf16[64,5,2048]{2,1,0:T(8,128)(2,1)} async-done(((bf16[64,5,2048]{2,1,0:T(8,128)(2,1)}), bf16[64,5,2048]{2,1,0:T(8,128)(2,1)}, u32[]{:S(2)}, u32[]{:S(2)}) %all-to-all-start) | async-done | bytes 1310752 | tf_op jit(solution)/shard_map/all_to_all | solution.py:81
  217.2 6.0 %all-to-all-start.2 = ((bf16[64,32,2,352]{3,1,2,0:T(8,128)(2,1)}), bf16[64,32,2,352]{3,1,2,0:T(8,128)(2,1)S(1)}, u32[]{:S(2)}, u32[]{:S(2)}) async-start(bf16[64,32,2,352]{3,1,2,0:T(8,128)(2,1)} %bitcast.46), calls=%async_computation.2 | async-start | bytes 6291456 | tf_op jit(solution)/shard_map/all_to_all | solution.py:56
  223.3 3.6 reshape.106
  230.8 37.4 %all-to-all-done.2 = bf16[64,32,2,352]{3,1,2,0:T(8,128)(2,1)S(1)} async-done(((bf16[64,32,2,352]{3,1,2,0:T(8,128)(2,1)}), bf16[64,32,2,352]{3,1,2,0:T(8,128)(2,1)S(1)}, u32[]{:S(2)}, u32[]{:S(2)}) %all-to-all-start.2) | async-done | bytes 2883616 | tf_op jit(solution)/shard_map/all_to_all | solution.py:56
  268.3 8.4 %all-to-all-start.3 = ((bf16[64,32,352]{2,1,0:T(8,128)(2,1)}), bf16[64,32,352]{2,1,0:T(8,128)(2,1)}, u32[]{:S(2)}, u32[]{:S(2)}) async-start(bf16[64,32,352]{2,1,0:T(8,128)(2,1)} %bitcast.49), calls=%async_computation.3 | async-start | bytes 3145728 | tf_op jit(solution)/shard_map/all_to_all | solution.py:57
  277.0 4.9 copy.59
  281.9 6.4 %reshape.109 = bf16[2048,704]{1,0:T(8,128)(2,1)S(1)} reshape(bf16[64,32,2,352]{3,2,1,0:T(2,128)(2,1)} %copy.59) | data formatting | bytes 5767168 | tf_op jit(solution)/shard_map/reshape | solution.py:59
  288.4 10.8 %fusion.47 = f32[1792,704]{0,1:T(8,128)} fusion(bf16[1792,2048]{1,0:T(8,128)(2,1)} %all-gather.11.cloned.1.call-done, bf16[2048,704]{1,0:T(8,128)(2,1)S(1)} %reshape.109), kind=kOutput, calls=%fused_computation.64 | convolution fusion | flops 5167382528 | bytes 15269888 | tf_op jit(solution)/shard_map/dot_general | solution.py:15
  299.2 6.7 %all-to-all-done.3 = bf16[64,32,352]{2,1,0:T(8,128)(2,1)} async-done(((bf16[64,32,352]{2,1,0:T(8,128)(2,1)}), bf16[64,32,352]{2,1,0:T(8,128)(2,1)}, u32[]{:S(2)}, u32[]{:S(2)}) %all-to-all-start.3) | async-done | bytes 1441824 | tf_op jit(solution)/shard_map/all_to_all | solution.py:57
  305.9 10.0 %convolution_convert_fusion.1 = bf16[1792,2048]{1,0:T(8,128)(2,1)} fusion(bf16[2048,352]{1,0:T(8,128)(2,1)} %bitcast.6, f32[1792,704]{0,1:T(8,128)} %fusion.47), kind=kOutput, calls=%fused_computation.1 | convolution fusion | flops 2591145984 | bytes 13828096 | tf_op jit(solution)/shard_map/dot_general | solution.py:17
  316.4 3.4 all-gather.9.cloned.1.call-done
  319.8 6.4 %fusion.46 = f32[1280,704]{0,1:T(8,128)S(1)} fusion(bf16[1280,2048]{1,0:T(8,128)(2,1)} %all-gather.9.cloned.1.call-done, bf16[2048,704]{1,0:T(8,128)(2,1)S(1)} %reshape.109), kind=kOutput, calls=%fused_computation.63 | convolution fusion | flops 3690987520 | bytes 11730944 | tf_op jit(solution)/shard_map/dot_general | solution.py:15
  326.2 6.2 %convolution_convert_fusion = bf16[1280,2048]{1,0:T(8,128)(2,1)} fusion(bf16[2048,352]{1,0:T(8,128)(2,1)} %bitcast.6, f32[1280,704]{0,1:T(8,128)S(1)} %fusion.46), kind=kOutput, calls=%fused_computation | convolution fusion | flops 1850818560 | bytes 10289152 | tf_op jit(solution)/shard_map/dot_general | solution.py:17
  332.4 60.7 %reduce-scatter.6.cloned.1.call-done = bf16[448,2048]{1,0:T(8,128)(2,1)} async-done(((bf16[1792,2048]{1,0:T(8,128)(2,1)}), bf16[448,2048]{1,0:T(8,128)(2,1)}) %reduce-scatter.6.cloned.1.call-update) | async-done | bytes 1835024 | tf_op jit(solution)/shard_map/reduce_scatter | solution.py:108
  393.1 3.7 reshape.114
  396.8 10.6 %all-to-all-start.6 = ((bf16[64,7,2048]{2,1,0:T(8,128)(2,1)}), bf16[64,7,2048]{2,1,0:T(8,128)(2,1)S(1)}, u32[]{:S(2)}, u32[]{:S(2)}) async-start(bf16[64,7,2048]{2,1,0:T(8,128)(2,1)} %reshape.114), calls=%async_computation.8 | async-start | bytes 4194304 | tf_op jit(solution)/shard_map/all_to_all | solution.py:115
  407.6 4.2 fusion.4
  411.8 9.0 %fusion = f32[256,2048]{1,0:T(8,128)} fusion(bf16[2048,2112]{1,0:T(8,128)(2,1)} %bitcast.55, bf16[256,2048]{1,0:T(8,128)(2,1)S(1)} %copy-done.8, f32[256,704]{0,1:T(8,128)} %fusion.4), kind=kOutput, calls=%fused_computation.4 | convolution fusion | flops 1477476352 | bytes 10158080 | tf_op jit(solution)/shard_map/dot_general | solution.py:139
  420.8 32.5 %reduce-scatter.4.cloned.1.call-done = bf16[320,2048]{1,0:T(8,128)(2,1)} async-done(((bf16[1280,2048]{1,0:T(8,128)(2,1)}), bf16[320,2048]{1,0:T(8,128)(2,1)}) %reduce-scatter.4.cloned.1.call-update) | async-done | bytes 1310736 | tf_op jit(solution)/shard_map/reduce_scatter | solution.py:108
  453.2 3.4 reshape.112
  458.6 8.7 %all-to-all-start.4 = ((bf16[64,5,2048]{2,1,0:T(8,128)(2,1)}), bf16[64,5,2048]{2,1,0:T(8,128)(2,1)}, u32[]{:S(2)}, u32[]{:S(2)}) async-start(bf16[64,5,2048]{2,1,0:T(8,128)(2,1)} %reshape.112), calls=%async_computation.5 | async-start | bytes 4194304 | tf_op jit(solution)/shard_map/all_to_all | solution.py:115
  468.3 50.3 %all-to-all-done.4 = bf16[64,5,2048]{2,1,0:T(8,128)(2,1)} async-done(((bf16[64,5,2048]{2,1,0:T(8,128)(2,1)}), bf16[64,5,2048]{2,1,0:T(8,128)(2,1)}, u32[]{:S(2)}, u32[]{:S(2)}) %all-to-all-start.4) | async-done | bytes 1310752 | tf_op jit(solution)/shard_map/all_to_all | solution.py:115
  518.5 5.1 pad_maximum_fusion
  523.6 4.8 reshape.115
  533.3 8.5 %all_to_all.49 = bf16[4,64,144]{2,1,0:T(8,128)(2,1)S(1)} all-to-all(bf16[4,64,144]{2,1,0:T(8,128)(2,1)S(1)} %bitcast.51), channel_id=1, replica_groups=mesh['dp'=4,'expert'=16,'mp'=4] {'mp'}, dimensions={0} | all-to-all | bytes 147456 | tf_op jit(solution)/shard_map/all_to_all | solution.py:151
  (72 shorter events, 36.8 us)
Async XLA Ops:
  7.2 27.9 %copy-start.5 = (s32[64,6]{0,1:T(8,128)S(1)}, s32[64,6]{0,1:T(8,128)}, u32[]{:S(2)}) copy-start(s32[64,6]{0,1:T(8,128)} %param.15) | copy-start | bytes 4612
  7.2 216.1 %all-gather.7.cloned.1.call-start = ((), (), s32[]{:S(2)}) async-start(), calls=%async_computation.11 | async-start | bytes 1310720 | tf_op jit(solution)/shard_map/all_gather | solution.py:95
  10.2 213.1 %all-gather.13.cloned.1.call-start = ((), (), s32[]{:S(2)}) async-start(), calls=%async_computation.17 | async-start | bytes 9469952 | tf_op jit(solution)/shard_map/all_gather | solution.py:93
  32.4 255.9 %all-gather.11.cloned.1.call-start = ((), (), s32[]{:S(2)}) async-start(), calls=%async_computation.14 | async-start | bytes 9175040 | tf_op jit(solution)/shard_map/all_gather | solution.py:107
  117.9 1.6 copy-start.4
  121.3 32.4 %all-to-all-start.1 = ((bf16[4,2048,144]{1,2,0:T(8,128)(2,1)}), bf16[4,2048,144]{1,2,0:T(8,128)(2,1)S(1)}, u32[]{:S(2)}, u32[]{:S(2)}) async-start(bf16[4,2048,144]{1,2,0:T(8,128)(2,1)} %broadcast_in_dim.12), calls=%async_computation.1 | async-start | bytes 4718592 | tf_op jit(solution)/shard_map/all_to_all | solution.py:97
  153.7 12.3 %copy-start = (bf16[4,2048,144]{1,2,0:T(8,128)(2,1)}, bf16[4,2048,144]{1,2,0:T(8,128)(2,1)S(1)}, u32[]{:S(2)}) copy-start(bf16[4,2048,144]{1,2,0:T(8,128)(2,1)S(1)} %all-to-all-done.1) | copy-start | bytes 7077892
  153.7 63.4 %all-to-all-start = ((bf16[64,5,2048]{2,1,0:T(8,128)(2,1)}), bf16[64,5,2048]{2,1,0:T(8,128)(2,1)}, u32[]{:S(2)}, u32[]{:S(2)}) async-start(bf16[64,5,2048]{2,1,0:T(8,128)(2,1)} %slice.61), calls=%async_computation | async-start | bytes 4194304 | tf_op jit(solution)/shard_map/all_to_all | solution.py:81
  217.2 51.1 %all-to-all-start.2 = ((bf16[64,32,2,352]{3,1,2,0:T(8,128)(2,1)}), bf16[64,32,2,352]{3,1,2,0:T(8,128)(2,1)S(1)}, u32[]{:S(2)}, u32[]{:S(2)}) async-start(bf16[64,32,2,352]{3,1,2,0:T(8,128)(2,1)} %bitcast.46), calls=%async_computation.2 | async-start | bytes 6291456 | tf_op jit(solution)/shard_map/all_to_all | solution.py:56
  223.2 96.6 %all-gather.9.cloned.1.call-start = ((), (), s32[]{:S(2)}) async-start(), calls=%async_computation.12 | async-start | bytes 6553600 | tf_op jit(solution)/shard_map/all_gather | solution.py:107
  268.3 37.6 %all-to-all-start.3 = ((bf16[64,32,352]{2,1,0:T(8,128)(2,1)}), bf16[64,32,352]{2,1,0:T(8,128)(2,1)}, u32[]{:S(2)}, u32[]{:S(2)}) async-start(bf16[64,32,352]{2,1,0:T(8,128)(2,1)} %bitcast.49), calls=%async_computation.3 | async-start | bytes 3145728 | tf_op jit(solution)/shard_map/all_to_all | solution.py:57
  276.7 116.4 %reduce-scatter.6.cloned.1.call-start = ((), (), s32[]{:S(2)}) async-start(), calls=%async_computation.15 | async-start | bytes 9175040 | tf_op jit(solution)/shard_map/reduce_scatter | solution.py:108
  315.9 137.3 %reduce-scatter.4.cloned.1.call-start = ((), (), s32[]{:S(2)}) async-start(), calls=%async_computation.13 | async-start | bytes 6553600 | tf_op jit(solution)/shard_map/reduce_scatter | solution.py:108
  332.4 75.1 %copy-start.8 = (bf16[256,2048]{1,0:T(8,128)(2,1)S(1)}, bf16[256,2048]{1,0:T(8,128)(2,1)}, u32[]{:S(2)}) copy-start(bf16[256,2048]{1,0:T(8,128)(2,1)} %all-gather.7.cloned.1.call-done) | copy-start | bytes 3145732
  396.8 61.8 %all-to-all-start.6 = ((bf16[64,7,2048]{2,1,0:T(8,128)(2,1)}), bf16[64,7,2048]{2,1,0:T(8,128)(2,1)S(1)}, u32[]{:S(2)}, u32[]{:S(2)}) async-start(bf16[64,7,2048]{2,1,0:T(8,128)(2,1)} %reshape.114), calls=%async_computation.8 | async-start | bytes 4194304 | tf_op jit(solution)/shard_map/all_to_all | solution.py:115
  407.3 121.0 %reduce-scatter.8.cloned.1.call-start = ((), (), s32[]{:S(2)}) async-start(), calls=%async_computation.16 | async-start | bytes 2621440 | tf_op jit(solution)/shard_map/reduce_scatter | solution.py:138
  420.7 46.6 %copy-start.6 = (s32[64,6]{0,1:T(8,128)S(1)}, s32[64,6]{0,1:T(8,128)}, u32[]{:S(2)}) copy-start(s32[64,6]{0,1:T(8,128)} %param.16) | copy-start | bytes 4612
  458.6 59.9 %all-to-all-start.4 = ((bf16[64,5,2048]{2,1,0:T(8,128)(2,1)}), bf16[64,5,2048]{2,1,0:T(8,128)(2,1)}, u32[]{:S(2)}, u32[]{:S(2)}) async-start(bf16[64,5,2048]{2,1,0:T(8,128)(2,1)} %reshape.112), calls=%async_computation.5 | async-start | bytes 4194304 | tf_op jit(solution)/shard_map/all_to_all | solution.py:115
  523.6 4.8 copy-start.2
  528.4 3.9 copy-start.7
  528.4 3.9 copy-start.1
  531.6 0.7 copy-start.3
Sparse Core Ops, SparseCore 0:
  10.4 29.3 all-gather.6
  41.6 97.7 all-gather.12
  141.3 79.4 all-gather.10
  227.1 92.6 all-gather.8
  322.2 70.8 reduce-scatter.5
  395.5 57.6 reduce-scatter.3
  455.8 31.9 reduce-scatter.7

commit v11 on v10

--- a/solution.py
+++ b/solution.py
@@ -74,7 +74,7 @@
     send = lax.dot_general(
         slot_token, normed, (((0,), (0,)), ((), ())), preferred_element_type=jnp.float32
     ).astype(jnp.bfloat16)
-    bounds = (0, 5 * capacity // 12, capacity) if capacity >= 3 else (0, capacity)
+    bounds = (0, 7 * capacity // 12, capacity) if capacity >= 3 else (0, capacity)
     spans = list(zip(bounds[:-1], bounds[1:]))
     send = send.reshape(n_groups, capacity, width)
     received = [

time: 559 us -> 588 us (1.052)
  waiting for transfers between devices: 256 us -> 281 us
    all_to_all x1, waiting for transfers between devices: 37.5 us -> 51.1 us  [on_device(): lax.all_to_all(send[:, lo:hi], ('dp', 'expert'), split_axis=0, concat_axi...]
    all_to_all x1, waiting for transfers between devices: 37.4 us -> 48.5 us  [on_device(): lax.all_to_all(in_send, ('expert', 'mp'), split_axis=0, concat_axis=1, ti...]
  transfers between devices with their start and end apart: 13 -> 13, of which waited for: 9 -> 8; matrix products, arithmetic and copies ran while one was open for 21% -> 20% of each run, Pallas kernels for 0% -> 0%
where the time goes in v11:
time: 588 us; the launch traced here: 578 us
  waiting for transfers between devices  281 us (48%)
  blocking collectives  105 us (18%)
  starting transfers between devices  54.5 us (9%)
  local copies, waits for them, and re-layouts  52.6 us (9%)
  matrix products  52.2 us (9%)
  other arithmetic  18.2 us (3%)
  between operations  14.9 us (3%)
    reduce_scatter x2, waiting for transfers between devices, on_device(): lax.psum_scatter(expert_part(rows, gate_up_w, down_w).astype(jnp.bfloat16...  93.9 us
    all_to_all x1, blocking collectives, on_device(): lax.all_to_all(send[:, lo:hi], ('dp', 'expert'), split_axis=0, concat_axi...  75.2 us
    all_to_all x1, waiting for transfers between devices, on_device(): lax.all_to_all(send[:, lo:hi], ('dp', 'expert'), split_axis=0, concat_axi...  51.1 us
    all_to_all x2, waiting for transfers between devices, on_device(): lax.all_to_all(summed.reshape(n_groups, chunk, width), ('dp', 'expert'),...  50.3 us
    all_to_all x1, waiting for transfers between devices, on_device(): lax.all_to_all(in_send, ('expert', 'mp'), split_axis=0, concat_axis=1, ti...  48.5 us
    all_to_all x1, waiting for transfers between devices, on_device(): lax.all_to_all(jnp.broadcast_to(kv_weight[None], (n_mp,) + kv_weight.shap...  24.4 us
    all_to_all x2, starting transfers between devices, on_device(): lax.all_to_all(summed.reshape(n_groups, chunk, width), ('dp', 'expert'),...  21.3 us
    all_gather x1, blocking collectives, on_device(): shared_cat = lax.all_gather(shared_cat, 'dp', axis=0, tiled=False)  21.2 us
  transfers between devices with their start and end apart: 13, of which 8 were waited for; matrix products, arithmetic and copies ran while one was open for 20% of the time, Pallas kernels for 0%

profile of v11, /device:TPU:8, one launch (start us, length us, event | category | flops | bytes accessed | tf_op | source)
XLA Modules:
  0.0 578.5 jit_solution(4935847121098201869)
XLA Ops:
  11.2 21.2 %all-gather = bf16[128,2112]{1,0:T(8,128)(2,1)} all-gather(bf16[32,2112]{1,0:T(8,128)(2,1)S(1)} %concatenate.9), channel_id=2, replica_groups=mesh['dp'=4,'expert'=16,'mp'=4] {'dp'}, dimensions={0}, use_global_device_ids=true | all-gather | bytes 675840 | tf_op jit(solution)/shard_map/all_gather | solution.py:92
  43.0 75.2 %all_to_all.48 = bf16[64,5,2048]{2,1,0:T(8,128)(2,1)S(1)} all-to-all(bf16[64,5,2048]{2,1,0:T(8,128)(2,1)S(1)} %slice.68), channel_id=1, replica_groups=mesh['dp'=4,'expert'=16,'mp'=4] {'dp','expert'}, dimensions={0} | all-to-all | bytes 2621440 | tf_op jit(solution)/shard_map/all_to_all | solution.py:81
  121.4 4.3 all-to-all-start.1
  128.9 24.4 %all-to-all-done.1 = bf16[4,2048,144]{1,2,0:T(8,128)(2,1)S(1)} async-done(((bf16[4,2048,144]{1,2,0:T(8,128)(2,1)}), bf16[4,2048,144]{1,2,0:T(8,128)(2,1)S(1)}, u32[]{:S(2)}, u32[]{:S(2)}) %all-to-all-start.1) | async-done | bytes 2359328 | tf_op jit(solution)/shard_map/all_to_all | solution.py:97
  153.3 12.9 %all-to-all-start = ((bf16[64,7,2048]{2,1,0:T(8,128)(2,1)}), bf16[64,7,2048]{2,1,0:T(8,128)(2,1)}, u32[]{:S(2)}, u32[]{:S(2)}) async-start(bf16[64,7,2048]{2,1,0:T(8,128)(2,1)} %slice.61), calls=%async_computation | async-start | bytes 4194304 | tf_op jit(solution)/shard_map/all_to_all | solution.py:81
  166.2 51.1 %all-to-all-done = bf16[64,7,2048]{2,1,0:T(8,128)(2,1)} async-done(((bf16[64,7,2048]{2,1,0:T(8,128)(2,1)}), bf16[64,7,2048]{2,1,0:T(8,128)(2,1)}, u32[]{:S(2)}, u32[]{:S(2)}) %all-to-all-start) | async-done | bytes 1835040 | tf_op jit(solution)/shard_map/all_to_all | solution.py:81
  217.3 3.7 reshape.106
  221.1 4.6 convert_element_type.61
  225.7 6.8 %reshape.107 = bf16[16,32,2,4,352]{4,3,2,1,0:T(4,128)(2,1)S(1)} reshape(bf16[16,32,2816]{2,1,0:T(8,128)(2,1)} %convert_element_type.61) | data formatting | bytes 5767168 | tf_op jit(solution)/shard_map/reshape | solution.py:45
  234.8 6.0 %all-to-all-start.2 = ((bf16[64,32,2,352]{3,1,2,0:T(8,128)(2,1)}), bf16[64,32,2,352]{3,1,2,0:T(8,128)(2,1)S(1)}, u32[]{:S(2)}, u32[]{:S(2)}) async-start(bf16[64,32,2,352]{3,1,2,0:T(8,128)(2,1)} %bitcast.46), calls=%async_computation.2 | async-start | bytes 6291456 | tf_op jit(solution)/shard_map/all_to_all | solution.py:56
  244.7 48.5 %all-to-all-done.2 = bf16[64,32,2,352]{3,1,2,0:T(8,128)(2,1)S(1)} async-done(((bf16[64,32,2,352]{3,1,2,0:T(8,128)(2,1)}), bf16[64,32,2,352]{3,1,2,0:T(8,128)(2,1)S(1)}, u32[]{:S(2)}, u32[]{:S(2)}) %all-to-all-start.2) | async-done | bytes 2883616 | tf_op jit(solution)/shard_map/all_to_all | solution.py:56
  293.2 9.1 %all-to-all-start.3 = ((bf16[64,32,352]{2,1,0:T(8,128)(2,1)}), bf16[64,32,352]{2,1,0:T(8,128)(2,1)}, u32[]{:S(2)}, u32[]{:S(2)}) async-start(bf16[64,32,352]{2,1,0:T(8,128)(2,1)} %bitcast.49), calls=%async_computation.3 | async-start | bytes 3145728 | tf_op jit(solution)/shard_map/all_to_all | solution.py:57
  302.5 4.9 copy.59
  307.4 6.4 %reshape.109 = bf16[2048,704]{1,0:T(8,128)(2,1)S(1)} reshape(bf16[64,32,2,352]{3,2,1,0:T(2,128)(2,1)} %copy.59) | data formatting | bytes 5767168 | tf_op jit(solution)/shard_map/reshape | solution.py:59
  313.9 8.2 %fusion.47 = f32[1280,704]{0,1:T(8,128)} fusion(bf16[1280,2048]{1,0:T(8,128)(2,1)} %all-gather.11.cloned.1.call-done, bf16[2048,704]{1,0:T(8,128)(2,1)S(1)} %reshape.109), kind=kOutput, calls=%fused_computation.64 | convolution fusion | flops 3690987520 | bytes 11730944 | tf_op jit(solution)/shard_map/dot_general | solution.py:15
  322.1 9.3 %all-to-all-done.3 = bf16[64,32,352]{2,1,0:T(8,128)(2,1)} async-done(((bf16[64,32,352]{2,1,0:T(8,128)(2,1)}), bf16[64,32,352]{2,1,0:T(8,128)(2,1)}, u32[]{:S(2)}, u32[]{:S(2)}) %all-to-all-start.3) | async-done | bytes 1441824 | tf_op jit(solution)/shard_map/all_to_all | solution.py:57
  331.4 7.8 %convolution_convert_fusion = bf16[1280,2048]{1,0:T(8,128)(2,1)} fusion(bf16[2048,352]{1,0:T(8,128)(2,1)} %bitcast.6, f32[1280,704]{0,1:T(8,128)} %fusion.47), kind=kOutput, calls=%fused_computation | convolution fusion | flops 1850818560 | bytes 10289152 | tf_op jit(solution)/shard_map/dot_general | solution.py:17
  339.4 3.7 all-gather.9.cloned.1.call-done
  343.1 9.2 %fusion.46 = f32[1792,704]{0,1:T(8,128)S(1)} fusion(bf16[1792,2048]{1,0:T(8,128)(2,1)} %all-gather.9.cloned.1.call-done, bf16[2048,704]{1,0:T(8,128)(2,1)S(1)} %reshape.109), kind=kOutput, calls=%fused_computation.63 | convolution fusion | flops 5167382528 | bytes 15269888 | tf_op jit(solution)/shard_map/dot_general | solution.py:15
  352.3 7.6 %convolution_convert_fusion.1 = bf16[1792,2048]{1,0:T(8,128)(2,1)} fusion(bf16[2048,352]{1,0:T(8,128)(2,1)} %bitcast.6, f32[1792,704]{0,1:T(8,128)S(1)} %fusion.46), kind=kOutput, calls=%fused_computation.1 | convolution fusion | flops 2591145984 | bytes 13828096 | tf_op jit(solution)/shard_map/dot_general | solution.py:17
  359.9 44.3 %reduce-scatter.6.cloned.1.call-done = bf16[320,2048]{1,0:T(8,128)(2,1)} async-done(((bf16[1280,2048]{1,0:T(8,128)(2,1)}), bf16[320,2048]{1,0:T(8,128)(2,1)}) %reduce-scatter.6.cloned.1.call-update) | async-done | bytes 1310736 | tf_op jit(solution)/shard_map/reduce_scatter | solution.py:108
  404.3 3.4 reshape.114
  407.7 10.5 %all-to-all-start.6 = ((bf16[64,5,2048]{2,1,0:T(8,128)(2,1)}), bf16[64,5,2048]{2,1,0:T(8,128)(2,1)S(1)}, u32[]{:S(2)}, u32[]{:S(2)}) async-start(bf16[64,5,2048]{2,1,0:T(8,128)(2,1)} %reshape.114), calls=%async_computation.8 | async-start | bytes 4194304 | tf_op jit(solution)/shard_map/all_to_all | solution.py:115
  418.5 4.5 fusion.4
  423.1 8.9 %fusion = f32[256,2048]{1,0:T(8,128)} fusion(bf16[2048,2112]{1,0:T(8,128)(2,1)} %bitcast.55, bf16[256,2048]{1,0:T(8,128)(2,1)S(1)} %copy-done.8, f32[256,704]{0,1:T(8,128)} %fusion.4), kind=kOutput, calls=%fused_computation.4 | convolution fusion | flops 1477476352 | bytes 10158080 | tf_op jit(solution)/shard_map/dot_general | solution.py:139
  432.0 49.5 %reduce-scatter.4.cloned.1.call-done = bf16[448,2048]{1,0:T(8,128)(2,1)} async-done(((bf16[1792,2048]{1,0:T(8,128)(2,1)}), bf16[448,2048]{1,0:T(8,128)(2,1)}) %reduce-scatter.4.cloned.1.call-update) | async-done | bytes 1835024 | tf_op jit(solution)/shard_map/reduce_scatter | solution.py:108
  481.5 3.7 reshape.112
  485.2 10.8 %all-to-all-start.4 = ((bf16[64,7,2048]{2,1,0:T(8,128)(2,1)}), bf16[64,7,2048]{2,1,0:T(8,128)(2,1)}, u32[]{:S(2)}, u32[]{:S(2)}) async-start(bf16[64,7,2048]{2,1,0:T(8,128)(2,1)} %reshape.112), calls=%async_computation.5 | async-start | bytes 4194304 | tf_op jit(solution)/shard_map/all_to_all | solution.py:115
  496.9 50.3 %all-to-all-done.4 = bf16[64,7,2048]{2,1,0:T(8,128)(2,1)} async-done(((bf16[64,7,2048]{2,1,0:T(8,128)(2,1)}), bf16[64,7,2048]{2,1,0:T(8,128)(2,1)}, u32[]{:S(2)}, u32[]{:S(2)}) %all-to-all-start.4) | async-done | bytes 1835040 | tf_op jit(solution)/shard_map/all_to_all | solution.py:115
  547.2 5.1 pad_maximum_fusion
  552.3 4.8 reshape.115
  562.0 8.5 %all_to_all.49 = bf16[4,64,144]{2,1,0:T(8,128)(2,1)S(1)} all-to-all(bf16[4,64,144]{2,1,0:T(8,128)(2,1)S(1)} %bitcast.51), channel_id=1, replica_groups=mesh['dp'=4,'expert'=16,'mp'=4] {'mp'}, dimensions={0} | all-to-all | bytes 147456 | tf_op jit(solution)/shard_map/all_to_all | solution.py:151
  (72 shorter events, 34.5 us)
Async XLA Ops:
  7.2 27.9 %copy-start.5 = (s32[64,6]{0,1:T(8,128)S(1)}, s32[64,6]{0,1:T(8,128)}, u32[]{:S(2)}) copy-start(s32[64,6]{0,1:T(8,128)} %param.15) | copy-start | bytes 4612
  7.2 159.0 %all-gather.7.cloned.1.call-start = ((), (), s32[]{:S(2)}) async-start(), calls=%async_computation.11 | async-start | bytes 1310720 | tf_op jit(solution)/shard_map/all_gather | solution.py:95
  10.2 207.2 %all-gather.13.cloned.1.call-start = ((), (), s32[]{:S(2)}) async-start(), calls=%async_computation.17 | async-start | bytes 9469952 | tf_op jit(solution)/shard_map/all_gather | solution.py:93
  32.4 281.4 %all-gather.11.cloned.1.call-start = ((), (), s32[]{:S(2)}) async-start(), calls=%async_computation.14 | async-start | bytes 6553600 | tf_op jit(solution)/shard_map/all_gather | solution.py:107
  118.2 1.4 copy-start.4
  121.4 31.9 %all-to-all-start.1 = ((bf16[4,2048,144]{1,2,0:T(8,128)(2,1)}), bf16[4,2048,144]{1,2,0:T(8,128)(2,1)S(1)}, u32[]{:S(2)}, u32[]{:S(2)}) async-start(bf16[4,2048,144]{1,2,0:T(8,128)(2,1)} %broadcast_in_dim.12), calls=%async_computation.1 | async-start | bytes 4718592 | tf_op jit(solution)/shard_map/all_to_all | solution.py:97
  153.3 67.8 %copy-start = (bf16[4,2048,144]{1,2,0:T(8,128)(2,1)}, bf16[4,2048,144]{1,2,0:T(8,128)(2,1)S(1)}, u32[]{:S(2)}) copy-start(bf16[4,2048,144]{1,2,0:T(8,128)(2,1)S(1)} %all-to-all-done.1) | copy-start | bytes 7077892
  153.3 64.1 %all-to-all-start = ((bf16[64,7,2048]{2,1,0:T(8,128)(2,1)}), bf16[64,7,2048]{2,1,0:T(8,128)(2,1)}, u32[]{:S(2)}, u32[]{:S(2)}) async-start(bf16[64,7,2048]{2,1,0:T(8,128)(2,1)} %slice.61), calls=%async_computation | async-start | bytes 4194304 | tf_op jit(solution)/shard_map/all_to_all | solution.py:81
  166.1 176.9 %all-gather.9.cloned.1.call-start = ((), (), s32[]{:S(2)}) async-start(), calls=%async_computation.12 | async-start | bytes 9175040 | tf_op jit(solution)/shard_map/all_gather | solution.py:107
  234.8 58.3 %all-to-all-start.2 = ((bf16[64,32,2,352]{3,1,2,0:T(8,128)(2,1)}), bf16[64,32,2,352]{3,1,2,0:T(8,128)(2,1)S(1)}, u32[]{:S(2)}, u32[]{:S(2)}) async-start(bf16[64,32,2,352]{3,1,2,0:T(8,128)(2,1)} %bitcast.46), calls=%async_computation.2 | async-start | bytes 6291456 | tf_op jit(solution)/shard_map/all_to_all | solution.py:56
  293.2 38.2 %all-to-all-start.3 = ((bf16[64,32,352]{2,1,0:T(8,128)(2,1)}), bf16[64,32,352]{2,1,0:T(8,128)(2,1)}, u32[]{:S(2)}, u32[]{:S(2)}) async-start(bf16[64,32,352]{2,1,0:T(8,128)(2,1)} %bitcast.49), calls=%async_computation.3 | async-start | bytes 3145728 | tf_op jit(solution)/shard_map/all_to_all | solution.py:57
  302.3 102.0 %reduce-scatter.6.cloned.1.call-start = ((), (), s32[]{:S(2)}) async-start(), calls=%async_computation.15 | async-start | bytes 6553600 | tf_op jit(solution)/shard_map/reduce_scatter | solution.py:108
  339.2 142.4 %reduce-scatter.4.cloned.1.call-start = ((), (), s32[]{:S(2)}) async-start(), calls=%async_computation.13 | async-start | bytes 9175040 | tf_op jit(solution)/shard_map/reduce_scatter | solution.py:108
  359.9 58.6 %copy-start.8 = (bf16[256,2048]{1,0:T(8,128)(2,1)S(1)}, bf16[256,2048]{1,0:T(8,128)(2,1)}, u32[]{:S(2)}) copy-start(bf16[256,2048]{1,0:T(8,128)(2,1)} %all-gather.7.cloned.1.call-done) | copy-start | bytes 3145732
  407.7 77.5 %all-to-all-start.6 = ((bf16[64,5,2048]{2,1,0:T(8,128)(2,1)}), bf16[64,5,2048]{2,1,0:T(8,128)(2,1)S(1)}, u32[]{:S(2)}, u32[]{:S(2)}) async-start(bf16[64,5,2048]{2,1,0:T(8,128)(2,1)} %reshape.114), calls=%async_computation.8 | async-start | bytes 4194304 | tf_op jit(solution)/shard_map/all_to_all | solution.py:115
  418.2 138.8 %reduce-scatter.8.cloned.1.call-start = ((), (), s32[]{:S(2)}) async-start(), calls=%async_computation.16 | async-start | bytes 2621440 | tf_op jit(solution)/shard_map/reduce_scatter | solution.py:138
  432.0 64.0 %copy-start.6 = (s32[64,6]{0,1:T(8,128)S(1)}, s32[64,6]{0,1:T(8,128)}, u32[]{:S(2)}) copy-start(s32[64,6]{0,1:T(8,128)} %param.16) | copy-start | bytes 4612
  485.2 62.0 %all-to-all-start.4 = ((bf16[64,7,2048]{2,1,0:T(8,128)(2,1)}), bf16[64,7,2048]{2,1,0:T(8,128)(2,1)}, u32[]{:S(2)}, u32[]{:S(2)}) async-start(bf16[64,7,2048]{2,1,0:T(8,128)(2,1)} %reshape.112), calls=%async_computation.5 | async-start | bytes 4194304 | tf_op jit(solution)/shard_map/all_to_all | solution.py:115
  552.3 4.8 copy-start.2
  557.0 3.9 copy-start.7
  557.1 3.9 copy-start.1
  560.3 0.7 copy-start.3
Sparse Core Ops, SparseCore 0:
  10.4 29.3 all-gather.6
  41.6 97.8 all-gather.12
  141.4 61.9 all-gather.10
  221.2 121.8 all-gather.8
  345.5 58.7 reduce-scatter.5
  406.7 74.8 reduce-scatter.3
  484.1 31.9 reduce-scatter.7
